TPU v7x, 32 devices: a whole 2x2x4 slice. The times are simulated.
32 devices in a mesh: dp: 8 (over y, x, core), blk: 4 (over z).
Axes of the slice: x: 2, y: 2, z: 4, core: 2. Of those that a mesh axis runs over, the one named last changes fastest.
Arguments:
- spans: bfloat16 [40960, 1024], P(('dp', 'blk')), may hold values from -6 to 6
- span_counts: int32 [32], P(('dp', 'blk')), may hold values from 16 to 1232, as said below
- session_ids: int32 [40960], P(('dp', 'blk')), may hold values from 0 to 15, as said below
- destinations: int32 [40960], P(('dp', 'blk')), may hold values from 0 to 7, as said below
- expert_weight: bfloat16 [8, 1024, 4096], P('dp'), may hold values from -0.1875 to 0.1875
- norm_gain: float32 [1024], replicated, may hold values from 0.1 to 1.9
- queries: bfloat16 [28672, 4096], P(('dp', 'blk')), may hold values from -6 to 6
- positives: int32 [28672], P(('dp', 'blk')), may hold values from 0 to 63
Outputs:
- loss_rows: float32 [28672], P(('dp', 'blk'))
- grad_queries: bfloat16 [28672, 4096], P(('dp', 'blk'))
- grad_sessions: float32 [512, 4096], P(('dp', 'blk'))
Inputs may be any that keep to these rules, and one draw needn't show every extreme that they name: `span_counts`: for each blk index the counts of the devices along dp sum to 2560, and one of them has the largest value. `destinations`: the live rows of the devices that share a blk index, in order of dp index and then of row, name the experts in cyclic order from a drawn start: each expert receives exactly 320 live rows of its blk index, and a device sends at most 154 live rows to one expert, the device with the largest count exactly 154 to each. Rows at or after a device's count name any expert. `session_ids`: on each device the ids of the live rows never fall, begin at 0 and take every value; rows at or after the count carry any id.
All inputs are finite; a program needn't handle non-finite values.
Results may differ from a plain program's by a relative error of at most 0.0072.
Values may be sent and summed in bfloat16 or wider, within the bound.
No kernel may reach another device: no remote copies, remote signals or barrier semaphores. Data moves between devices by JAX's collectives and lax.ppermute only.
A program may use at most 128 MiB of HBM per device.

v0:
```python
import jax
import jax.numpy as jnp
from jax import lax
from jax.sharding import PartitionSpec as P

SESS_DEV = 16


logit_scale = 20.0
epsilon = 1e-06


def passed_along(shard, axis, by):
    length = lax.axis_size(axis)
    return lax.ppermute(shard, axis, [(i, (i + by) % length) for i in range(length)])


def unit_rows(values):
    widened = values.astype(jnp.float32)
    return (
        widened * lax.rsqrt(jnp.sum(widened * widened, axis=-1, keepdims=True) + epsilon)
    ).astype(jnp.bfloat16)


def contract_rows(left_side, right_side):
    return lax.dot_general(
        left_side, right_side, (((1,), (1,)), ((), ())), preferred_element_type=jnp.float32
    )


def contract_first(left_side, right_side):
    return lax.dot_general(
        left_side, right_side, (((0,), (0,)), ((), ())), preferred_element_type=jnp.float32
    )


def on_device(
    spans, span_counts, session_ids, destinations, expert_weight, norm_gain, queries, positives
):
    rows_dev = spans.shape[0]
    hidden_width = spans.shape[1]
    groups = lax.axis_size("dp")
    capacity = (rows_dev - 3 * SESS_DEV) // groups
    received = rows_dev // 4
    live_rows = jnp.arange(rows_dev, dtype=jnp.int32) < span_counts[0]
    expert_ids = jnp.arange(groups, dtype=jnp.int32)
    expert_marks = ((destinations[:, None] == expert_ids[None, :]) & live_rows[:, None]).astype(
        jnp.int32
    )
    before = jnp.cumsum(expert_marks, axis=0) - expert_marks
    slot_index = jnp.where(
        live_rows,
        destinations * capacity + jnp.sum(before * expert_marks, axis=1),
        groups * capacity,
    )
    send_counts = jnp.sum(expert_marks, axis=0)
    send_rows = (
        jnp.zeros((groups * capacity, hidden_width), jnp.bfloat16)
        .at[slot_index]
        .set(spans, mode="drop")
        .reshape(groups, capacity, hidden_width)
    )
    slot_session = (
        jnp.full((groups * capacity,), -1, jnp.int32).at[slot_index].set(session_ids, mode="drop")
    )
    got_rows, got_counts = (
        lax.all_to_all(send_rows, "dp", split_axis=0, concat_axis=0, tiled=True),
        lax.all_to_all(send_counts, "dp", split_axis=0, concat_axis=0, tiled=True),
    )
    slot_rank = jnp.arange(capacity, dtype=jnp.int32)
    valid_slots = slot_rank[None, :] < got_counts[:, None]
    packed_at = jnp.where(
        valid_slots, (jnp.cumsum(got_counts) - got_counts)[:, None] + slot_rank[None, :], received
    ).reshape(groups * capacity)
    packed = (
        jnp.zeros((received, hidden_width), jnp.bfloat16)
        .at[packed_at]
        .set(got_rows.reshape(groups * capacity, hidden_width), mode="drop")
    )
    widened = packed.astype(jnp.float32)
    normed = (
        widened
        * lax.rsqrt(jnp.mean(widened * widened, axis=-1, keepdims=True) + epsilon)
        * norm_gain
    ).astype(jnp.bfloat16)
    embedded = jax.nn.gelu(
        jnp.dot(normed, expert_weight[0], preferred_element_type=jnp.float32), approximate=True
    ).astype(jnp.bfloat16)
    emb_width = embedded.shape[1]
    gather_at = jnp.minimum(packed_at, received - 1)
    outgoing = jnp.where(
        valid_slots.reshape(groups * capacity)[:, None],
        embedded[gather_at],
        jnp.zeros((), jnp.bfloat16),
    ).reshape(groups, capacity, emb_width)
    returned = lax.all_to_all(outgoing, "dp", split_axis=0, concat_axis=0, tiled=True)
    selector = (jnp.arange(SESS_DEV, dtype=jnp.int32)[:, None] == slot_session[None, :]).astype(
        jnp.bfloat16
    )
    pooled = jnp.dot(
        selector, returned.reshape(groups * capacity, emb_width), preferred_element_type=jnp.float32
    )
    doc_unit = unit_rows(pooled)
    query_unit = unit_rows(queries)
    doc_rows = doc_unit.shape[0]
    doc_piece = lax.all_gather(doc_unit, "blk", axis=0, tiled=True)
    piece_rows = doc_piece.shape[0]
    logits = logit_scale * contract_rows(query_unit, doc_piece)
    weights = jnp.exp(logits)
    inside = (positives >= 0) & (positives < piece_rows)
    matches = positives[:, None] == jnp.arange(piece_rows, dtype=jnp.int32)[None, :]
    picked = doc_piece[jnp.clip(positives, 0, piece_rows - 1)].astype(jnp.float32)
    totals = jnp.sum(weights, axis=1)
    numerator = jnp.dot(weights.astype(jnp.bfloat16), doc_piece, preferred_element_type=jnp.float32)
    chosen_logit = jnp.sum(jnp.where(matches, logits, 0.0), axis=1)
    chosen_doc = jnp.where(inside[:, None], picked, 0.0)
    cycle_size = lax.axis_size("blk")
    position = lax.axis_index("blk")

    def backward(step_index, running):
        travelling, accumulated = running
        row_start = (position - step_index) % cycle_size * doc_rows
        logits = logit_scale * contract_rows(query_unit, travelling)
        matches = (positives - row_start)[:, None] == jnp.arange(doc_rows, dtype=jnp.int32)[None, :]
        coefficient = (jnp.exp(logits) / totals[:, None] - matches.astype(jnp.float32)).astype(
            jnp.bfloat16
        )
        accumulated = accumulated + logit_scale * contract_first(coefficient, query_unit)
        travelling = passed_along(travelling, "blk", 1)
        accumulated = passed_along(accumulated, "blk", 1)
        return (travelling, accumulated)

    grad_docs = lax.fori_loop(
        0, cycle_size, backward, (doc_unit, jnp.zeros((doc_rows, emb_width), jnp.float32))
    )[1]
    loss_rows = jnp.log(totals) - chosen_logit
    grad_queries = (logit_scale * (numerator / totals[:, None] - chosen_doc)).astype(jnp.bfloat16)
    return (loss_rows, grad_queries, grad_docs)


def solution(mesh):
    placed = (
        P(("dp", "blk"), None),
        P(("dp", "blk")),
        P(("dp", "blk")),
        P(("dp", "blk")),
        P("dp", None, None),
        P(),
        P(("dp", "blk"), None),
        P(("dp", "blk")),
    )
    return jax.shard_map(
        on_device,
        mesh=mesh,
        in_specs=placed,
        out_specs=(P(("dp", "blk")), P(("dp", "blk"), None), P(("dp", "blk"), None)),
        check_vma=False,
    )
```

profile of v0, /device:TPU:2, one launch (start us, length us, event | category | flops | bytes accessed | tf_op | source)
XLA Modules:
  0.0 355.8 jit_solution(18068380321817378988)
XLA Ops:
  11.3 9.7 %scatter_custom_fusion.1 = bf16[1232,1024]{1,0:T(8,128)(2,1)S(1)} fusion(s32[1280]{0:T(1024)S(1)} %compare_select_fusion.2, bf16[1280,1024]{1,0:T(8,128)(2,1)} %param.10, bf16[]{:T(256)} %constant.108.clone.1), kind=kCustom, calls=%fused_computation.41 | custom fusion | bytes 2523648 | tf_op jit(solution)/shard_map/scatter | solution.py:60
  27.8 30.0 %all-to-all-done.1 = bf16[8,154,1024]{2,1,0:T(8,128)(2,1)S(1)} async-done(((bf16[8,154,1024]{2,1,0:T(8,128)(2,1)}), bf16[8,154,1024]{2,1,0:T(8,128)(2,1)S(1)}, u32[]{:S(2)}, u32[]{:S(2)}) %all-to-all-start.1) | async-done | bytes 2523168 | tf_op jit(solution)/shard_map/all_to_all | solution.py:67
  59.6 9.5 %scatter_custom_fusion.2 = bf16[320,1024]{1,0:T(8,128)(2,1)S(1)} fusion(s32[1232]{0:T(1024)S(1)} %get-tuple-element.186, bf16[1232,1024]{1,0:T(8,128)(2,1)} %reshape.246, bf16[]{:T(256)} %constant.108.clone.1), kind=kCustom, calls=%fused_computation.46 | custom fusion | bytes 655872 | tf_op jit(solution)/shard_map/scatter | solution.py:78
  69.4 7.3 %fusion.21 = bf16[320,4096]{1,0:T(8,128)(2,1)S(1)} fusion(bf16[1,1024,4096]{2,1,0:T(8,128)(2,1)} %param.14, bf16[320,1024]{1,0:T(8,128)(2,1)S(1)} %scatter_custom_fusion.2, f32[1024]{0:T(1024)S(1)} %copy-done.2, f32[320]{0:T(512)S(1)} %add_rsqrt_fusion.1), kind=kOutput, calls=%fused_computation.35 | convolution fusion | flops 2697461760 | bytes 11670784 | tf_op jit(solution)/shard_map/dot_general | solution.py:87
  76.7 8.2 %gather_fusion = bf16[1232,4096]{1,0:T(8,128)(2,1)} fusion(bf16[320,4096]{1,0:T(8,128)(2,1)S(1)} %fusion.21, s32[2048]{0:T(1024)S(1)} %pad_clamp_fusion), kind=kCustom, calls=%fused_computation | custom fusion | bytes 20190016 | tf_op jit(solution)/shard_map/gather | solution.py:93
  85.0 12.1 %gather.9 = bf16[8,154,4096]{2,1,0:T(8,128)(2,1)} reshape(bf16[1232,4096]{1,0:T(8,128)(2,1)} %gather_fusion) | data formatting | bytes 20185088 | tf_op jit(solution)/shard_map/gather | solution.py:93
  97.1 10.0 %broadcast_select_fusion = bf16[8,154,4096]{2,1,0:T(8,128)(2,1)} fusion(bf16[8,154,4096]{2,1,0:T(8,128)(2,1)} %gather.9, pred[8,154]{1,0:T(8,128)(4,1)S(1)} %iota_compare_fusion.7), kind=kLoop, calls=%fused_computation.24 | loop fusion | flops 5046272 | bytes 20186320 | tf_op jit(solution)/shard_map/jit(_where)/select_n | solution.py:91
  107.0 6.7 %all-to-all-start.2 = ((bf16[8,154,4096]{2,1,0:T(8,128)(2,1)}), bf16[8,154,4096]{2,1,0:T(8,128)(2,1)}, u32[]{:S(2)}, u32[]{:S(2)}) async-start(bf16[8,154,4096]{2,1,0:T(8,128)(2,1)} %broadcast_select_fusion), calls=%async_computation.2 | async-start | bytes 20971520 | tf_op jit(solution)/shard_map/all_to_all | solution.py:96
  113.7 5.6 %scatter_custom_fusion = s32[1232]{0:T(1024)S(1)} fusion(s32[1280]{0:T(1024)S(1)} %compare_select_fusion.2, s32[1280]{0:T(1024)} %param.12, s32[]{:T(128)} %constant.103.clone.1), kind=kCustom, calls=%fused_computation.82 | custom fusion | bytes 5440 | tf_op jit(solution)/shard_map/scatter | solution.py:64
  124.0 9.0 %fusion.11 = bf16[896,4096]{1,0:T(8,128)(2,1)} fusion(bf16[896,4096]{1,0:T(8,128)(2,1)} %param.16, f32[896]{0:T(1024)S(1)} %add_rsqrt_fusion), kind=kLoop, calls=%fused_computation.22 | loop fusion | flops 11010048 | bytes 14683648 | tf_op jit(solution)/shard_map/convert_element_type | solution.py:22
  132.9 95.9 %all-to-all-done.2 = bf16[8,154,4096]{2,1,0:T(8,128)(2,1)} async-done(((bf16[8,154,4096]{2,1,0:T(8,128)(2,1)}), bf16[8,154,4096]{2,1,0:T(8,128)(2,1)}, u32[]{:S(2)}, u32[]{:S(2)}) %all-to-all-start.2) | async-done | bytes 10092576 | tf_op jit(solution)/shard_map/all_to_all | solution.py:96
  228.8 12.2 %reshape.209 = bf16[1232,4096]{1,0:T(8,128)(2,1)} reshape(bf16[8,154,4096]{2,1,0:T(8,128)(2,1)} %all-to-all-done.2) | data formatting | bytes 20185088 | tf_op jit(solution)/shard_map/reshape | solution.py:101
  246.7 16.3 %all_gather.3 = bf16[64,4096]{1,0:T(8,128)(2,1)S(1)} all-gather(bf16[16,4096]{1,0:T(8,128)(2,1)S(1)} %multiply_convert_fusion.1), channel_id=1, replica_groups=mesh['dp'=8,'blk'=4] {'blk'}, dimensions={0}, use_global_device_ids=true | all-gather | bytes 655360 | tf_op jit(solution)/shard_map/all_gather | solution.py:106
  265.4 75.4 %while.17 = (s32[]{:T(128)}, bf16[16,4096]{1,0:T(8,128)(2,1)S(1)}, f32[16,4096]{1,0:T(8,128)S(1)}, bf16[896,4096]{1,0:T(8,128)(2,1)}, f32[896]{0:T(1024)S(1)}, /...) while((s32[]{:T(128)}, bf16[16,4096]{1,0:T(8,128)(2,1)S(1)}, ...), condition=%wide.region_14.15_spmd, body=%wide.region_13.14_spmd.sunk | while | flops 235099024 | bytes 9845070 | solution.py:133
  265.4 8.7 %fusion.59 = f32[16,4096]{1,0:T(8,128)S(1)} fusion(f32[16,4096]{1,0:T(8,128)S(1)} %get-tuple-element.261, bf16[896,4096]{1,0:T(8,128)(2,1)} %get-tuple-element.274, bf16[16,4096]{1,0:T(8,128)(2,1)S(1)} %copy.20, s32[896]{0:T(1024)S(1)} %broadcast_subtract_fusion.2, f32[896]{0:T(1024)S(1)} %get-tuple-element.275), kind=kOutput, calls=%fused_computation.6.clone.1 | convolution fusion | flops 235098112 | bytes 8002560 | tf_op jit(solution)/shard_map/while/body/eval_jaxpr/dot_general | solution.py:32
  276.1 9.1 %collective-permute-done = bf16[16,4096]{1,0:T(8,128)(2,1)S(1)} collective-permute-done((bf16[16,4096]{1,0:T(8,128)(2,1)S(1)}, bf16[16,4096]{1,0:T(8,128)(2,1)S(1)}, u32[]{:S(2)}, u32[]{:S(2)}) %collective-permute-start) | collective-permute-done | bytes 131104 | tf_op jit(solution)/shard_map/while/body/eval_jaxpr/ppermute | solution.py:15
  285.3 8.7 %fusion.59 = f32[16,4096]{1,0:T(8,128)S(1)} fusion(f32[16,4096]{1,0:T(8,128)S(1)} %get-tuple-element.261, bf16[896,4096]{1,0:T(8,128)(2,1)} %get-tuple-element.274, bf16[16,4096]{1,0:T(8,128)(2,1)S(1)} %copy.20, s32[896]{0:T(1024)S(1)} %broadcast_subtract_fusion.2, f32[896]{0:T(1024)S(1)} %get-tuple-element.275), kind=kOutput, calls=%fused_computation.6.clone.1 | convolution fusion | flops 235098112 | bytes 8002560 | tf_op jit(solution)/shard_map/while/body/eval_jaxpr/dot_general | solution.py:32
  294.1 10.0 %collective-permute-done = bf16[16,4096]{1,0:T(8,128)(2,1)S(1)} collective-permute-done((bf16[16,4096]{1,0:T(8,128)(2,1)S(1)}, bf16[16,4096]{1,0:T(8,128)(2,1)S(1)}, u32[]{:S(2)}, u32[]{:S(2)}) %collective-permute-start) | collective-permute-done | bytes 131104 | tf_op jit(solution)/shard_map/while/body/eval_jaxpr/ppermute | solution.py:15
  304.2 8.7 %fusion.59 = f32[16,4096]{1,0:T(8,128)S(1)} fusion(f32[16,4096]{1,0:T(8,128)S(1)} %get-tuple-element.261, bf16[896,4096]{1,0:T(8,128)(2,1)} %get-tuple-element.274, bf16[16,4096]{1,0:T(8,128)(2,1)S(1)} %copy.20, s32[896]{0:T(1024)S(1)} %broadcast_subtract_fusion.2, f32[896]{0:T(1024)S(1)} %get-tuple-element.275), kind=kOutput, calls=%fused_computation.6.clone.1 | convolution fusion | flops 235098112 | bytes 8002560 | tf_op jit(solution)/shard_map/while/body/eval_jaxpr/dot_general | solution.py:32
  312.9 9.5 %collective-permute-done = bf16[16,4096]{1,0:T(8,128)(2,1)S(1)} collective-permute-done((bf16[16,4096]{1,0:T(8,128)(2,1)S(1)}, bf16[16,4096]{1,0:T(8,128)(2,1)S(1)}, u32[]{:S(2)}, u32[]{:S(2)}) %collective-permute-start) | collective-permute-done | bytes 131104 | tf_op jit(solution)/shard_map/while/body/eval_jaxpr/ppermute | solution.py:15
  322.5 8.7 %fusion.59 = f32[16,4096]{1,0:T(8,128)S(1)} fusion(f32[16,4096]{1,0:T(8,128)S(1)} %get-tuple-element.261, bf16[896,4096]{1,0:T(8,128)(2,1)} %get-tuple-element.274, bf16[16,4096]{1,0:T(8,128)(2,1)S(1)} %copy.20, s32[896]{0:T(1024)S(1)} %broadcast_subtract_fusion.2, f32[896]{0:T(1024)S(1)} %get-tuple-element.275), kind=kOutput, calls=%fused_computation.6.clone.1 | convolution fusion | flops 235098112 | bytes 8002560 | tf_op jit(solution)/shard_map/while/body/eval_jaxpr/dot_general | solution.py:32
  331.2 9.5 %collective-permute-done = bf16[16,4096]{1,0:T(8,128)(2,1)S(1)} collective-permute-done((bf16[16,4096]{1,0:T(8,128)(2,1)S(1)}, bf16[16,4096]{1,0:T(8,128)(2,1)S(1)}, u32[]{:S(2)}, u32[]{:S(2)}) %collective-permute-start) | collective-permute-done | bytes 131104 | tf_op jit(solution)/shard_map/while/body/eval_jaxpr/ppermute | solution.py:15
  340.8 6.6 %gather_fusion.1 = bf16[896,4096]{1,0:T(8,128)(2,1)} fusion(bf16[64,4096]{1,0:T(8,128)(2,1)S(1)} %all_gather.3, s32[1024]{0:T(1024)S(1)} %pad_clamp_fusion.1), kind=kCustom, calls=%fused_computation.1 | custom fusion | bytes 14683648 | tf_op jit(solution)/shard_map/gather | solution.py:112
  348.0 7.2 %multiply_convert_fusion = bf16[896,4096]{1,0:T(8,128)(2,1)} fusion(bf16[896,4096]{1,0:T(8,128)(2,1)} %gather_fusion.1, f32[896]{0:T(1024)S(1)} %get-tuple-element.296, pred[896]{0:T(1024)(128)(4,1)S(1)} %compare_and_fusion, bf16[64,4096]{1,0:T(8,128)(2,1)S(1)} %all_gather.3, f32[896,64]{0,1:T(8,128)S(1)} %get-tuple-element.203), kind=kOutput, calls=%fused_computation.23 | convolution fusion | flops 491839488 | bytes 15438208 | tf_op jit(solution)/shard_map/dot_general | solution.py:114
  (63 shorter events, 35.0 us)
Async XLA Ops:
  6.4 16.5 %all-to-all-start = ((s32[8,1,1]{2,1,0:T(1,128)}), s32[8,1,1]{2,1,0:T(1,128)S(1)}, u32[]{:S(2)}, u32[]{:S(2)}) async-start(s32[8,1,1]{2,1,0:T(1,128)} %copy.13), calls=%async_computation | async-start | bytes 8192 | tf_op jit(solution)/shard_map/all_to_all | solution.py:68
  21.0 48.4 %copy-start.2 = (f32[1024]{0:T(1024)S(1)}, f32[1024]{0:T(1024)}, u32[]{:S(2)}) copy-start(f32[1024]{0:T(1024)} %param.15) | copy-start | bytes 12292
  22.9 35.0 %all-to-all-start.1 = ((bf16[8,154,1024]{2,1,0:T(8,128)(2,1)}), bf16[8,154,1024]{2,1,0:T(8,128)(2,1)S(1)}, u32[]{:S(2)}, u32[]{:S(2)}) async-start(bf16[8,154,1024]{2,1,0:T(8,128)(2,1)} %reshape.207), calls=%async_computation.1 | async-start | bytes 5242880 | tf_op jit(solution)/shard_map/all_to_all | solution.py:67
  107.0 12.3 %copy-start.1 = (s32[896]{0:T(1024)S(1)}, s32[896]{0:T(1024)}, u32[]{:S(2)}) copy-start(s32[896]{0:T(1024)} %param.17) | copy-start | bytes 10756
  107.0 121.8 %all-to-all-start.2 = ((bf16[8,154,4096]{2,1,0:T(8,128)(2,1)}), bf16[8,154,4096]{2,1,0:T(8,128)(2,1)}, u32[]{:S(2)}, u32[]{:S(2)}) async-start(bf16[8,154,4096]{2,1,0:T(8,128)(2,1)} %broadcast_select_fusion), calls=%async_computation.2 | async-start | bytes 20971520 | tf_op jit(solution)/shard_map/all_to_all | solution.py:96
  241.0 22.0 %copy-start = (bf16[896,4096]{1,0:T(8,128)(2,1)S(1)}, bf16[896,4096]{1,0:T(8,128)(2,1)}, u32[]{:S(2)}) copy-start(bf16[896,4096]{1,0:T(8,128)(2,1)} %fusion.11) | copy-start | bytes 22020100
  274.1 11.1 %collective-permute-start.1 = (f32[16,4096]{1,0:T(8,128)S(1)}, f32[16,4096]{1,0:T(8,128)S(1)}, u32[]{:S(2)}, u32[]{:S(2)}) collective-permute-start(f32[16,4096]{1,0:T(8,128)S(1)} %fusion.59), channel_id=1, source_target_pairs={{0,1},{1,2},{2,3},{3,0},{4,5},{5,6},{6,7},{7,4},{8,9},{9,10},{10,1... | collective-permute-start | bytes 786440 | tf_op jit(solution)/shard_map/while/body/eval_jaxpr/ppermute | solution.py:15
  276.1 9.2 %collective-permute-start = (bf16[16,4096]{1,0:T(8,128)(2,1)S(1)}, bf16[16,4096]{1,0:T(8,128)(2,1)S(1)}, u32[]{:S(2)}, u32[]{:S(2)}) collective-permute-start(bf16[16,4096]{1,0:T(8,128)(2,1)S(1)} %copy.20), channel_id=1, source_target_pairs={{0,1},{1,2},{2,3},{3,0},{4,5},{5,6},{6,7},{7,4},{8,9},{9,10},{10,1... | collective-permute-start | bytes 393224 | tf_op jit(solution)/shard_map/while/body/eval_jaxpr/ppermute | solution.py:15
  294.0 10.1 %collective-permute-start.1 = (f32[16,4096]{1,0:T(8,128)S(1)}, f32[16,4096]{1,0:T(8,128)S(1)}, u32[]{:S(2)}, u32[]{:S(2)}) collective-permute-start(f32[16,4096]{1,0:T(8,128)S(1)} %fusion.59), channel_id=1, source_target_pairs={{0,1},{1,2},{2,3},{3,0},{4,5},{5,6},{6,7},{7,4},{8,9},{9,10},{10,1... | collective-permute-start | bytes 786440 | tf_op jit(solution)/shard_map/while/body/eval_jaxpr/ppermute | solution.py:15
  294.0 10.1 %collective-permute-start = (bf16[16,4096]{1,0:T(8,128)(2,1)S(1)}, bf16[16,4096]{1,0:T(8,128)(2,1)S(1)}, u32[]{:S(2)}, u32[]{:S(2)}) collective-permute-start(bf16[16,4096]{1,0:T(8,128)(2,1)S(1)} %copy.20), channel_id=1, source_target_pairs={{0,1},{1,2},{2,3},{3,0},{4,5},{5,6},{6,7},{7,4},{8,9},{9,10},{10,1... | collective-permute-start | bytes 393224 | tf_op jit(solution)/shard_map/while/body/eval_jaxpr/ppermute | solution.py:15
  312.9 9.6 %collective-permute-start.1 = (f32[16,4096]{1,0:T(8,128)S(1)}, f32[16,4096]{1,0:T(8,128)S(1)}, u32[]{:S(2)}, u32[]{:S(2)}) collective-permute-start(f32[16,4096]{1,0:T(8,128)S(1)} %fusion.59), channel_id=1, source_target_pairs={{0,1},{1,2},{2,3},{3,0},{4,5},{5,6},{6,7},{7,4},{8,9},{9,10},{10,1... | collective-permute-start | bytes 786440 | tf_op jit(solution)/shard_map/while/body/eval_jaxpr/ppermute | solution.py:15
  312.9 9.6 %collective-permute-start = (bf16[16,4096]{1,0:T(8,128)(2,1)S(1)}, bf16[16,4096]{1,0:T(8,128)(2,1)S(1)}, u32[]{:S(2)}, u32[]{:S(2)}) collective-permute-start(bf16[16,4096]{1,0:T(8,128)(2,1)S(1)} %copy.20), channel_id=1, source_target_pairs={{0,1},{1,2},{2,3},{3,0},{4,5},{5,6},{6,7},{7,4},{8,9},{9,10},{10,1... | collective-permute-start | bytes 393224 | tf_op jit(solution)/shard_map/while/body/eval_jaxpr/ppermute | solution.py:15
  331.2 9.6 %collective-permute-start.1 = (f32[16,4096]{1,0:T(8,128)S(1)}, f32[16,4096]{1,0:T(8,128)S(1)}, u32[]{:S(2)}, u32[]{:S(2)}) collective-permute-start(f32[16,4096]{1,0:T(8,128)S(1)} %fusion.59), channel_id=1, source_target_pairs={{0,1},{1,2},{2,3},{3,0},{4,5},{5,6},{6,7},{7,4},{8,9},{9,10},{10,1... | collective-permute-start | bytes 786440 | tf_op jit(solution)/shard_map/while/body/eval_jaxpr/ppermute | solution.py:15
  331.2 9.6 %collective-permute-start = (bf16[16,4096]{1,0:T(8,128)(2,1)S(1)}, bf16[16,4096]{1,0:T(8,128)(2,1)S(1)}, u32[]{:S(2)}, u32[]{:S(2)}) collective-permute-start(bf16[16,4096]{1,0:T(8,128)(2,1)S(1)} %copy.20), channel_id=1, source_target_pairs={{0,1},{1,2},{2,3},{3,0},{4,5},{5,6},{6,7},{7,4},{8,9},{9,10},{10,1... | collective-permute-start | bytes 393224 | tf_op jit(solution)/shard_map/while/body/eval_jaxpr/ppermute | solution.py:15
where the time goes:
time: 357 us; the launch traced here: 356 us
  waiting for transfers between devices  164 us (46%)
  local copies, waits for them, and re-layouts  69.4 us (19%)
  matrix products  57.2 us (16%)
  other arithmetic  29.9 us (8%)
  starting transfers between devices  17.3 us (5%)
  blocking collectives  16.3 us (5%)
    all_to_all x1, waiting for transfers between devices, on_device(): lax.all_to_all(outgoing, 'dp', split_axis=0, concat_axis=0, tiled=True)  95.9 us
    ppermute x8, waiting for transfers between devices, passed_along(): lax.ppermute(shard, axis, [(i, (i + by) % length) for i in range(length)])  38.2 us
    dot_general x4, matrix products, contract_first(): lax.dot_general(left_side, right_side, (((0,), (0,)), ((), ())), preferre...  34.8 us
    all_to_all x1, waiting for transfers between devices, on_device(): lax.all_to_all(send_rows, 'dp', split_axis=0, concat_axis=0, tiled=True)  30 us
    gather x2, local copies, waits for them, and re-layouts, on_device(): embedded[gather_at]  20.4 us
    all_gather x1, blocking collectives, on_device(): doc_piece = lax.all_gather(doc_unit, 'blk', axis=0, tiled=True)  16.3 us
    reshape x1, local copies, waits for them, and re-layouts, on_device(): returned.reshape(groups * capacity, emb_width)  12.2 us
    select_n x1, other arithmetic, on_device(): jnp.where(valid_slots.reshape(groups * capacity)[:, None], embedded[gathe...  9.97 us
  transfers between devices with their start and end apart: 11, of which 6 were waited for; matrix products, arithmetic and copies ran while one was open for 9% of the time, Pallas kernels for 0%

commit v1 on v0

v1 whole, which is shorter than its diff:
```python
import jax
import jax.numpy as jnp
from jax import lax
from jax.sharding import PartitionSpec as P

SESS_DEV = 16


logit_scale = 20.0
epsilon = 1e-06


def unit_rows(values):
    widened = values.astype(jnp.float32)
    return (
        widened * lax.rsqrt(jnp.sum(widened * widened, axis=-1, keepdims=True) + epsilon)
    ).astype(jnp.bfloat16)


def contract_rows(left_side, right_side):
    return lax.dot_general(
        left_side, right_side, (((1,), (1,)), ((), ())), preferred_element_type=jnp.float32
    )


def contract_first(left_side, right_side):
    return lax.dot_general(
        left_side, right_side, (((0,), (0,)), ((), ())), preferred_element_type=jnp.float32
    )


def on_device(
    spans, span_counts, session_ids, destinations, expert_weight, norm_gain, queries, positives
):
    rows_dev = spans.shape[0]
    hidden_width = spans.shape[1]
    groups = lax.axis_size("dp")
    capacity = (rows_dev - 3 * SESS_DEV) // groups
    received = rows_dev // 4
    cycle = rows_dev // groups
    count = span_counts[0]

    lane_of = (jnp.arange(groups, dtype=jnp.int32) - destinations[0]) % groups
    by_lane = spans.reshape(cycle, groups, hidden_width)
    send_rows = jnp.swapaxes(jnp.take(by_lane, lane_of, axis=1), 0, 1)[:, :capacity]
    row_of = lane_of[:, None] + groups * jnp.arange(capacity, dtype=jnp.int32)[None, :]
    ids_by_lane = session_ids.reshape(cycle, groups)
    send_ids = jnp.where(
        row_of < count, jnp.swapaxes(jnp.take(ids_by_lane, lane_of, axis=1), 0, 1)[:, :capacity], -1
    )
    got_rows = lax.all_to_all(send_rows, "dp", split_axis=0, concat_axis=0, tiled=True)
    got_ids = lax.all_to_all(send_ids, "dp", split_axis=0, concat_axis=0, tiled=True)

    got_counts = jnp.sum((got_ids >= 0).astype(jnp.int32), axis=1)
    starts = jnp.cumsum(got_counts) - got_counts
    packed_index = jnp.arange(received, dtype=jnp.int32)
    source_of = (
        jnp.sum((starts[None, :] <= packed_index[:, None]).astype(jnp.int32), axis=1) - 1
    )
    slot_of = source_of * capacity + packed_index - starts[source_of]
    packed_live = packed_index < jnp.sum(got_counts)
    slot_of = jnp.where(packed_live, slot_of, 0)
    packed = got_rows.reshape(groups * capacity, hidden_width)[slot_of]
    packed_key = jnp.where(
        packed_live, source_of * SESS_DEV + got_ids.reshape(groups * capacity)[slot_of], -1
    )

    widened = packed.astype(jnp.float32)
    normed = (
        widened
        * lax.rsqrt(jnp.mean(widened * widened, axis=-1, keepdims=True) + epsilon)
        * norm_gain
    ).astype(jnp.bfloat16)
    embedded = jax.nn.gelu(
        jnp.dot(normed, expert_weight[0], preferred_element_type=jnp.float32), approximate=True
    ).astype(jnp.bfloat16)
    emb_width = embedded.shape[1]
    selector = (
        jnp.arange(groups * SESS_DEV, dtype=jnp.int32)[:, None] == packed_key[None, :]
    ).astype(jnp.bfloat16)
    partial = jnp.dot(selector, embedded, preferred_element_type=jnp.float32)
    pooled = lax.psum_scatter(partial, "dp", scatter_dimension=0, tiled=True)

    doc_unit = unit_rows(pooled)
    query_unit = unit_rows(queries)
    doc_piece = lax.all_gather(doc_unit, "blk", axis=0, tiled=True)
    piece_rows = doc_piece.shape[0]
    logits = logit_scale * contract_rows(query_unit, doc_piece)
    weights = jnp.exp(logits)
    totals = jnp.sum(weights, axis=1)
    numerator = jnp.dot(weights.astype(jnp.bfloat16), doc_piece, preferred_element_type=jnp.float32)
    matches = positives[:, None] == jnp.arange(piece_rows, dtype=jnp.int32)[None, :]
    chosen_logit = jnp.sum(jnp.where(matches, logits, 0.0), axis=1)
    chosen_doc = doc_piece[jnp.clip(positives, 0, piece_rows - 1)].astype(jnp.float32)
    loss_rows = jnp.log(totals) - chosen_logit
    grad_queries = (logit_scale * (numerator / totals[:, None] - chosen_doc)).astype(jnp.bfloat16)
    coefficient = (weights / totals[:, None] - matches.astype(jnp.float32)).astype(jnp.bfloat16)
    grad_part = logit_scale * contract_first(coefficient, query_unit)
    grad_docs = lax.psum_scatter(grad_part, "blk", scatter_dimension=0, tiled=True)
    return (loss_rows, grad_queries, grad_docs)


def solution(mesh):
    placed = (
        P(("dp", "blk"), None),
        P(("dp", "blk")),
        P(("dp", "blk")),
        P(("dp", "blk")),
        P("dp", None, None),
        P(),
        P(("dp", "blk"), None),
        P(("dp", "blk")),
    )
    return jax.shard_map(
        on_device,
        mesh=mesh,
        in_specs=placed,
        out_specs=(P(("dp", "blk")), P(("dp", "blk"), None), P(("dp", "blk"), None)),
        check_vma=False,
    )
```

time: 357 us -> 180 us (0.50)
  waiting for transfers between devices: 164 us -> 71.6 us
  local copies, waits for them, and re-layouts: 69.4 us -> 22.4 us
  matrix products: 57.2 us -> 23.5 us
  between operations: 1.44 us -> 14.9 us
  other arithmetic: 29.9 us -> 20.8 us
  starting transfers between devices: 17.3 us -> 8.69 us
    all_to_all x2 -> x1, waiting for transfers between devices: 95.9 us -> 0.01 us  [on_device(): lax.all_to_all(send_ids, 'dp', split_axis=0, concat_axis=0, tiled=True)]
    reduce_scatter x0 -> x2, waiting for transfers between devices: none -> 51.3 us  [the longest x1 37 us: on_device(): pooled = lax.psum_scatter(partial, 'dp', scatter_dimension=0, tiled=True)]
    ppermute x8 -> x0, waiting for transfers between devices: 38.2 us -> none  [passed_along(): lax.ppermute(shard, axis, [(i, (i + by) % length) for i in range(length)])]
    dot_general x4 -> x1, matrix products: 34.8 us -> 2.76 us  [contract_first(): lax.dot_general(left_side, right_side, (((0,), (0,)), ((), ())), preferre...]
    scatter x3 -> x0, local copies, waits for them, and re-layouts: 24.8 us -> none  [the longest x1 9.67 us: on_device(): send_rows = jnp.zeros((groups * capacity, hidden_width), jnp.bfloat16).at...]
    gather x2 -> x5, local copies, waits for them, and re-layouts: 20.4 us -> 7.8 us  [the longest x1 2.23 us: on_device(): got_ids.reshape(groups * capacity)[slot_of]]
    all_to_all x1, waiting for transfers between devices: 30 us -> 20.2 us  [on_device(): lax.all_to_all(send_rows, 'dp', split_axis=0, concat_axis=0, tiled=True)]
    reshape x3 -> x5, local copies, waits for them, and re-layouts: 15.8 us -> 6.17 us  [the longest x1 3.18 us: on_device(): by_lane = spans.reshape(cycle, groups, hidden_width)]
  transfers between devices with their start and end apart: 11 -> 4, of which waited for: 6 -> 3; matrix products, arithmetic and copies ran while one was open for 9% -> 21% of each run, Pallas kernels for 0% -> 0%
where the time goes in v1:
time: 180 us; the launch traced here: 178 us
  waiting for transfers between devices  71.6 us (40%)
  matrix products  23.5 us (13%)
  local copies, waits for them, and re-layouts  22.4 us (12%)
  other arithmetic  20.8 us (12%)
  blocking collectives  16 us (9%)
  between operations  14.9 us (8%)
  starting transfers between devices  8.69 us (5%)
    reduce_scatter x1, waiting for transfers between devices, on_device(): pooled = lax.psum_scatter(partial, 'dp', scatter_dimension=0, tiled=True)  37 us
    all_to_all x1, waiting for transfers between devices, on_device(): lax.all_to_all(send_rows, 'dp', split_axis=0, concat_axis=0, tiled=True)  20.2 us
    all_gather x1, blocking collectives, on_device(): doc_piece = lax.all_gather(doc_unit, 'blk', axis=0, tiled=True)  16 us
    reduce_scatter x1, waiting for transfers between devices, on_device(): lax.psum_scatter(grad_part, 'blk', scatter_dimension=0, tiled=True)  14.3 us
    dot_general x1, matrix products, on_device(): partial = jnp.dot(selector, embedded, preferred_element_type=jnp.float32)  8.53 us
    gather x1, local copies, waits for them, and re-layouts, on_device(): doc_piece[jnp.clip(positives, 0, piece_rows - 1)].astype(jnp.float32)  6.6 us
    dot_general x1, matrix products, on_device(): jnp.dot(weights.astype(jnp.bfloat16), doc_piece, preferred_element_type=j...  6.56 us
    dot_general x1, matrix products, contract_rows(): lax.dot_general(left_side, right_side, (((1,), (1,)), ((), ())), preferre...  5.69 us
  transfers between devices with their start and end apart: 4, of which 3 were waited for; matrix products, arithmetic and copies ran while one was open for 21% of the time, Pallas kernels for 0%

profile of v1, /device:TPU:2, one launch (start us, length us, event | category | flops | bytes accessed | tf_op | source)
XLA Modules:
  0.0 177.9 jit_solution(11820777106611902792)
XLA Ops:
  7.2 1.2 slice.9
  11.0 0.8 reshape.202
  13.1 4.3 %all-to-all-start = ((s32[8,1,154]{2,1,0:T(1,128)}), s32[8,1,154]{2,1,0:T(1,128)S(1)}, u32[]{:S(2)}, u32[]{:S(2)}) async-start(s32[8,1,154]{2,1,0:T(1,128)} %copy.18), calls=%async_computation | async-start | bytes 16384 | tf_op jit(solution)/shard_map/all_to_all | solution.py:52
  17.4 3.2 %copy.19 = bf16[160,8,1024]{2,0,1:T(8,128)(2,1)S(1)} copy(bf16[160,8,1024]{2,1,0:T(8,128)(2,1)} %bitcast.30) | data formatting | bytes 5242880 | tf_op jit(solution)/shard_map/reshape | solution.py:44
  20.6 2.2 %gather_fusion.2 = bf16[8,160,1024]{2,1,0:T(8,128)(2,1)} fusion(bf16[160,8,1024]{2,0,1:T(8,128)(2,1)S(1)} %copy.19, s32[1024]{0:T(1024)S(1)} %pad_clamp_fusion.2), kind=kCustom, calls=%fused_computation.2 | custom fusion | bytes 5242912 | tf_op jit(solution)/shard_map/jit(_take)/gather | solution.py:45
  22.8 3.6 %slice_select_fusion = bf16[8,154,1024]{2,1,0:T(8,128)(2,1)} fusion(bf16[8,160,1024]{2,1,0:T(8,128)(2,1)} %gather_fusion.2, pred[8]{0:T(512)(128)(4,1)S(1)} %compare_and_fusion), kind=kLoop, calls=%fused_computation.23 | loop fusion | flops 1261568 | bytes 5046280 | tf_op jit(solution)/shard_map/jit(_take)/select_n | solution.py:45
  26.4 4.4 %all-to-all-start.1 = ((bf16[8,154,1024]{2,1,0:T(8,128)(2,1)}), bf16[8,154,1024]{2,1,0:T(8,128)(2,1)}, u32[]{:S(2)}, u32[]{:S(2)}) async-start(bf16[8,154,1024]{2,1,0:T(8,128)(2,1)} %slice_select_fusion), calls=%async_computation.1 | async-start | bytes 5242880 | tf_op jit(solution)/shard_map/all_to_all | solution.py:51
  30.8 0.8 fusion.48
  32.6 4.4 %fusion.39 = (s32[320]{0:T(512)S(1)}, s32[320,1]{0,1:T(1,128)S(1)}) fusion(s32[]{:T(128)} %bitcast.7, s32[]{:T(128)} %bitcast.8, s32[]{:T(128)} %bitcast.9, s32[]{:T(128)} %bitcast.10, s32[]{:T(128)} %bitcast.11, s32[]{:T(128)} %bitcast.13, s32[]{:T(128)} %bitcast.12, s32[320]{0:T(512)S(1)} %get-tuple-element.11, s32[320]{0:T(512)S(1)} %get-tuple-element.10), kind=kLoop, calls=%fused_computation.81 | loop fusion | flops 4480 | bytes 5148 | tf_op jit(solution)/shard_map/gather | solution.py:60
  38.4 2.2 %gather_fusion.1 = s32[320]{0:T(512)S(1)} fusion(s32[1232]{0:T(1024)S(1)} %reshape.205, s32[1024]{0:T(1024)S(1)} %pad_clamp_fusion.1), kind=kCustom, calls=%fused_computation.1 | custom fusion | bytes 3840 | tf_op jit(solution)/shard_map/gather | solution.py:65
  41.3 20.2 %all-to-all-done.1 = bf16[8,154,1024]{2,1,0:T(8,128)(2,1)} async-done(((bf16[8,154,1024]{2,1,0:T(8,128)(2,1)}), bf16[8,154,1024]{2,1,0:T(8,128)(2,1)}, u32[]{:S(2)}, u32[]{:S(2)}) %all-to-all-start.1) | async-done | bytes 2523168 | tf_op jit(solution)/shard_map/all_to_all | solution.py:51
  61.5 2.1 %reshape.207 = bf16[1232,1024]{1,0:T(8,128)(2,1)S(1)} reshape(bf16[8,154,1024]{2,1,0:T(8,128)(2,1)} %all-to-all-done.1) | data formatting | bytes 5046272 | tf_op jit(solution)/shard_map/reshape | solution.py:63
  63.6 2.1 %gather_fusion.3 = bf16[320,1024]{1,0:T(8,128)(2,1)S(1)} fusion(bf16[1232,1024]{1,0:T(8,128)(2,1)S(1)} %reshape.207, s32[1024]{0:T(1024)S(1)} %pad_clamp_fusion.1), kind=kCustom, calls=%fused_computation.3 | custom fusion | bytes 1312000 | tf_op jit(solution)/shard_map/gather | solution.py:63
  65.9 8.5 %fusion.18 = f32[128,4096]{1,0:T(8,128)} fusion(bf16[1,1024,4096]{2,1,0:T(8,128)(2,1)} %param.12, bf16[320,1024]{1,0:T(8,128)(2,1)S(1)} %gather_fusion.3, f32[1024]{0:T(1024)S(1)} %copy-done.1, f32[320]{0:T(512)S(1)} %add_rsqrt_fusion.1, s32[320]{0:T(512)S(1)} %add_select_fusion), kind=kOutput, calls=%fused_computation.24 | convolution fusion | flops 3033047040 | bytes 11147776 | tf_op jit(solution)/shard_map/dot_general | solution.py:81
  74.5 4.6 %fusion = f32[896]{0:T(1024)S(1)} fusion(bf16[896,4096]{1,0:T(8,128)(2,1)} %param.14), kind=kLoop, calls=%fused_computation.7 | loop fusion | flops 11009152 | bytes 7343616 | tf_op jit(solution)/shard_map/reduce_sum | solution.py:16
  79.1 37.0 %reduce-scatter.3.cloned.1.call-done = f32[16,4096]{1,0:T(8,128)} async-done(((f32[128,4096]{1,0:T(8,128)}), f32[16,4096]{1,0:T(8,128)}) %reduce-scatter.3.cloned.1.call-update) | async-done | bytes 262160 | tf_op jit(solution)/shard_map/reduce_scatter | solution.py:82
  116.2 1.1 multiply_reduce_fusion
  117.3 1.2 multiply_convert_fusion.1
  118.5 16.0 %all_gather.3 = bf16[64,4096]{1,0:T(8,128)(2,1)S(1)} all-gather(bf16[16,4096]{1,0:T(8,128)(2,1)S(1)} %multiply_convert_fusion.1), channel_id=1, replica_groups=mesh['dp'=8,'blk'=4] {'blk'}, dimensions={0}, use_global_device_ids=true | all-gather | bytes 655360 | tf_op jit(solution)/shard_map/all_gather | solution.py:86
  134.4 5.7 %exponential_reduce_fusion = (f32[896]{0:T(1024)S(1)}, f32[896]{0:T(1024)S(1)}, f32[896,64]{0,1:T(8,128)S(1)}) fusion(s32[896]{0:T(1024)S(1)} %copy-done, bf16[64,4096]{1,0:T(8,128)(2,1)S(1)} %all_gather.3, bf16[896,4096]{1,0:T(8,128)(2,1)} %param.14, f32[896]{0:T(1024)S(1)} %add_rsqrt_fusion), kind=kOutput, calls=%fused_computation.39 | convolution fusion | flops 481057024 | bytes 8108032 | tf_op jit(solution)/shard_map/dot_general | solution.py:21
  140.2 2.8 %convolution_multiply_fusion = f32[64,4096]{1,0:T(8,128)} fusion(bf16[896,4096]{1,0:T(8,128)(2,1)S(1)} %bitcast.29, f32[896]{0:T(1024)S(1)} %add_rsqrt_fusion, f32[896,64]{0,1:T(8,128)S(1)} %get-tuple-element.20, f32[896]{0:T(1024)S(1)} %get-tuple-element.3, s32[896]{0:T(1024)S(1)} %copy-done), kind=kOutput, calls=%fused_computation.21 | convolution fusion | flops 481320960 | bytes 8628736 | tf_op jit(solution)/shard_map/dot_general | solution.py:27
  143.0 6.6 %gather_fusion.4 = bf16[896,4096]{1,0:T(8,128)(2,1)} fusion(bf16[64,4096]{1,0:T(8,128)(2,1)S(1)} %all_gather.3, s32[1024]{0:T(1024)S(1)} %pad_clamp_fusion), kind=kCustom, calls=%fused_computation.4 | custom fusion | bytes 14683648 | tf_op jit(solution)/shard_map/gather | solution.py:94
  150.2 6.6 %multiply_convert_fusion = bf16[896,4096]{1,0:T(8,128)(2,1)} fusion(bf16[896,4096]{1,0:T(8,128)(2,1)} %gather_fusion.4, f32[896]{0:T(1024)S(1)} %get-tuple-element.3, bf16[64,4096]{1,0:T(8,128)(2,1)S(1)} %all_gather.3, f32[896,64]{0,1:T(8,128)S(1)} %get-tuple-element.20), kind=kOutput, calls=%fused_computation.9 | convolution fusion | flops 488169472 | bytes 15437312 | tf_op jit(solution)/shard_map/dot_general | solution.py:91
  156.7 14.3 %reduce-scatter.5.cloned.1.call-done = f32[16,4096]{1,0:T(8,128)} async-done(((f32[64,4096]{1,0:T(8,128)}), f32[16,4096]{1,0:T(8,128)}) %reduce-scatter.5.cloned.1.call-update) | async-done | bytes 262160 | tf_op jit(solution)/shard_map/reduce_scatter | solution.py:99
  (41 shorter events, 7.4 us)
Async XLA Ops:
  13.1 13.2 %all-to-all-start = ((s32[8,1,154]{2,1,0:T(1,128)}), s32[8,1,154]{2,1,0:T(1,128)S(1)}, u32[]{:S(2)}, u32[]{:S(2)}) async-start(s32[8,1,154]{2,1,0:T(1,128)} %copy.18), calls=%async_computation | async-start | bytes 16384 | tf_op jit(solution)/shard_map/all_to_all | solution.py:52
  26.4 35.2 %all-to-all-start.1 = ((bf16[8,154,1024]{2,1,0:T(8,128)(2,1)}), bf16[8,154,1024]{2,1,0:T(8,128)(2,1)}, u32[]{:S(2)}, u32[]{:S(2)}) async-start(bf16[8,154,1024]{2,1,0:T(8,128)(2,1)} %slice_select_fusion), calls=%async_computation.1 | async-start | bytes 5242880 | tf_op jit(solution)/shard_map/all_to_all | solution.py:51
  30.7 85.4 %reduce-scatter.3.cloned.1.call-start = ((), (), s32[]{:S(2)}) async-start(), calls=%async_computation.4 | async-start | bytes 2359296 | tf_op jit(solution)/shard_map/reduce_scatter | solution.py:82
  41.3 24.6 %copy-start.1 = (f32[1024]{0:T(1024)S(1)}, f32[1024]{0:T(1024)}, u32[]{:S(2)}) copy-start(f32[1024]{0:T(1024)} %param.13) | copy-start | bytes 12292
  74.5 4.7 %copy-start = (s32[896]{0:T(1024)S(1)}, s32[896]{0:T(1024)}, u32[]{:S(2)}) copy-start(s32[896]{0:T(1024)} %param.15) | copy-start | bytes 10756
  74.5 96.6 %reduce-scatter.5.cloned.1.call-start = ((), (), s32[]{:S(2)}) async-start(), calls=%async_computation.5 | async-start | bytes 1310720 | tf_op jit(solution)/shard_map/reduce_scatter | solution.py:99
  117.3 22.9 %slice-start = ((s8[7340032]{0:T(1024)(128)(4,1)}), s8[4194304]{0:T(1024)(128)(4,1)S(1)}, s32[]{:S(2)}) async-start(s8[7340032]{0:T(1024)(128)(4,1)} %bitcast.28), calls=%async_computation.6 | async-start | bytes 8388608
  134.4 5.7 %slice-start.1 = ((s8[7340032]{0:T(1024)(128)(4,1)}), s8[3145728]{0:T(1024)(128)(4,1)S(1)}, s32[]{:S(2)}) async-start(s8[7340032]{0:T(1024)(128)(4,1)} %bitcast.28), calls=%async_computation.7 | async-start | bytes 6291456
Sparse Core Ops, SparseCore 0:
  74.6 41.5 reduce-scatter.2
  143.1 27.9 reduce-scatter.4

commit v2 on v1

--- a/solution.py
+++ b/solution.py
@@ -79,7 +79,9 @@
         jnp.arange(groups * SESS_DEV, dtype=jnp.int32)[:, None] == packed_key[None, :]
     ).astype(jnp.bfloat16)
     partial = jnp.dot(selector, embedded, preferred_element_type=jnp.float32)
-    pooled = lax.psum_scatter(partial, "dp", scatter_dimension=0, tiled=True)
+    partial = partial.astype(jnp.bfloat16).reshape(groups, SESS_DEV, emb_width)
+    returned = lax.all_to_all(partial, "dp", split_axis=0, concat_axis=0, tiled=True)
+    pooled = jnp.sum(returned.astype(jnp.float32), axis=0)
 
     doc_unit = unit_rows(pooled)
     query_unit = unit_rows(queries)
@@ -91,7 +93,9 @@
     numerator = jnp.dot(weights.astype(jnp.bfloat16), doc_piece, preferred_element_type=jnp.float32)
     matches = positives[:, None] == jnp.arange(piece_rows, dtype=jnp.int32)[None, :]
     chosen_logit = jnp.sum(jnp.where(matches, logits, 0.0), axis=1)
-    chosen_doc = doc_piece[jnp.clip(positives, 0, piece_rows - 1)].astype(jnp.float32)
+    chosen_doc = jnp.dot(
+        matches.astype(jnp.bfloat16), doc_piece, preferred_element_type=jnp.float32
+    )
     loss_rows = jnp.log(totals) - chosen_logit
     grad_queries = (logit_scale * (numerator / totals[:, None] - chosen_doc)).astype(jnp.bfloat16)
     coefficient = (weights / totals[:, None] - matches.astype(jnp.float32)).astype(jnp.bfloat16)

time: 180 us -> 162 us (0.900)
  waiting for transfers between devices: 71.6 us -> 48.7 us
  matrix products: 23.5 us -> 32.1 us
  local copies, waits for them, and re-layouts: 22.4 us -> 15.8 us
  starting transfers between devices: 8.69 us -> 13.6 us
  other arithmetic: 20.8 us -> 18.9 us
    reduce_scatter x1 -> x0, waiting for transfers between devices: 37 us -> none  [on_device(): pooled = lax.psum_scatter(partial, 'dp', scatter_dimension=0, tiled=True)]
    all_to_all x0 -> x1, waiting for transfers between devices: none -> 9.32 us  [on_device(): lax.all_to_all(partial, 'dp', split_axis=0, concat_axis=0, tiled=True)]
    dot_general x0 -> x1, matrix products: none -> 8.18 us  [on_device(): jnp.dot(matches.astype(jnp.bfloat16), doc_piece, preferred_element_type=j...]
    gather x1 -> x0, local copies, waits for them, and re-layouts: 6.6 us -> none  [on_device(): doc_piece[jnp.clip(positives, 0, piece_rows - 1)].astype(jnp.float32)]
    all_to_all x0 -> x1, starting transfers between devices: none -> 4.99 us  [on_device(): lax.all_to_all(partial, 'dp', split_axis=0, concat_axis=0, tiled=True)]
    reduce_scatter x1, waiting for transfers between devices: 14.3 us -> 19.1 us  [on_device(): lax.psum_scatter(grad_part, 'blk', scatter_dimension=0, tiled=True)]
  transfers between devices with their start and end apart: 4 -> 4, of which waited for: 3 -> 3; matrix products, arithmetic and copies ran while one was open for 21% -> 20% of each run, Pallas kernels for 0% -> 0%
where the time goes in v2:
time: 162 us; the launch traced here: 160 us
  waiting for transfers between devices  48.7 us (30%)
  matrix products  32.1 us (20%)
  other arithmetic  18.9 us (12%)
  blocking collectives  16.2 us (10%)
  local copies, waits for them, and re-layouts  15.8 us (10%)
  between operations  14.8 us (9%)
  starting transfers between devices  13.6 us (8%)
    all_to_all x1, waiting for transfers between devices, on_device(): lax.all_to_all(send_rows, 'dp', split_axis=0, concat_axis=0, tiled=True)  20.3 us
    reduce_scatter x1, waiting for transfers between devices, on_device(): lax.psum_scatter(grad_part, 'blk', scatter_dimension=0, tiled=True)  19.1 us
    all_gather x1, blocking collectives, on_device(): doc_piece = lax.all_gather(doc_unit, 'blk', axis=0, tiled=True)  16.2 us
    all_to_all x1, waiting for transfers between devices, on_device(): lax.all_to_all(partial, 'dp', split_axis=0, concat_axis=0, tiled=True)  9.32 us
    dot_general x1, matrix products, on_device(): jnp.dot(matches.astype(jnp.bfloat16), doc_piece, preferred_element_type=j...  8.18 us
    dot_general x1, matrix products, on_device(): partial = jnp.dot(selector, embedded, preferred_element_type=jnp.float32)  8.17 us
    dot_general x1, matrix products, on_device(): jnp.dot(weights.astype(jnp.bfloat16), doc_piece, preferred_element_type=j...  7.32 us
    dot_general x1, matrix products, contract_rows(): lax.dot_general(left_side, right_side, (((1,), (1,)), ((), ())), preferre...  5.69 us
  transfers between devices with their start and end apart: 4, of which 3 were waited for; matrix products, arithmetic and copies ran while one was open for 20% of the time, Pallas kernels for 0%

profile of v2, /device:TPU:2, one launch (start us, length us, event | category | flops | bytes accessed | tf_op | source)
XLA Modules:
  0.0 160.2 jit_solution(16266714974385167331)
XLA Ops:
  7.2 1.2 slice.9
  10.4 0.8 reshape.205
  13.2 4.3 %all-to-all-start = ((s32[8,1,154]{2,1,0:T(1,128)}), s32[8,1,154]{2,1,0:T(1,128)S(1)}, u32[]{:S(2)}, u32[]{:S(2)}) async-start(s32[8,1,154]{2,1,0:T(1,128)} %copy.18), calls=%async_computation | async-start | bytes 16384 | tf_op jit(solution)/shard_map/all_to_all | solution.py:52
  17.4 3.2 %copy.19 = bf16[160,8,1024]{2,0,1:T(8,128)(2,1)S(1)} copy(bf16[160,8,1024]{2,1,0:T(8,128)(2,1)} %bitcast.32) | data formatting | bytes 5242880 | tf_op jit(solution)/shard_map/reshape | solution.py:44
  20.6 2.2 %gather_fusion.2 = bf16[8,160,1024]{2,1,0:T(8,128)(2,1)} fusion(bf16[160,8,1024]{2,0,1:T(8,128)(2,1)S(1)} %copy.19, s32[1024]{0:T(1024)S(1)} %pad_clamp_fusion.1), kind=kCustom, calls=%fused_computation.2 | custom fusion | bytes 5242912 | tf_op jit(solution)/shard_map/jit(_take)/gather | solution.py:45
  22.8 3.6 %slice_select_fusion = bf16[8,154,1024]{2,1,0:T(8,128)(2,1)} fusion(bf16[8,160,1024]{2,1,0:T(8,128)(2,1)} %gather_fusion.2, pred[8]{0:T(512)(128)(4,1)S(1)} %compare_and_fusion), kind=kLoop, calls=%fused_computation.23 | loop fusion | flops 1261568 | bytes 5046280 | tf_op jit(solution)/shard_map/jit(_take)/select_n | solution.py:45
  26.4 4.4 %all-to-all-start.1 = ((bf16[8,154,1024]{2,1,0:T(8,128)(2,1)}), bf16[8,154,1024]{2,1,0:T(8,128)(2,1)}, u32[]{:S(2)}, u32[]{:S(2)}) async-start(bf16[8,154,1024]{2,1,0:T(8,128)(2,1)} %slice_select_fusion), calls=%async_computation.1 | async-start | bytes 5242880 | tf_op jit(solution)/shard_map/all_to_all | solution.py:51
  30.7 0.8 fusion.49
  31.8 0.7 fusion.50
  32.6 4.4 %fusion.40 = (s32[320]{0:T(512)S(1)}, s32[320,1]{0,1:T(1,128)S(1)}) fusion(s32[]{:T(128)} %bitcast.7, s32[]{:T(128)} %bitcast.8, s32[]{:T(128)} %bitcast.9, s32[]{:T(128)} %bitcast.10, s32[]{:T(128)} %bitcast.11, s32[]{:T(128)} %bitcast.13, s32[]{:T(128)} %bitcast.12, s32[320]{0:T(512)S(1)} %get-tuple-element.11, s32[320]{0:T(512)S(1)} %get-tuple-element.10), kind=kLoop, calls=%fused_computation.81 | loop fusion | flops 4480 | bytes 5148 | tf_op jit(solution)/shard_map/gather | solution.py:60
  38.4 2.2 %gather_fusion.1 = s32[320]{0:T(512)S(1)} fusion(s32[1232]{0:T(1024)S(1)} %reshape.208, s32[1024]{0:T(1024)S(1)} %pad_clamp_fusion), kind=kCustom, calls=%fused_computation.1 | custom fusion | bytes 3840 | tf_op jit(solution)/shard_map/gather | solution.py:65
  41.3 20.3 %all-to-all-done.1 = bf16[8,154,1024]{2,1,0:T(8,128)(2,1)} async-done(((bf16[8,154,1024]{2,1,0:T(8,128)(2,1)}), bf16[8,154,1024]{2,1,0:T(8,128)(2,1)}, u32[]{:S(2)}, u32[]{:S(2)}) %all-to-all-start.1) | async-done | bytes 2523168 | tf_op jit(solution)/shard_map/all_to_all | solution.py:51
  61.5 2.1 %reshape.210 = bf16[1232,1024]{1,0:T(8,128)(2,1)S(1)} reshape(bf16[8,154,1024]{2,1,0:T(8,128)(2,1)} %all-to-all-done.1) | data formatting | bytes 5046272 | tf_op jit(solution)/shard_map/reshape | solution.py:63
  63.6 2.1 %gather_fusion.3 = bf16[320,1024]{1,0:T(8,128)(2,1)S(1)} fusion(bf16[1232,1024]{1,0:T(8,128)(2,1)S(1)} %reshape.210, s32[1024]{0:T(1024)S(1)} %pad_clamp_fusion), kind=kCustom, calls=%fused_computation.3 | custom fusion | bytes 1312000 | tf_op jit(solution)/shard_map/gather | solution.py:63
  65.9 8.2 %convolution_convert_fusion = bf16[128,4096]{1,0:T(8,128)(2,1)} fusion(bf16[1,1024,4096]{2,1,0:T(8,128)(2,1)} %param.12, bf16[320,1024]{1,0:T(8,128)(2,1)S(1)} %gather_fusion.3, f32[1024]{0:T(1024)S(1)} %copy-done, f32[320]{0:T(512)S(1)} %add_rsqrt_fusion.1, s32[320]{0:T(512)S(1)} %add_select_fusion), kind=kOutput, calls=%fused_computation.20 | convolution fusion | flops 3033571328 | bytes 10099200 | tf_op jit(solution)/shard_map/dot_general | solution.py:81
  74.1 5.0 %all-to-all-start.2 = ((bf16[8,16,4096]{2,1,0:T(8,128)(2,1)}), bf16[8,16,4096]{2,1,0:T(8,128)(2,1)S(1)}, u32[]{:S(2)}, u32[]{:S(2)}) async-start(bf16[8,16,4096]{2,1,0:T(8,128)(2,1)} %bitcast.16), calls=%async_computation.2 | async-start | bytes 2097152 | tf_op jit(solution)/shard_map/all_to_all | solution.py:83
  79.1 4.6 %fusion = f32[896]{0:T(1024)S(1)} fusion(bf16[896,4096]{1,0:T(8,128)(2,1)} %param.14), kind=kLoop, calls=%fused_computation.6 | loop fusion | flops 11009152 | bytes 7343616 | tf_op jit(solution)/shard_map/reduce_sum | solution.py:16
  83.7 9.3 %all-to-all-done.2 = bf16[8,16,4096]{2,1,0:T(8,128)(2,1)S(1)} async-done(((bf16[8,16,4096]{2,1,0:T(8,128)(2,1)}), bf16[8,16,4096]{2,1,0:T(8,128)(2,1)S(1)}, u32[]{:S(2)}, u32[]{:S(2)}) %all-to-all-start.2) | async-done | bytes 1048608 | tf_op jit(solution)/shard_map/all_to_all | solution.py:83
  93.4 16.2 %all_gather.3 = bf16[64,4096]{1,0:T(8,128)(2,1)S(1)} all-gather(bf16[16,4096]{1,0:T(8,128)(2,1)S(1)} %multiply_convert_fusion.1), channel_id=1, replica_groups=mesh['dp'=8,'blk'=4] {'blk'}, dimensions={0}, use_global_device_ids=true | all-gather | bytes 655360 | tf_op jit(solution)/shard_map/all_gather | solution.py:88
  109.7 5.7 %exponential_reduce_fusion = (f32[896]{0:T(1024)S(1)}, f32[896]{0:T(1024)S(1)}, f32[896,64]{0,1:T(8,128)S(1)}) fusion(s32[896]{0:T(1024)S(1)} %copy-done.1, bf16[64,4096]{1,0:T(8,128)(2,1)S(1)} %all_gather.3, bf16[896,4096]{1,0:T(8,128)(2,1)} %param.14, f32[896]{0:T(1024)S(1)} %add_rsqrt_fusion), kind=kOutput, calls=%fused_computation.39 | convolution fusion | flops 481057024 | bytes 8108032 | tf_op jit(solution)/shard_map/dot_general | solution.py:21
  115.4 7.3 %fusion.31 = f32[896,4096]{1,0:T(8,128)} fusion(bf16[64,4096]{1,0:T(8,128)(2,1)S(1)} %all_gather.3, f32[896,64]{0,1:T(8,128)S(1)} %get-tuple-element.20), kind=kOutput, calls=%fused_computation.41 | convolution fusion | flops 469819392 | bytes 15433728 | tf_op jit(solution)/shard_map/dot_general | solution.py:93
  122.7 2.7 %convolution_multiply_fusion = f32[64,4096]{1,0:T(8,128)} fusion(bf16[896,4096]{1,0:T(8,128)(2,1)S(1)} %bitcast.31, f32[896]{0:T(1024)S(1)} %add_rsqrt_fusion, f32[896,64]{0,1:T(8,128)S(1)} %get-tuple-element.20, f32[896]{0:T(1024)S(1)} %get-tuple-element.3, s32[896]{0:T(1024)S(1)} %copy-done.1), kind=kOutput, calls=%fused_computation.21 | convolution fusion | flops 481320960 | bytes 8628736 | tf_op jit(solution)/shard_map/dot_general | solution.py:27
  126.1 8.2 %multiply_convert_fusion = bf16[896,4096]{1,0:T(8,128)(2,1)} fusion(f32[896,4096]{1,0:T(8,128)} %fusion.31, bf16[64,4096]{1,0:T(8,128)(2,1)S(1)} %all_gather.3, f32[896]{0:T(1024)S(1)} %get-tuple-element.3, s32[896]{0:T(1024)S(1)} %copy-done.1), kind=kOutput, calls=%fused_computation.8 | convolution fusion | flops 484499456 | bytes 22551552 | tf_op jit(solution)/shard_map/dot_general | solution.py:96
  134.3 19.1 %reduce-scatter.2.cloned.1.call-done = f32[16,4096]{1,0:T(8,128)} async-done(((f32[64,4096]{1,0:T(8,128)}), f32[16,4096]{1,0:T(8,128)}) %reduce-scatter.2.cloned.1.call-update) | async-done | bytes 262160 | tf_op jit(solution)/shard_map/reduce_scatter | solution.py:103
  (39 shorter events, 6.9 us)
Async XLA Ops:
  13.2 13.2 %all-to-all-start = ((s32[8,1,154]{2,1,0:T(1,128)}), s32[8,1,154]{2,1,0:T(1,128)S(1)}, u32[]{:S(2)}, u32[]{:S(2)}) async-start(s32[8,1,154]{2,1,0:T(1,128)} %copy.18), calls=%async_computation | async-start | bytes 16384 | tf_op jit(solution)/shard_map/all_to_all | solution.py:52
  26.4 35.2 %all-to-all-start.1 = ((bf16[8,154,1024]{2,1,0:T(8,128)(2,1)}), bf16[8,154,1024]{2,1,0:T(8,128)(2,1)}, u32[]{:S(2)}, u32[]{:S(2)}) async-start(bf16[8,154,1024]{2,1,0:T(8,128)(2,1)} %slice_select_fusion), calls=%async_computation.1 | async-start | bytes 5242880 | tf_op jit(solution)/shard_map/all_to_all | solution.py:51
  41.3 24.7 %copy-start = (f32[1024]{0:T(1024)S(1)}, f32[1024]{0:T(1024)}, u32[]{:S(2)}) copy-start(f32[1024]{0:T(1024)} %param.13) | copy-start | bytes 12292
  74.1 18.9 %all-to-all-start.2 = ((bf16[8,16,4096]{2,1,0:T(8,128)(2,1)}), bf16[8,16,4096]{2,1,0:T(8,128)(2,1)S(1)}, u32[]{:S(2)}, u32[]{:S(2)}) async-start(bf16[8,16,4096]{2,1,0:T(8,128)(2,1)} %bitcast.16), calls=%async_computation.2 | async-start | bytes 2097152 | tf_op jit(solution)/shard_map/all_to_all | solution.py:83
  79.1 30.5 %copy-start.1 = (s32[896]{0:T(1024)S(1)}, s32[896]{0:T(1024)}, u32[]{:S(2)}) copy-start(s32[896]{0:T(1024)} %param.15) | copy-start | bytes 10756
  79.1 74.3 %reduce-scatter.2.cloned.1.call-start = ((), (), s32[]{:S(2)}) async-start(), calls=%async_computation.4 | async-start | bytes 1310720 | tf_op jit(solution)/shard_map/reduce_scatter | solution.py:103
  109.7 13.0 %slice-start = ((s8[7340032]{0:T(1024)(128)(4,1)}), s8[4194304]{0:T(1024)(128)(4,1)S(1)}, s32[]{:S(2)}) async-start(s8[7340032]{0:T(1024)(128)(4,1)} %bitcast.30), calls=%async_computation.5 | async-start | bytes 8388608
  115.4 7.3 %slice-start.1 = ((s8[7340032]{0:T(1024)(128)(4,1)}), s8[3145728]{0:T(1024)(128)(4,1)S(1)}, s32[]{:S(2)}) async-start(s8[7340032]{0:T(1024)(128)(4,1)} %bitcast.30), calls=%async_computation.6 | async-start | bytes 6291456
Sparse Core Ops, SparseCore 0:
  125.6 27.7 reduce-scatter.1

commit v3 on v2

--- a/solution.py
+++ b/solution.py
@@ -37,19 +37,17 @@
     groups = lax.axis_size("dp")
     capacity = (rows_dev - 3 * SESS_DEV) // groups
     received = rows_dev // 4
-    cycle = rows_dev // groups
     count = span_counts[0]
 
     lane_of = (jnp.arange(groups, dtype=jnp.int32) - destinations[0]) % groups
-    by_lane = spans.reshape(cycle, groups, hidden_width)
-    send_rows = jnp.swapaxes(jnp.take(by_lane, lane_of, axis=1), 0, 1)[:, :capacity]
     row_of = lane_of[:, None] + groups * jnp.arange(capacity, dtype=jnp.int32)[None, :]
-    ids_by_lane = session_ids.reshape(cycle, groups)
-    send_ids = jnp.where(
-        row_of < count, jnp.swapaxes(jnp.take(ids_by_lane, lane_of, axis=1), 0, 1)[:, :capacity], -1
-    )
-    got_rows = lax.all_to_all(send_rows, "dp", split_axis=0, concat_axis=0, tiled=True)
-    got_ids = lax.all_to_all(send_ids, "dp", split_axis=0, concat_axis=0, tiled=True)
+    send_rows = spans[row_of.reshape(groups * capacity)].reshape(groups, capacity, hidden_width)
+    tag = jnp.where(row_of < count, session_ids[row_of] + 1, 0).astype(jnp.bfloat16)
+    tag_row = jnp.zeros((groups, 1, hidden_width), jnp.bfloat16).at[:, 0, :capacity].set(tag)
+    send = jnp.concatenate([send_rows, tag_row], axis=1)
+    got = lax.all_to_all(send, "dp", split_axis=0, concat_axis=0, tiled=True)
+    block = capacity + 1
+    got_ids = got[:, capacity, :capacity].astype(jnp.int32) - 1
 
     got_counts = jnp.sum((got_ids >= 0).astype(jnp.int32), axis=1)
     starts = jnp.cumsum(got_counts) - got_counts
@@ -57,12 +55,12 @@
     source_of = (
         jnp.sum((starts[None, :] <= packed_index[:, None]).astype(jnp.int32), axis=1) - 1
     )
-    slot_of = source_of * capacity + packed_index - starts[source_of]
+    rank_of = packed_index - starts[source_of]
     packed_live = packed_index < jnp.sum(got_counts)
-    slot_of = jnp.where(packed_live, slot_of, 0)
-    packed = got_rows.reshape(groups * capacity, hidden_width)[slot_of]
+    rank_of = jnp.where(packed_live, rank_of, 0)
+    packed = got.reshape(groups * block, hidden_width)[source_of * block + rank_of]
     packed_key = jnp.where(
-        packed_live, source_of * SESS_DEV + got_ids.reshape(groups * capacity)[slot_of], -1
+        packed_live, source_of * SESS_DEV + got_ids.reshape(groups * capacity)[source_of * capacity + rank_of], -1
     )
 
     widened = packed.astype(jnp.float32)
@@ -85,7 +83,17 @@
 
     doc_unit = unit_rows(pooled)
     query_unit = unit_rows(queries)
-    doc_piece = lax.all_gather(doc_unit, "blk", axis=0, tiled=True)
+    cycle_size = lax.axis_size("blk")
+    position = lax.axis_index("blk")
+    arrived = [doc_unit] + [
+        lax.ppermute(doc_unit, "blk", [(i, (i + shift) % cycle_size) for i in range(cycle_size)])
+        for shift in range(1, cycle_size)
+    ]
+    stacked = jnp.stack(arrived)
+    source_order = (position - jnp.arange(cycle_size, dtype=jnp.int32)) % cycle_size
+    doc_piece = jnp.zeros_like(stacked).at[source_order].set(stacked).reshape(
+        cycle_size * doc_unit.shape[0], doc_unit.shape[1]
+    )
     piece_rows = doc_piece.shape[0]
     logits = logit_scale * contract_rows(query_unit, doc_piece)
     weights = jnp.exp(logits)
@@ -100,7 +108,10 @@
     grad_queries = (logit_scale * (numerator / totals[:, None] - chosen_doc)).astype(jnp.bfloat16)
     coefficient = (weights / totals[:, None] - matches.astype(jnp.float32)).astype(jnp.bfloat16)
     grad_part = logit_scale * contract_first(coefficient, query_unit)
-    grad_docs = lax.psum_scatter(grad_part, "blk", scatter_dimension=0, tiled=True)
+    grad_terms = lax.all_to_all(
+        grad_part.reshape(cycle_size, doc_unit.shape[0], emb_width), "blk", split_axis=0, concat_axis=0, tiled=True
+    )
+    grad_docs = jnp.sum(grad_terms, axis=0)
     return (loss_rows, grad_queries, grad_docs)
 
 

time: 162 us -> 173 us (1.068)
  blocking collectives: 16.2 us -> 34.8 us
  local copies, waits for them, and re-layouts: 15.8 us -> 31.9 us
  between operations: 14.8 us -> 1.54 us
  waiting for transfers between devices: 48.7 us -> 37.4 us
    all_to_all x0 -> x1, blocking collectives: none -> 34.8 us  [on_device(): got = lax.all_to_all(send, 'dp', split_axis=0, concat_axis=0, tiled=True)]
    reduce_scatter x1 -> x0, waiting for transfers between devices: 19.1 us -> none  [on_device(): lax.psum_scatter(grad_part, 'blk', scatter_dimension=0, tiled=True)]
    all_gather x1 -> x0, blocking collectives: 16.2 us -> none  [on_device(): doc_piece = lax.all_gather(doc_unit, 'blk', axis=0, tiled=True)]
    gather x5, local copies, waits for them, and re-layouts: 7.79 us -> 19.9 us  [the longest x1 7.08 us: on_device(): session_ids[row_of] + 1]
    ppermute x0 -> x3, waiting for transfers between devices: none -> 10.5 us  [on_device(): lax.ppermute(doc_unit, 'blk', [(i, (i + shift) % cycle_size) for i in ran...]
    ppermute x0 -> x3, starting transfers between devices: none -> 4.67 us  [on_device(): lax.ppermute(doc_unit, 'blk', [(i, (i + shift) % cycle_size) for i in ran...]
    all_to_all x2 -> x1, starting transfers between devices: 8.6 us -> 4.25 us  [on_device(): lax.all_to_all(grad_part.reshape(cycle_size, doc_unit.shape[0], emb_width...]
    select_n x3 -> x4, other arithmetic: 4.91 us -> 0.78 us  [the longest x1 0.67 us: on_device(): got_ids.reshape(groups * capacity)[source_of * capacity + rank_of]]
  transfers between devices with their start and end apart: 4 -> 5, of which waited for: 3 -> 4; matrix products, arithmetic and copies ran while one was open for 20% -> 7% of each run, Pallas kernels for 0% -> 0%
where the time goes in v3:
time: 173 us
  waiting for transfers between devices  37.4 us (22%)
  blocking collectives  34.8 us (20%)
  matrix products  32.1 us (19%)
  local copies, waits for them, and re-layouts  31.9 us (18%)
  other arithmetic  20.4 us (12%)
  starting transfers between devices  14.5 us (8%)
    all_to_all x1, blocking collectives, on_device(): got = lax.all_to_all(send, 'dp', split_axis=0, concat_axis=0, tiled=True)  34.8 us
    all_to_all x1, waiting for transfers between devices, on_device(): lax.all_to_all(grad_part.reshape(cycle_size, doc_unit.shape[0], emb_width...  17.5 us
    ppermute x3, waiting for transfers between devices, on_device(): lax.ppermute(doc_unit, 'blk', [(i, (i + shift) % cycle_size) for i in ran...  10.5 us
    all_to_all x1, waiting for transfers between devices, on_device(): lax.all_to_all(partial, 'dp', split_axis=0, concat_axis=0, tiled=True)  9.41 us
    dot_general x1, matrix products, on_device(): jnp.dot(matches.astype(jnp.bfloat16), doc_piece, preferred_element_type=j...  8.19 us
    dot_general x1, matrix products, on_device(): partial = jnp.dot(selector, embedded, preferred_element_type=jnp.float32)  8.17 us
    dot_general x1, matrix products, on_device(): jnp.dot(weights.astype(jnp.bfloat16), doc_piece, preferred_element_type=j...  7.32 us
    gather x1, local copies, waits for them, and re-layouts, on_device(): session_ids[row_of] + 1  7.08 us
  transfers between devices with their start and end apart: 5, of which 4 were waited for; matrix products, arithmetic and copies ran while one was open for 7% of the time, Pallas kernels for 0%

profile of v3, /device:TPU:2, one launch (start us, length us, event | category | flops | bytes accessed | tf_op | source)
XLA Modules:
  0.0 172.7 jit_solution(16208635291084812510)
XLA Ops:
  2.9 7.1 %gather_fusion.1 = s32[1232]{0:T(1024)S(1)} fusion(s32[1280]{0:T(1024)S(1)} %copy-done.1, s32[2048]{0:T(1024)S(1)} %pad_clamp_fusion), kind=kCustom, calls=%fused_computation.1 | custom fusion | bytes 14784 | tf_op jit(solution)/shard_map/gather | solution.py:45
  10.9 5.0 %gather_fusion = bf16[1232,1024]{1,0:T(8,128)(2,1)} fusion(bf16[1280,1024]{1,0:T(8,128)(2,1)S(1)} %copy-done, s32[2048]{0:T(1024)S(1)} %pad_clamp_fusion.1), kind=kCustom, calls=%fused_computation | custom fusion | bytes 5051200 | tf_op jit(solution)/shard_map/gather | solution.py:44
  16.0 3.1 %reshape.428 = bf16[8,154,1024]{2,1,0:T(8,128)(2,1)} reshape(bf16[1232,1024]{1,0:T(8,128)(2,1)} %gather_fusion) | data formatting | bytes 5046272 | tf_op jit(solution)/shard_map/reshape | solution.py:44
  19.2 2.1 %fusion.18 = bf16[8,155,1024]{2,1,0:T(8,128)(2,1)S(1)} fusion(bf16[8,1,154]{2,1,0:T(2,128)(2,1)S(1)} %fusion.39, bf16[8,154,1024]{2,1,0:T(8,128)(2,1)} %reshape.428), kind=kLoop, calls=%fused_computation.26 | loop fusion | flops 7618560 | bytes 5065120 | tf_op jit(solution)/shard_map/concatenate | solution.py:47
  21.2 34.8 %all_to_all.15 = bf16[8,155,1024]{2,1,0:T(8,128)(2,1)S(1)} all-to-all(bf16[8,155,1024]{2,1,0:T(8,128)(2,1)S(1)} %fusion.18), channel_id=1, replica_groups=mesh['dp'=8,'blk'=4] {'dp'}, dimensions={0} | all-to-all | bytes 5079040 | tf_op jit(solution)/shard_map/all_to_all | solution.py:48
  59.3 4.3 %fusion.44 = (s32[320]{0:T(512)S(1)}, s32[320,1]{0,1:T(1,128)S(1)}) fusion(s32[]{:T(128)} %bitcast.6, s32[]{:T(128)} %bitcast.7, s32[]{:T(128)} %bitcast.8, s32[]{:T(128)} %bitcast.9, s32[]{:T(128)} %bitcast.10, s32[]{:T(128)} %bitcast.12, s32[]{:T(128)} %bitcast.11, s32[320]{0:T(512)S(1)} %get-tuple-element.24, s32[320]{0:T(512)S(1)} %get-tuple-element.25), kind=kLoop, calls=%fused_computation.93 | loop fusion | flops 4480 | bytes 5148 | tf_op jit(solution)/shard_map/gather | solution.py:58
  65.0 4.0 %reshape.431 = bf16[1240,1024]{1,0:T(8,128)(2,1)} reshape(bf16[8,155,1024]{2,1,0:T(8,128)(2,1)} %copy-done.2) | data formatting | bytes 5079040 | tf_op jit(solution)/shard_map/reshape | solution.py:61
  68.9 4.8 %gather_fusion.3 = bf16[320,1024]{1,0:T(8,128)(2,1)S(1)} fusion(bf16[1240,1024]{1,0:T(8,128)(2,1)} %reshape.431, s32[1024]{0:T(1024)S(1)} %get-tuple-element.35), kind=kCustom, calls=%fused_computation.3 | custom fusion | bytes 1312000 | tf_op jit(solution)/shard_map/gather | solution.py:61
  74.1 2.2 %gather_fusion.2 = s32[320]{0:T(512)S(1)} fusion(s32[1232]{0:T(1024)S(1)} %sub.71, s32[1024]{0:T(1024)S(1)} %get-tuple-element.36), kind=kCustom, calls=%fused_computation.2 | custom fusion | bytes 3840 | tf_op jit(solution)/shard_map/gather | solution.py:63
  77.0 8.2 %convolution_convert_fusion = bf16[128,4096]{1,0:T(8,128)(2,1)} fusion(bf16[1,1024,4096]{2,1,0:T(8,128)(2,1)} %param.14, bf16[320,1024]{1,0:T(8,128)(2,1)S(1)} %gather_fusion.3, f32[1024]{0:T(1024)S(1)} %copy-done.3, f32[320]{0:T(512)S(1)} %add_rsqrt_fusion.1, s32[320]{0:T(512)S(1)} %add_select_fusion), kind=kOutput, calls=%fused_computation.23 | convolution fusion | flops 3033571328 | bytes 10099200 | tf_op jit(solution)/shard_map/dot_general | solution.py:79
  85.2 5.6 %all-to-all-start.1 = ((bf16[8,16,4096]{2,1,0:T(8,128)(2,1)}), bf16[8,16,4096]{2,1,0:T(8,128)(2,1)}, u32[]{:S(2)}, u32[]{:S(2)}) async-start(bf16[8,16,4096]{2,1,0:T(8,128)(2,1)} %bitcast.43), calls=%async_computation.1 | async-start | bytes 2097152 | tf_op jit(solution)/shard_map/all_to_all | solution.py:81
  90.8 4.6 %fusion = f32[896]{0:T(1024)S(1)} fusion(bf16[896,4096]{1,0:T(8,128)(2,1)} %param.16), kind=kLoop, calls=%fused_computation.7 | loop fusion | flops 11009152 | bytes 7343616 | tf_op jit(solution)/shard_map/reduce_sum | solution.py:16
  95.4 9.4 %all-to-all-done.1 = bf16[8,16,4096]{2,1,0:T(8,128)(2,1)} async-done(((bf16[8,16,4096]{2,1,0:T(8,128)(2,1)}), bf16[8,16,4096]{2,1,0:T(8,128)(2,1)}, u32[]{:S(2)}, u32[]{:S(2)}) %all-to-all-start.1) | async-done | bytes 1048608 | tf_op jit(solution)/shard_map/all_to_all | solution.py:81
  106.4 3.7 %collective-permute-start.2 = (bf16[16,4096]{1,0:T(8,128)(2,1)S(1)}, bf16[16,4096]{1,0:T(8,128)(2,1)S(1)}, u32[]{:S(2)}, u32[]{:S(2)}) collective-permute-start(bf16[16,4096]{1,0:T(8,128)(2,1)S(1)} %multiply_convert_fusion.1), channel_id=1, source_target_pairs={{0,3},{1,0},{2,1},{3,2},{4,7},{5,4},{6,5},{7,6},{8,11},{9,8},{10,9... | collective-permute-start | bytes 393224 | tf_op jit(solution)/shard_map/ppermute | solution.py:89
  111.2 2.8 %collective-permute-done.2 = bf16[16,4096]{1,0:T(8,128)(2,1)S(1)} collective-permute-done((bf16[16,4096]{1,0:T(8,128)(2,1)S(1)}, bf16[16,4096]{1,0:T(8,128)(2,1)S(1)}, u32[]{:S(2)}, u32[]{:S(2)}) %collective-permute-start.2) | collective-permute-done | bytes 131104 | tf_op jit(solution)/shard_map/ppermute | solution.py:89
  114.0 7.6 %collective-permute-done.1 = bf16[16,4096]{1,0:T(8,128)(2,1)S(1)} collective-permute-done((bf16[16,4096]{1,0:T(8,128)(2,1)S(1)}, bf16[16,4096]{1,0:T(8,128)(2,1)S(1)}, u32[]{:S(2)}, u32[]{:S(2)}) %collective-permute-start.1) | collective-permute-done | bytes 131104 | tf_op jit(solution)/shard_map/ppermute | solution.py:89
  122.6 1.7 scatter_fusion
  124.3 5.7 %exponential_reduce_fusion = (f32[896]{0:T(1024)S(1)}, f32[896]{0:T(1024)S(1)}, f32[896,64]{0,1:T(8,128)S(1)}) fusion(s32[896]{0:T(1024)S(1)} %copy-done.4, bf16[64,4096]{1,0:T(8,128)(2,1)S(1)} %bitcast.40, bf16[896,4096]{1,0:T(8,128)(2,1)} %param.16, f32[896]{0:T(1024)S(1)} %add_rsqrt_fusion), kind=kOutput, calls=%fused_computation.45 | convolution fusion | flops 481057024 | bytes 8108032 | tf_op jit(solution)/shard_map/dot_general | solution.py:21
  130.0 7.3 %fusion.34 = f32[896,4096]{1,0:T(8,128)} fusion(bf16[64,4096]{1,0:T(8,128)(2,1)S(1)} %bitcast.41, f32[896,64]{0,1:T(8,128)S(1)} %get-tuple-element.34), kind=kOutput, calls=%fused_computation.47 | convolution fusion | flops 469819392 | bytes 15433728 | tf_op jit(solution)/shard_map/dot_general | solution.py:101
  137.3 2.8 %convolution_multiply_fusion = f32[64,4096]{1,0:T(8,128)} fusion(bf16[896,4096]{1,0:T(8,128)(2,1)S(1)} %bitcast.39, f32[896]{0:T(1024)S(1)} %add_rsqrt_fusion, f32[896,64]{0,1:T(8,128)S(1)} %get-tuple-element.34, f32[896]{0:T(1024)S(1)} %get-tuple-element.18, s32[896]{0:T(1024)S(1)} %copy-done.4), kind=kOutput, calls=%fused_computation.24 | convolution fusion | flops 481320960 | bytes 8628736 | tf_op jit(solution)/shard_map/dot_general | solution.py:27
  140.7 4.2 %all-to-all-start.2 = ((f32[4,16,4096]{2,1,0:T(8,128)}), f32[4,16,4096]{2,1,0:T(8,128)}, u32[]{:S(2)}, u32[]{:S(2)}) async-start(f32[4,16,4096]{2,1,0:T(8,128)} %bitcast.44), calls=%async_computation.2 | async-start | bytes 2097152 | tf_op jit(solution)/shard_map/all_to_all | solution.py:111
  145.0 8.2 %multiply_convert_fusion = bf16[896,4096]{1,0:T(8,128)(2,1)} fusion(f32[896,4096]{1,0:T(8,128)} %fusion.34, bf16[64,4096]{1,0:T(8,128)(2,1)S(1)} %bitcast.42, f32[896]{0:T(1024)S(1)} %get-tuple-element.18, s32[896]{0:T(1024)S(1)} %copy-done.4), kind=kOutput, calls=%fused_computation.9 | convolution fusion | flops 484499456 | bytes 22551552 | tf_op jit(solution)/shard_map/dot_general | solution.py:104
  153.2 17.5 %all-to-all-done.2 = f32[4,16,4096]{2,1,0:T(8,128)} async-done(((f32[4,16,4096]{2,1,0:T(8,128)}), f32[4,16,4096]{2,1,0:T(8,128)}, u32[]{:S(2)}, u32[]{:S(2)}) %all-to-all-start.2) | async-done | bytes 1048608 | tf_op jit(solution)/shard_map/all_to_all | solution.py:111
  170.7 2.0 %reduce_sum.102 = f32[16,4096]{1,0:T(8,128)} reduce(f32[4,16,4096]{2,1,0:T(8,128)} %all-to-all-done.2, f32[]{:T(128)} %constant.94.clone.1), dimensions={0}, to_apply=%region_11.12 | reduce | flops 196608 | bytes 1310724 | tf_op jit(solution)/shard_map/reduce_sum | solution.py:114
  (55 shorter events, 12.4 us)
Async XLA Ops:
  0.6 10.3 %copy-start = (bf16[1280,1024]{1,0:T(8,128)(2,1)S(1)}, bf16[1280,1024]{1,0:T(8,128)(2,1)}, u32[]{:S(2)}) copy-start(bf16[1280,1024]{1,0:T(8,128)(2,1)} %param.10) | copy-start | bytes 7864324
  0.6 2.3 %copy-start.1 = (s32[1280]{0:T(1024)S(1)}, s32[1280]{0:T(1024)}, u32[]{:S(2)}) copy-start(s32[1280]{0:T(1024)} %param.12) | copy-start | bytes 15364
  56.1 1.5 copy-start.2
  68.9 8.1 %copy-start.3 = (f32[1024]{0:T(1024)S(1)}, f32[1024]{0:T(1024)}, u32[]{:S(2)}) copy-start(f32[1024]{0:T(1024)} %param.15) | copy-start | bytes 12292
  85.2 19.6 %all-to-all-start.1 = ((bf16[8,16,4096]{2,1,0:T(8,128)(2,1)}), bf16[8,16,4096]{2,1,0:T(8,128)(2,1)}, u32[]{:S(2)}, u32[]{:S(2)}) async-start(bf16[8,16,4096]{2,1,0:T(8,128)(2,1)} %bitcast.43), calls=%async_computation.1 | async-start | bytes 2097152 | tf_op jit(solution)/shard_map/all_to_all | solution.py:81
  90.8 33.5 %copy-start.4 = (s32[896]{0:T(1024)S(1)}, s32[896]{0:T(1024)}, u32[]{:S(2)}) copy-start(s32[896]{0:T(1024)} %param.17) | copy-start | bytes 10756
  106.4 7.6 %collective-permute-start.2 = (bf16[16,4096]{1,0:T(8,128)(2,1)S(1)}, bf16[16,4096]{1,0:T(8,128)(2,1)S(1)}, u32[]{:S(2)}, u32[]{:S(2)}) collective-permute-start(bf16[16,4096]{1,0:T(8,128)(2,1)S(1)} %multiply_convert_fusion.1), channel_id=1, source_target_pairs={{0,3},{1,0},{2,1},{3,2},{4,7},{5,4},{6,5},{7,6},{8,11},{9,8},{10,9... | collective-permute-start | bytes 393224 | tf_op jit(solution)/shard_map/ppermute | solution.py:89
  110.1 11.6 %collective-permute-start.1 = (bf16[16,4096]{1,0:T(8,128)(2,1)S(1)}, bf16[16,4096]{1,0:T(8,128)(2,1)S(1)}, u32[]{:S(2)}, u32[]{:S(2)}) collective-permute-start(bf16[16,4096]{1,0:T(8,128)(2,1)S(1)} %multiply_convert_fusion.1), channel_id=1, source_target_pairs={{0,2},{1,3},{2,0},{3,1},{4,6},{5,7},{6,4},{7,5},{8,10},{9,11},{10,... | collective-permute-start | bytes 393224 | tf_op jit(solution)/shard_map/ppermute | solution.py:89
  110.1 11.6 %collective-permute-start = (bf16[16,4096]{1,0:T(8,128)(2,1)S(1)}, bf16[16,4096]{1,0:T(8,128)(2,1)S(1)}, u32[]{:S(2)}, u32[]{:S(2)}) collective-permute-start(bf16[16,4096]{1,0:T(8,128)(2,1)S(1)} %multiply_convert_fusion.1), channel_id=1, source_target_pairs={{0,1},{1,2},{2,3},{3,0},{4,5},{5,6},{6,7},{7,4},{8,9},{9,10},{10,1... | collective-permute-start | bytes 393224 | tf_op jit(solution)/shard_map/ppermute | solution.py:89
  124.3 13.1 %slice-start = ((s8[7340032]{0:T(1024)(128)(4,1)}), s8[4194304]{0:T(1024)(128)(4,1)S(1)}, s32[]{:S(2)}) async-start(s8[7340032]{0:T(1024)(128)(4,1)} %bitcast.38), calls=%async_computation.3 | async-start | bytes 8388608
  130.0 7.3 %slice-start.1 = ((s8[7340032]{0:T(1024)(128)(4,1)}), s8[3145728]{0:T(1024)(128)(4,1)S(1)}, s32[]{:S(2)}) async-start(s8[7340032]{0:T(1024)(128)(4,1)} %bitcast.38), calls=%async_computation.4 | async-start | bytes 6291456
  140.7 30.0 %all-to-all-start.2 = ((f32[4,16,4096]{2,1,0:T(8,128)}), f32[4,16,4096]{2,1,0:T(8,128)}, u32[]{:S(2)}, u32[]{:S(2)}) async-start(f32[4,16,4096]{2,1,0:T(8,128)} %bitcast.44), calls=%async_computation.2 | async-start | bytes 2097152 | tf_op jit(solution)/shard_map/all_to_all | solution.py:111

commit v4 on v2

--- a/solution.py
+++ b/solution.py
@@ -1,6 +1,8 @@
 import jax
 import jax.numpy as jnp
 from jax import lax
+from jax.experimental import pallas as pl
+from jax.experimental.pallas import tpu as pltpu
 from jax.sharding import PartitionSpec as P
 
 SESS_DEV = 16
@@ -27,6 +29,61 @@
     return lax.dot_general(
         left_side, right_side, (((0,), (0,)), ((), ())), preferred_element_type=jnp.float32
     )
+
+
+def contrast_kernel(q_ref, d_ref, pos_ref, loss_ref, gq_ref, gd_ref):
+    @pl.when(pl.program_id(0) == 0)
+    def _():
+        gd_ref[...] = jnp.zeros_like(gd_ref)
+
+    widened = q_ref[...].astype(jnp.float32)
+    query_unit = (
+        widened * lax.rsqrt(jnp.sum(widened * widened, axis=-1, keepdims=True) + epsilon)
+    ).astype(jnp.bfloat16)
+    docs = d_ref[...]
+    logits = logit_scale * contract_rows(query_unit, docs)
+    weights = jnp.exp(logits)
+    totals = jnp.sum(weights, axis=1, keepdims=True)
+    numerator = jnp.dot(weights.astype(jnp.bfloat16), docs, preferred_element_type=jnp.float32)
+    matches = pos_ref[...] == lax.broadcasted_iota(jnp.int32, logits.shape, 1)
+    hits = matches.astype(jnp.float32)
+    chosen_logit = jnp.sum(jnp.where(matches, logits, 0.0), axis=1, keepdims=True)
+    chosen_doc = jnp.dot(hits.astype(jnp.bfloat16), docs, preferred_element_type=jnp.float32)
+    loss_ref[...] = jnp.log(totals) - chosen_logit
+    gq_ref[...] = (logit_scale * (numerator / totals - chosen_doc)).astype(jnp.bfloat16)
+    coefficient_t = (weights / totals - hits).T.astype(jnp.bfloat16)
+    gd_ref[...] += logit_scale * jnp.dot(
+        coefficient_t, query_unit, preferred_element_type=jnp.float32
+    )
+
+
+def contrast(queries, doc_piece, positives, tile=128):
+    rows, width = queries.shape
+    docs = doc_piece.shape[0]
+    steps = rows // tile
+    return pl.pallas_call(
+        contrast_kernel,
+        grid=(steps,),
+        in_specs=[
+            pl.BlockSpec((tile, width), lambda i: (i, 0)),
+            pl.BlockSpec((docs, width), lambda i: (0, 0)),
+            pl.BlockSpec((tile, 1), lambda i: (i, 0)),
+        ],
+        out_specs=[
+            pl.BlockSpec((tile, 1), lambda i: (i, 0)),
+            pl.BlockSpec((tile, width), lambda i: (i, 0)),
+            pl.BlockSpec((docs, width), lambda i: (0, 0)),
+        ],
+        out_shape=[
+            jax.ShapeDtypeStruct((rows, 1), jnp.float32),
+            jax.ShapeDtypeStruct((rows, width), jnp.bfloat16),
+            jax.ShapeDtypeStruct((docs, width), jnp.float32),
+        ],
+        compiler_params=pltpu.CompilerParams(dimension_semantics=("arbitrary",)),
+        cost_estimate=pl.CostEstimate(
+            flops=8 * rows * docs * width, transcendentals=rows * docs, bytes_accessed=4 * rows * width
+        ),
+    )(queries, doc_piece, positives.reshape(rows, 1))
 
 
 def on_device(
@@ -84,22 +141,19 @@
     pooled = jnp.sum(returned.astype(jnp.float32), axis=0)
 
     doc_unit = unit_rows(pooled)
-    query_unit = unit_rows(queries)
-    doc_piece = lax.all_gather(doc_unit, "blk", axis=0, tiled=True)
-    piece_rows = doc_piece.shape[0]
-    logits = logit_scale * contract_rows(query_unit, doc_piece)
-    weights = jnp.exp(logits)
-    totals = jnp.sum(weights, axis=1)
-    numerator = jnp.dot(weights.astype(jnp.bfloat16), doc_piece, preferred_element_type=jnp.float32)
-    matches = positives[:, None] == jnp.arange(piece_rows, dtype=jnp.int32)[None, :]
-    chosen_logit = jnp.sum(jnp.where(matches, logits, 0.0), axis=1)
-    chosen_doc = jnp.dot(
-        matches.astype(jnp.bfloat16), doc_piece, preferred_element_type=jnp.float32
+    cycle_size = lax.axis_size("blk")
+    position = lax.axis_index("blk")
+    arrived = jnp.stack(
+        [doc_unit]
+        + [
+            lax.ppermute(doc_unit, "blk", [(i, (i + shift) % cycle_size) for i in range(cycle_size)])
+            for shift in range(1, cycle_size)
+        ]
     )
-    loss_rows = jnp.log(totals) - chosen_logit
-    grad_queries = (logit_scale * (numerator / totals[:, None] - chosen_doc)).astype(jnp.bfloat16)
-    coefficient = (weights / totals[:, None] - matches.astype(jnp.float32)).astype(jnp.bfloat16)
-    grad_part = logit_scale * contract_first(coefficient, query_unit)
+    arrival_of = (position - jnp.arange(cycle_size, dtype=jnp.int32)) % cycle_size
+    doc_piece = arrived[arrival_of].reshape(cycle_size * doc_unit.shape[0], emb_width)
+    loss_col, grad_queries, grad_part = contrast(queries, doc_piece, positives)
+    loss_rows = loss_col.reshape(loss_col.shape[0])
     grad_docs = lax.psum_scatter(grad_part, "blk", scatter_dimension=0, tiled=True)
     return (loss_rows, grad_queries, grad_docs)
 

time: 162 us -> 163 us (level)
  matrix products: 32.1 us -> 8.18 us
  waiting for transfers between devices: 48.7 us -> 68.4 us
  Pallas kernels: 0 us -> 17.1 us
  blocking collectives: 16.2 us -> 0 us
  starting transfers between devices: 13.6 us -> 18.3 us
  other arithmetic: 18.9 us -> 15.7 us
  local copies, waits for them, and re-layouts: 15.8 us -> 18.1 us
    dot_general x4 -> x0, matrix products: 23.9 us -> none  [the longest x1 8.18 us: on_device(): jnp.dot(matches.astype(jnp.bfloat16), doc_piece, preferred_element_type=j...]
    pallas_call x0 -> x1, Pallas kernels: none -> 17.1 us  [contrast(): pl.pallas_call(contrast_kernel, grid=(steps,), in_specs=[pl.BlockSpec((ti...]
    all_gather x1 -> x0, blocking collectives: 16.2 us -> none  [on_device(): doc_piece = lax.all_gather(doc_unit, 'blk', axis=0, tiled=True)]
    ppermute x0 -> x3, waiting for transfers between devices: none -> 10.5 us  [on_device(): lax.ppermute(doc_unit, 'blk', [(i, (i + shift) % cycle_size) for i in ran...]
    reduce_scatter x1, waiting for transfers between devices: 19.1 us -> 24.7 us  [on_device(): lax.psum_scatter(grad_part, 'blk', scatter_dimension=0, tiled=True)]
    ppermute x0 -> x3, starting transfers between devices: none -> 4.66 us  [on_device(): lax.ppermute(doc_unit, 'blk', [(i, (i + shift) % cycle_size) for i in ran...]
    reduce_sum x2 -> x1, other arithmetic: 4.73 us -> 0.15 us  [unit_rows(): jnp.sum(widened * widened, axis=-1, keepdims=True) + epsilon]
    all_to_all x1, waiting for transfers between devices: 9.32 us -> 12.9 us  [on_device(): lax.all_to_all(partial, 'dp', split_axis=0, concat_axis=0, tiled=True)]
  transfers between devices with their start and end apart: 4 -> 7, of which waited for: 3 -> 5; matrix products, arithmetic and copies ran while one was open for 20% -> 14% of each run, Pallas kernels for 0% -> 0%
where the time goes in v4:
time: 163 us; the launch traced here: 161 us
  waiting for transfers between devices  68.4 us (42%)
  starting transfers between devices  18.3 us (11%)
  local copies, waits for them, and re-layouts  18.1 us (11%)
  Pallas kernels  17.1 us (10%)
  other arithmetic  15.7 us (10%)
  between operations  14.8 us (9%)
  matrix products  8.18 us (5%)
    reduce_scatter x1, waiting for transfers between devices, on_device(): lax.psum_scatter(grad_part, 'blk', scatter_dimension=0, tiled=True)  24.7 us
    all_to_all x1, waiting for transfers between devices, on_device(): lax.all_to_all(send_rows, 'dp', split_axis=0, concat_axis=0, tiled=True)  20.3 us
    pallas_call x1, Pallas kernels, contrast(): pl.pallas_call(contrast_kernel, grid=(steps,), in_specs=[pl.BlockSpec((ti...  17.1 us
    all_to_all x1, waiting for transfers between devices, on_device(): lax.all_to_all(partial, 'dp', split_axis=0, concat_axis=0, tiled=True)  12.9 us
    ppermute x3, waiting for transfers between devices, on_device(): lax.ppermute(doc_unit, 'blk', [(i, (i + shift) % cycle_size) for i in ran...  10.5 us
    dot_general x1, matrix products, on_device(): partial = jnp.dot(selector, embedded, preferred_element_type=jnp.float32)  8.18 us
    gather x3, other arithmetic, on_device(): slot_of = source_of * capacity + packed_index - starts[source_of]  5.09 us
    all_to_all x1, starting transfers between devices, on_device(): lax.all_to_all(partial, 'dp', split_axis=0, concat_axis=0, tiled=True)  4.99 us
  transfers between devices with their start and end apart: 7, of which 5 were waited for; matrix products, arithmetic and copies ran while one was open for 14% of the time, Pallas kernels for 0%

profile of v4, /device:TPU:2, one launch (start us, length us, event | category | flops | bytes accessed | tf_op | source)
XLA Modules:
  0.0 160.6 jit_solution(13131805434462914459)
XLA Ops:
  7.2 1.2 slice.9
  11.0 0.8 reshape.284
  13.1 4.3 %all-to-all-start = ((s32[8,1,154]{2,1,0:T(1,128)}), s32[8,1,154]{2,1,0:T(1,128)S(1)}, u32[]{:S(2)}, u32[]{:S(2)}) async-start(s32[8,1,154]{2,1,0:T(1,128)} %copy.21), calls=%async_computation | async-start | bytes 16384 | tf_op jit(solution)/shard_map/all_to_all | solution.py:109
  17.4 3.2 %copy.22 = bf16[160,8,1024]{2,0,1:T(8,128)(2,1)S(1)} copy(bf16[160,8,1024]{2,1,0:T(8,128)(2,1)} %bitcast.37) | data formatting | bytes 5242880 | tf_op jit(solution)/shard_map/reshape | solution.py:101
  20.6 2.2 %gather_fusion.2 = bf16[8,160,1024]{2,1,0:T(8,128)(2,1)} fusion(bf16[160,8,1024]{2,0,1:T(8,128)(2,1)S(1)} %copy.22, s32[1024]{0:T(1024)S(1)} %pad_clamp_fusion.2), kind=kCustom, calls=%fused_computation.2 | custom fusion | bytes 5242912 | tf_op jit(solution)/shard_map/jit(_take)/gather | solution.py:102
  22.8 3.6 %slice_select_fusion = bf16[8,154,1024]{2,1,0:T(8,128)(2,1)} fusion(bf16[8,160,1024]{2,1,0:T(8,128)(2,1)} %gather_fusion.2, pred[8]{0:T(512)(128)(4,1)S(1)} %compare_and_fusion), kind=kLoop, calls=%fused_computation.17 | loop fusion | flops 1261568 | bytes 5046280 | tf_op jit(solution)/shard_map/jit(_take)/select_n | solution.py:102
  26.4 4.4 %all-to-all-start.1 = ((bf16[8,154,1024]{2,1,0:T(8,128)(2,1)}), bf16[8,154,1024]{2,1,0:T(8,128)(2,1)}, u32[]{:S(2)}, u32[]{:S(2)}) async-start(bf16[8,154,1024]{2,1,0:T(8,128)(2,1)} %slice_select_fusion), calls=%async_computation.1 | async-start | bytes 5242880 | tf_op jit(solution)/shard_map/all_to_all | solution.py:108
  32.6 4.4 %fusion.29 = (s32[320]{0:T(512)S(1)}, s32[320,1]{0,1:T(1,128)S(1)}) fusion(s32[]{:T(128)} %bitcast.7, s32[]{:T(128)} %bitcast.8, s32[]{:T(128)} %bitcast.9, s32[]{:T(128)} %bitcast.10, s32[]{:T(128)} %bitcast.11, s32[]{:T(128)} %bitcast.13, s32[]{:T(128)} %bitcast.12, s32[320]{0:T(512)S(1)} %get-tuple-element.15, s32[320]{0:T(512)S(1)} %get-tuple-element.14), kind=kLoop, calls=%fused_computation.71 | loop fusion | flops 4480 | bytes 5148 | tf_op jit(solution)/shard_map/gather | solution.py:117
  38.3 2.2 %gather_fusion.1 = s32[320]{0:T(512)S(1)} fusion(s32[1232]{0:T(1024)S(1)} %reshape.287, s32[1024]{0:T(1024)S(1)} %pad_clamp_fusion.1), kind=kCustom, calls=%fused_computation.1 | custom fusion | bytes 3840 | tf_op jit(solution)/shard_map/gather | solution.py:122
  41.2 20.3 %all-to-all-done.1 = bf16[8,154,1024]{2,1,0:T(8,128)(2,1)} async-done(((bf16[8,154,1024]{2,1,0:T(8,128)(2,1)}), bf16[8,154,1024]{2,1,0:T(8,128)(2,1)}, u32[]{:S(2)}, u32[]{:S(2)}) %all-to-all-start.1) | async-done | bytes 2523168 | tf_op jit(solution)/shard_map/all_to_all | solution.py:108
  61.5 2.1 %reshape.289 = bf16[1232,1024]{1,0:T(8,128)(2,1)S(1)} reshape(bf16[8,154,1024]{2,1,0:T(8,128)(2,1)} %all-to-all-done.1) | data formatting | bytes 5046272 | tf_op jit(solution)/shard_map/reshape | solution.py:120
  63.6 2.1 %gather_fusion.3 = bf16[320,1024]{1,0:T(8,128)(2,1)S(1)} fusion(bf16[1232,1024]{1,0:T(8,128)(2,1)S(1)} %reshape.289, s32[1024]{0:T(1024)S(1)} %pad_clamp_fusion.1), kind=kCustom, calls=%fused_computation.3 | custom fusion | bytes 1312000 | tf_op jit(solution)/shard_map/gather | solution.py:120
  66.0 8.2 %convolution_convert_fusion = bf16[128,4096]{1,0:T(8,128)(2,1)} fusion(bf16[1,1024,4096]{2,1,0:T(8,128)(2,1)} %param.12, bf16[320,1024]{1,0:T(8,128)(2,1)S(1)} %gather_fusion.3, f32[1024]{0:T(1024)S(1)} %copy-done.1, f32[320]{0:T(512)S(1)} %add_rsqrt_fusion, s32[320]{0:T(512)S(1)} %add_select_fusion), kind=kOutput, calls=%fused_computation.16 | convolution fusion | flops 3033571328 | bytes 10099200 | tf_op jit(solution)/shard_map/dot_general | solution.py:138
  74.1 5.0 %all-to-all-start.2 = ((bf16[8,16,4096]{2,1,0:T(8,128)(2,1)}), bf16[8,16,4096]{2,1,0:T(8,128)(2,1)S(1)}, u32[]{:S(2)}, u32[]{:S(2)}) async-start(bf16[8,16,4096]{2,1,0:T(8,128)(2,1)} %bitcast.16), calls=%async_computation.2 | async-start | bytes 2097152 | tf_op jit(solution)/shard_map/all_to_all | solution.py:140
  79.1 1.0 reshape.378.pos_ref
  80.1 12.9 %all-to-all-done.2 = bf16[8,16,4096]{2,1,0:T(8,128)(2,1)S(1)} async-done(((bf16[8,16,4096]{2,1,0:T(8,128)(2,1)}), bf16[8,16,4096]{2,1,0:T(8,128)(2,1)S(1)}, u32[]{:S(2)}, u32[]{:S(2)}) %all-to-all-start.2) | async-done | bytes 1048608 | tf_op jit(solution)/shard_map/all_to_all | solution.py:140
  93.4 3.7 %collective-permute-start.2 = (bf16[16,4096]{1,0:T(8,128)(2,1)S(1)}, bf16[16,4096]{1,0:T(8,128)(2,1)S(1)}, u32[]{:S(2)}, u32[]{:S(2)}) collective-permute-start(bf16[16,4096]{1,0:T(8,128)(2,1)S(1)} %multiply_convert_fusion), channel_id=1, source_target_pairs={{0,3},{1,0},{2,1},{3,2},{4,7},{5,4},{6,5},{7,6},{8,11},{9,8},{10,9... | collective-permute-start | bytes 393224 | tf_op jit(solution)/shard_map/ppermute | solution.py:149
  97.1 1.0 collective-permute-start
  98.2 2.8 %collective-permute-done.2 = bf16[16,4096]{1,0:T(8,128)(2,1)S(1)} collective-permute-done((bf16[16,4096]{1,0:T(8,128)(2,1)S(1)}, bf16[16,4096]{1,0:T(8,128)(2,1)S(1)}, u32[]{:S(2)}, u32[]{:S(2)}) %collective-permute-start.2) | collective-permute-done | bytes 131104 | tf_op jit(solution)/shard_map/ppermute | solution.py:149
  101.0 7.6 %collective-permute-done.1 = bf16[16,4096]{1,0:T(8,128)(2,1)S(1)} collective-permute-done((bf16[16,4096]{1,0:T(8,128)(2,1)S(1)}, bf16[16,4096]{1,0:T(8,128)(2,1)S(1)}, u32[]{:S(2)}, u32[]{:S(2)}) %collective-permute-start.1) | collective-permute-done | bytes 131104 | tf_op jit(solution)/shard_map/ppermute | solution.py:149
  108.7 1.4 gather_fusion.4
  110.1 17.1 %shard_map.103 = (f32[896,1]{1,0:T(8,128)}, bf16[896,4096]{1,0:T(8,128)(2,1)}, f32[64,4096]{1,0:T(8,128)}) custom-call(bf16[896,4096]{1,0:T(8,128)(2,1)} %q_ref.1, bf16[64,4096]{1,0:T(8,128)(2,1)} %bitcast.38, s32[896,1]{1,0:T(8,128)} %reshape.378.pos_ref), custom_call_target="tpu_custom_call" | custom-call | flops 1879048192 | bytes 14680064 | tf_op jit(solution)/shard_map/pallas_call | solution.py:64
  127.2 1.8 %reduce.7 = f32[896]{0:T(1024)} reduce(f32[896,1]{1,0:T(8,128)} %get-tuple-element.6, f32[]{:T(128)} %constant.112), dimensions={1}, to_apply=%get-tuple-element.6.reduce_sub_computation | reduce | bytes 7172 | tf_op jit(solution)/shard_map/pallas_call | solution.py:64
  129.1 24.7 %reduce-scatter.2.cloned.1.call-done = f32[16,4096]{1,0:T(8,128)} async-done(((f32[64,4096]{1,0:T(8,128)}), f32[16,4096]{1,0:T(8,128)}) %reduce-scatter.2.cloned.1.call-update) | async-done | bytes 262160 | tf_op jit(solution)/shard_map/reduce_scatter | solution.py:157
  (40 shorter events, 8.0 us)
Async XLA Ops:
  13.1 13.2 %all-to-all-start = ((s32[8,1,154]{2,1,0:T(1,128)}), s32[8,1,154]{2,1,0:T(1,128)S(1)}, u32[]{:S(2)}, u32[]{:S(2)}) async-start(s32[8,1,154]{2,1,0:T(1,128)} %copy.21), calls=%async_computation | async-start | bytes 16384 | tf_op jit(solution)/shard_map/all_to_all | solution.py:109
  26.4 35.2 %all-to-all-start.1 = ((bf16[8,154,1024]{2,1,0:T(8,128)(2,1)}), bf16[8,154,1024]{2,1,0:T(8,128)(2,1)}, u32[]{:S(2)}, u32[]{:S(2)}) async-start(bf16[8,154,1024]{2,1,0:T(8,128)(2,1)} %slice_select_fusion), calls=%async_computation.1 | async-start | bytes 5242880 | tf_op jit(solution)/shard_map/all_to_all | solution.py:108
  63.6 2.4 %copy-start.1 = (f32[1024]{0:T(1024)S(1)}, f32[1024]{0:T(1024)}, u32[]{:S(2)}) copy-start(f32[1024]{0:T(1024)} %param.13) | copy-start | bytes 12292
  65.9 13.2 %copy-start = (s32[896]{0:T(1024)S(1)}, s32[896]{0:T(1024)}, u32[]{:S(2)}) copy-start(s32[896]{0:T(1024)} %param.15) | copy-start | bytes 10756
  74.1 18.9 %all-to-all-start.2 = ((bf16[8,16,4096]{2,1,0:T(8,128)(2,1)}), bf16[8,16,4096]{2,1,0:T(8,128)(2,1)S(1)}, u32[]{:S(2)}, u32[]{:S(2)}) async-start(bf16[8,16,4096]{2,1,0:T(8,128)(2,1)} %bitcast.16), calls=%async_computation.2 | async-start | bytes 2097152 | tf_op jit(solution)/shard_map/all_to_all | solution.py:140
  79.1 74.6 %reduce-scatter.2.cloned.1.call-start = ((), (), s32[]{:S(2)}) async-start(), calls=%async_computation.4 | async-start | bytes 1310720 | tf_op jit(solution)/shard_map/reduce_scatter | solution.py:157
  93.4 7.6 %collective-permute-start.2 = (bf16[16,4096]{1,0:T(8,128)(2,1)S(1)}, bf16[16,4096]{1,0:T(8,128)(2,1)S(1)}, u32[]{:S(2)}, u32[]{:S(2)}) collective-permute-start(bf16[16,4096]{1,0:T(8,128)(2,1)S(1)} %multiply_convert_fusion), channel_id=1, source_target_pairs={{0,3},{1,0},{2,1},{3,2},{4,7},{5,4},{6,5},{7,6},{8,11},{9,8},{10,9... | collective-permute-start | bytes 393224 | tf_op jit(solution)/shard_map/ppermute | solution.py:149
  97.1 11.6 %collective-permute-start.1 = (bf16[16,4096]{1,0:T(8,128)(2,1)S(1)}, bf16[16,4096]{1,0:T(8,128)(2,1)S(1)}, u32[]{:S(2)}, u32[]{:S(2)}) collective-permute-start(bf16[16,4096]{1,0:T(8,128)(2,1)S(1)} %multiply_convert_fusion), channel_id=1, source_target_pairs={{0,2},{1,3},{2,0},{3,1},{4,6},{5,7},{6,4},{7,5},{8,10},{9,11},{10,... | collective-permute-start | bytes 393224 | tf_op jit(solution)/shard_map/ppermute | solution.py:149
  97.1 11.6 %collective-permute-start = (bf16[16,4096]{1,0:T(8,128)(2,1)S(1)}, bf16[16,4096]{1,0:T(8,128)(2,1)S(1)}, u32[]{:S(2)}, u32[]{:S(2)}) collective-permute-start(bf16[16,4096]{1,0:T(8,128)(2,1)S(1)} %multiply_convert_fusion), channel_id=1, source_target_pairs={{0,1},{1,2},{2,3},{3,0},{4,5},{5,6},{6,7},{7,4},{8,9},{9,10},{10,1... | collective-permute-start | bytes 393224 | tf_op jit(solution)/shard_map/ppermute | solution.py:149
Sparse Core Ops, SparseCore 0:
  127.4 26.3 reduce-scatter.1

commit v5 on v4

--- a/solution.py
+++ b/solution.py
@@ -31,7 +31,7 @@
     )
 
 
-def contrast_kernel(q_ref, d_ref, pos_ref, loss_ref, gq_ref, gd_ref):
+def score_kernel(q_ref, d_ref, hit_ref, loss_ref, wb_ref, tot_ref, gd_ref):
     @pl.when(pl.program_id(0) == 0)
     def _():
         gd_ref[...] = jnp.zeros_like(gd_ref)
@@ -40,50 +40,76 @@
     query_unit = (
         widened * lax.rsqrt(jnp.sum(widened * widened, axis=-1, keepdims=True) + epsilon)
     ).astype(jnp.bfloat16)
-    docs = d_ref[...]
-    logits = logit_scale * contract_rows(query_unit, docs)
+    logits = logit_scale * contract_rows(query_unit, d_ref[...])
     weights = jnp.exp(logits)
     totals = jnp.sum(weights, axis=1, keepdims=True)
-    numerator = jnp.dot(weights.astype(jnp.bfloat16), docs, preferred_element_type=jnp.float32)
-    matches = pos_ref[...] == lax.broadcasted_iota(jnp.int32, logits.shape, 1)
-    hits = matches.astype(jnp.float32)
-    chosen_logit = jnp.sum(jnp.where(matches, logits, 0.0), axis=1, keepdims=True)
-    chosen_doc = jnp.dot(hits.astype(jnp.bfloat16), docs, preferred_element_type=jnp.float32)
+    hits = hit_ref[...].astype(jnp.float32)
+    chosen_logit = jnp.sum(hits * logits, axis=1, keepdims=True)
     loss_ref[...] = jnp.log(totals) - chosen_logit
-    gq_ref[...] = (logit_scale * (numerator / totals - chosen_doc)).astype(jnp.bfloat16)
+    wb_ref[...] = weights.astype(jnp.bfloat16)
+    tot_ref[...] = totals
     coefficient_t = (weights / totals - hits).T.astype(jnp.bfloat16)
     gd_ref[...] += logit_scale * jnp.dot(
         coefficient_t, query_unit, preferred_element_type=jnp.float32
     )
 
 
-def contrast(queries, doc_piece, positives, tile=128):
+def query_grad_kernel(wb_ref, tot_ref, hit_ref, d_ref, gq_ref):
+    docs = d_ref[...]
+    numerator = jnp.dot(wb_ref[...], docs, preferred_element_type=jnp.float32)
+    chosen_doc = jnp.dot(hit_ref[...], docs, preferred_element_type=jnp.float32)
+    gq_ref[...] = (logit_scale * (numerator / tot_ref[...] - chosen_doc)).astype(jnp.bfloat16)
+
+
+def scores(queries, doc_piece, hits, tile=128):
     rows, width = queries.shape
     docs = doc_piece.shape[0]
-    steps = rows // tile
     return pl.pallas_call(
-        contrast_kernel,
-        grid=(steps,),
+        score_kernel,
+        grid=(rows // tile,),
         in_specs=[
             pl.BlockSpec((tile, width), lambda i: (i, 0)),
             pl.BlockSpec((docs, width), lambda i: (0, 0)),
-            pl.BlockSpec((tile, 1), lambda i: (i, 0)),
+            pl.BlockSpec((tile, docs), lambda i: (i, 0)),
         ],
         out_specs=[
             pl.BlockSpec((tile, 1), lambda i: (i, 0)),
-            pl.BlockSpec((tile, width), lambda i: (i, 0)),
+            pl.BlockSpec((tile, docs), lambda i: (i, 0)),
+            pl.BlockSpec((tile, 1), lambda i: (i, 0)),
             pl.BlockSpec((docs, width), lambda i: (0, 0)),
         ],
         out_shape=[
             jax.ShapeDtypeStruct((rows, 1), jnp.float32),
-            jax.ShapeDtypeStruct((rows, width), jnp.bfloat16),
+            jax.ShapeDtypeStruct((rows, docs), jnp.bfloat16),
+            jax.ShapeDtypeStruct((rows, 1), jnp.float32),
             jax.ShapeDtypeStruct((docs, width), jnp.float32),
         ],
         compiler_params=pltpu.CompilerParams(dimension_semantics=("arbitrary",)),
         cost_estimate=pl.CostEstimate(
-            flops=8 * rows * docs * width, transcendentals=rows * docs, bytes_accessed=4 * rows * width
+            flops=4 * rows * docs * width, transcendentals=rows * docs, bytes_accessed=2 * rows * width
         ),
-    )(queries, doc_piece, positives.reshape(rows, 1))
+    )(queries, doc_piece, hits)
+
+
+def query_grads(weights, totals, hits, doc_piece, tile=128):
+    rows, docs = weights.shape
+    width = doc_piece.shape[1]
+    return pl.pallas_call(
+        query_grad_kernel,
+        grid=(rows // tile,),
+        in_specs=[
+            pl.BlockSpec((tile, docs), lambda i: (i, 0)),
+            pl.BlockSpec((tile, 1), lambda i: (i, 0)),
+            pl.BlockSpec((tile, docs), lambda i: (i, 0)),
+            pl.BlockSpec((docs, width), lambda i: (0, 0)),
+        ],
+        out_specs=pl.BlockSpec((tile, width), lambda i: (i, 0)),
+        out_shape=jax.ShapeDtypeStruct((rows, width), jnp.bfloat16),
+        compiler_params=pltpu.CompilerParams(dimension_semantics=("arbitrary",)),
+        cost_estimate=pl.CostEstimate(
+            flops=4 * rows * docs * width, transcendentals=0, bytes_accessed=2 * rows * width
+        ),
+    )(weights, totals, hits, doc_piece)
 
 
 def on_device(
@@ -152,9 +178,14 @@
     )
     arrival_of = (position - jnp.arange(cycle_size, dtype=jnp.int32)) % cycle_size
     doc_piece = arrived[arrival_of].reshape(cycle_size * doc_unit.shape[0], emb_width)
-    loss_col, grad_queries, grad_part = contrast(queries, doc_piece, positives)
+    piece_rows = doc_piece.shape[0]
+    hits = (positives[:, None] == jnp.arange(piece_rows, dtype=jnp.int32)[None, :]).astype(
+        jnp.bfloat16
+    )
+    loss_col, weights, totals, grad_part = scores(queries, doc_piece, hits)
+    grad_docs = lax.psum_scatter(grad_part, "blk", scatter_dimension=0, tiled=True)
+    grad_queries = query_grads(weights, totals, hits, doc_piece)
     loss_rows = loss_col.reshape(loss_col.shape[0])
-    grad_docs = lax.psum_scatter(grad_part, "blk", scatter_dimension=0, tiled=True)
     return (loss_rows, grad_queries, grad_docs)
 
 

time: 163 us -> 158 us (0.969)
  waiting for transfers between devices: 68.4 us -> 60.4 us
  Pallas kernels: 17.1 us -> 20.5 us
    reduce_scatter x1, waiting for transfers between devices: 24.7 us -> 16.6 us  [on_device(): lax.psum_scatter(grad_part, 'blk', scatter_dimension=0, tiled=True)]
    pallas_call x1 -> x2, Pallas kernels: 17.1 us -> 20.5 us  [the longest x1 12.4 us: scores(): pl.pallas_call(score_kernel, grid=(rows // tile,), in_specs=[pl.BlockSpec...]
  transfers between devices with their start and end apart: 7 -> 7, of which waited for: 5 -> 5; matrix products, arithmetic and copies ran while one was open for 14% -> 14% of each run, Pallas kernels for 0% -> 5%
where the time goes in v5:
time: 158 us; the launch traced here: 156 us
  waiting for transfers between devices  60.4 us (38%)
  Pallas kernels  20.5 us (13%)
  starting transfers between devices  18.3 us (12%)
  local copies, waits for them, and re-layouts  17.2 us (11%)
  other arithmetic  16.6 us (11%)
  between operations  14.8 us (9%)
  matrix products  8.18 us (5%)
    all_to_all x1, waiting for transfers between devices, on_device(): lax.all_to_all(send_rows, 'dp', split_axis=0, concat_axis=0, tiled=True)  20.3 us
    reduce_scatter x1, waiting for transfers between devices, on_device(): lax.psum_scatter(grad_part, 'blk', scatter_dimension=0, tiled=True)  16.6 us
    all_to_all x1, waiting for transfers between devices, on_device(): lax.all_to_all(partial, 'dp', split_axis=0, concat_axis=0, tiled=True)  13 us
    pallas_call x1, Pallas kernels, scores(): pl.pallas_call(score_kernel, grid=(rows // tile,), in_specs=[pl.BlockSpec...  12.4 us
    ppermute x3, waiting for transfers between devices, on_device(): lax.ppermute(doc_unit, 'blk', [(i, (i + shift) % cycle_size) for i in ran...  10.5 us
    dot_general x1, matrix products, on_device(): partial = jnp.dot(selector, embedded, preferred_element_type=jnp.float32)  8.18 us
    pallas_call x1, Pallas kernels, query_grads(): pl.pallas_call(query_grad_kernel, grid=(rows // tile,), in_specs=[pl.Bloc...  8.04 us
    gather x3, other arithmetic, on_device(): slot_of = source_of * capacity + packed_index - starts[source_of]  5.09 us
  transfers between devices with their start and end apart: 7, of which 5 were waited for; matrix products, arithmetic and copies ran while one was open for 14% of the time, Pallas kernels for 5%

profile of v5, /device:TPU:2, one launch (start us, length us, event | category | flops | bytes accessed | tf_op | source)
XLA Modules:
  0.0 155.9 jit_solution(592721207684542816)
XLA Ops:
  7.2 1.2 slice.9
  13.1 4.3 %all-to-all-start = ((s32[8,1,154]{2,1,0:T(1,128)}), s32[8,1,154]{2,1,0:T(1,128)S(1)}, u32[]{:S(2)}, u32[]{:S(2)}) async-start(s32[8,1,154]{2,1,0:T(1,128)} %copy.18), calls=%async_computation | async-start | bytes 16384 | tf_op jit(solution)/shard_map/all_to_all | solution.py:135
  17.4 3.2 %copy.19 = bf16[160,8,1024]{2,0,1:T(8,128)(2,1)S(1)} copy(bf16[160,8,1024]{2,1,0:T(8,128)(2,1)} %bitcast.39) | data formatting | bytes 5242880 | tf_op jit(solution)/shard_map/reshape | solution.py:127
  20.6 2.2 %gather_fusion.2 = bf16[8,160,1024]{2,1,0:T(8,128)(2,1)} fusion(bf16[160,8,1024]{2,0,1:T(8,128)(2,1)S(1)} %copy.19, s32[1024]{0:T(1024)S(1)} %pad_clamp_fusion.2), kind=kCustom, calls=%fused_computation.2 | custom fusion | bytes 5242912 | tf_op jit(solution)/shard_map/jit(_take)/gather | solution.py:128
  22.8 3.6 %slice_select_fusion = bf16[8,154,1024]{2,1,0:T(8,128)(2,1)} fusion(bf16[8,160,1024]{2,1,0:T(8,128)(2,1)} %gather_fusion.2, pred[8]{0:T(512)(128)(4,1)S(1)} %compare_and_fusion), kind=kLoop, calls=%fused_computation.17 | loop fusion | flops 1261568 | bytes 5046280 | tf_op jit(solution)/shard_map/jit(_take)/select_n | solution.py:128
  26.4 4.4 %all-to-all-start.1 = ((bf16[8,154,1024]{2,1,0:T(8,128)(2,1)}), bf16[8,154,1024]{2,1,0:T(8,128)(2,1)}, u32[]{:S(2)}, u32[]{:S(2)}) async-start(bf16[8,154,1024]{2,1,0:T(8,128)(2,1)} %slice_select_fusion), calls=%async_computation.1 | async-start | bytes 5242880 | tf_op jit(solution)/shard_map/all_to_all | solution.py:134
  32.6 4.4 %fusion.30 = (s32[320]{0:T(512)S(1)}, s32[320,1]{0,1:T(1,128)S(1)}) fusion(s32[]{:T(128)} %bitcast.7, s32[]{:T(128)} %bitcast.8, s32[]{:T(128)} %bitcast.9, s32[]{:T(128)} %bitcast.10, s32[]{:T(128)} %bitcast.11, s32[]{:T(128)} %bitcast.13, s32[]{:T(128)} %bitcast.12, s32[320]{0:T(512)S(1)} %get-tuple-element.17, s32[320]{0:T(512)S(1)} %get-tuple-element.16), kind=kLoop, calls=%fused_computation.73 | loop fusion | flops 4480 | bytes 5148 | tf_op jit(solution)/shard_map/gather | solution.py:143
  38.3 2.2 %gather_fusion.1 = s32[320]{0:T(512)S(1)} fusion(s32[1232]{0:T(1024)S(1)} %reshape.285, s32[1024]{0:T(1024)S(1)} %pad_clamp_fusion.1), kind=kCustom, calls=%fused_computation.1 | custom fusion | bytes 3840 | tf_op jit(solution)/shard_map/gather | solution.py:148
  41.2 20.3 %all-to-all-done.1 = bf16[8,154,1024]{2,1,0:T(8,128)(2,1)} async-done(((bf16[8,154,1024]{2,1,0:T(8,128)(2,1)}), bf16[8,154,1024]{2,1,0:T(8,128)(2,1)}, u32[]{:S(2)}, u32[]{:S(2)}) %all-to-all-start.1) | async-done | bytes 2523168 | tf_op jit(solution)/shard_map/all_to_all | solution.py:134
  61.5 2.1 %reshape.287 = bf16[1232,1024]{1,0:T(8,128)(2,1)S(1)} reshape(bf16[8,154,1024]{2,1,0:T(8,128)(2,1)} %all-to-all-done.1) | data formatting | bytes 5046272 | tf_op jit(solution)/shard_map/reshape | solution.py:146
  63.6 2.1 %gather_fusion.3 = bf16[320,1024]{1,0:T(8,128)(2,1)S(1)} fusion(bf16[1232,1024]{1,0:T(8,128)(2,1)S(1)} %reshape.287, s32[1024]{0:T(1024)S(1)} %pad_clamp_fusion.1), kind=kCustom, calls=%fused_computation.3 | custom fusion | bytes 1312000 | tf_op jit(solution)/shard_map/gather | solution.py:146
  66.0 8.2 %convolution_convert_fusion = bf16[128,4096]{1,0:T(8,128)(2,1)} fusion(bf16[1,1024,4096]{2,1,0:T(8,128)(2,1)} %param.12, bf16[320,1024]{1,0:T(8,128)(2,1)S(1)} %gather_fusion.3, f32[1024]{0:T(1024)S(1)} %copy-done.1, f32[320]{0:T(512)S(1)} %add_rsqrt_fusion, s32[320]{0:T(512)S(1)} %add_select_fusion), kind=kOutput, calls=%fused_computation.16 | convolution fusion | flops 3033571328 | bytes 10099200 | tf_op jit(solution)/shard_map/dot_general | solution.py:164
  74.1 5.0 %all-to-all-start.2 = ((bf16[8,16,4096]{2,1,0:T(8,128)(2,1)}), bf16[8,16,4096]{2,1,0:T(8,128)(2,1)S(1)}, u32[]{:S(2)}, u32[]{:S(2)}) async-start(bf16[8,16,4096]{2,1,0:T(8,128)(2,1)} %bitcast.16), calls=%async_computation.2 | async-start | bytes 2097152 | tf_op jit(solution)/shard_map/all_to_all | solution.py:166
  79.2 0.9 fusion.23.hit_ref
  80.0 13.0 %all-to-all-done.2 = bf16[8,16,4096]{2,1,0:T(8,128)(2,1)S(1)} async-done(((bf16[8,16,4096]{2,1,0:T(8,128)(2,1)}), bf16[8,16,4096]{2,1,0:T(8,128)(2,1)S(1)}, u32[]{:S(2)}, u32[]{:S(2)}) %all-to-all-start.2) | async-done | bytes 1048608 | tf_op jit(solution)/shard_map/all_to_all | solution.py:166
  93.4 3.7 %collective-permute-start.2 = (bf16[16,4096]{1,0:T(8,128)(2,1)S(1)}, bf16[16,4096]{1,0:T(8,128)(2,1)S(1)}, u32[]{:S(2)}, u32[]{:S(2)}) collective-permute-start(bf16[16,4096]{1,0:T(8,128)(2,1)S(1)} %multiply_convert_fusion), channel_id=1, source_target_pairs={{0,3},{1,0},{2,1},{3,2},{4,7},{5,4},{6,5},{7,6},{8,11},{9,8},{10,9... | collective-permute-start | bytes 393224 | tf_op jit(solution)/shard_map/ppermute | solution.py:175
  97.1 1.0 collective-permute-start
  98.2 2.8 %collective-permute-done.2 = bf16[16,4096]{1,0:T(8,128)(2,1)S(1)} collective-permute-done((bf16[16,4096]{1,0:T(8,128)(2,1)S(1)}, bf16[16,4096]{1,0:T(8,128)(2,1)S(1)}, u32[]{:S(2)}, u32[]{:S(2)}) %collective-permute-start.2) | collective-permute-done | bytes 131104 | tf_op jit(solution)/shard_map/ppermute | solution.py:175
  101.0 7.6 %collective-permute-done.1 = bf16[16,4096]{1,0:T(8,128)(2,1)S(1)} collective-permute-done((bf16[16,4096]{1,0:T(8,128)(2,1)S(1)}, bf16[16,4096]{1,0:T(8,128)(2,1)S(1)}, u32[]{:S(2)}, u32[]{:S(2)}) %collective-permute-start.1) | collective-permute-done | bytes 131104 | tf_op jit(solution)/shard_map/ppermute | solution.py:175
  108.7 1.4 gather_fusion.4
  110.1 12.4 %shard_map.103 = (f32[896,1]{1,0:T(8,128)}, bf16[896,64]{1,0:T(8,128)(2,1)}, f32[896,1]{1,0:T(8,128)}, f32[64,4096]{1,0:T(8,128)}) custom-call(bf16[896,4096]{1,0:T(8,128)(2,1)} %q_ref.1, bf16[64,4096]{1,0:T(8,128)(2,1)} %bitcast.37, bf16[896,64]{1,0:T(8,128)(2,1)} %fusion.23.hit_ref), custom_call_target="tpu_custom_call" | custom-call | flops 939524096 | bytes 7340032 | tf_op jit(solution)/shard_map/pallas_call | solution.py:67
  122.6 1.8 %reduce.7 = f32[896]{0:T(1024)} reduce(f32[896,1]{1,0:T(8,128)} %get-tuple-element.7, f32[]{:T(128)} %constant.112), dimensions={1}, to_apply=%get-tuple-element.7.reduce_sub_computation | reduce | bytes 7172 | tf_op jit(solution)/shard_map/pallas_call | solution.py:67
  124.4 8.0 %shard_map.104 = bf16[896,4096]{1,0:T(8,128)(2,1)} custom-call(bf16[896,64]{1,0:T(8,128)(2,1)} %get-tuple-element.8.wb_ref, f32[896,1]{1,0:T(8,128)} %get-tuple-element.9.tot_ref, bf16[896,64]{1,0:T(8,128)(2,1)} %fusion.23.hit_ref, bf16[64,4096]{1,0:T(8,128)(2,1)} %bitcast.38), custom_call_target="tpu_custom_call" | custom-call | flops 939524096 | bytes 7340032 | tf_op jit(solution)/shard_map/pallas_call | solution.py:97
  132.5 16.6 %reduce-scatter.2.cloned.1.call-done = f32[16,4096]{1,0:T(8,128)} async-done(((f32[64,4096]{1,0:T(8,128)}), f32[16,4096]{1,0:T(8,128)}) %reduce-scatter.2.cloned.1.call-update) | async-done | bytes 262160 | tf_op jit(solution)/shard_map/reduce_scatter | solution.py:186
  (41 shorter events, 8.8 us)
Async XLA Ops:
  13.1 13.2 %all-to-all-start = ((s32[8,1,154]{2,1,0:T(1,128)}), s32[8,1,154]{2,1,0:T(1,128)S(1)}, u32[]{:S(2)}, u32[]{:S(2)}) async-start(s32[8,1,154]{2,1,0:T(1,128)} %copy.18), calls=%async_computation | async-start | bytes 16384 | tf_op jit(solution)/shard_map/all_to_all | solution.py:135
  26.4 35.2 %all-to-all-start.1 = ((bf16[8,154,1024]{2,1,0:T(8,128)(2,1)}), bf16[8,154,1024]{2,1,0:T(8,128)(2,1)}, u32[]{:S(2)}, u32[]{:S(2)}) async-start(bf16[8,154,1024]{2,1,0:T(8,128)(2,1)} %slice_select_fusion), calls=%async_computation.1 | async-start | bytes 5242880 | tf_op jit(solution)/shard_map/all_to_all | solution.py:134
  63.6 2.4 %copy-start.1 = (f32[1024]{0:T(1024)S(1)}, f32[1024]{0:T(1024)}, u32[]{:S(2)}) copy-start(f32[1024]{0:T(1024)} %param.13) | copy-start | bytes 12292
  65.9 13.2 %copy-start = (s32[896]{0:T(1024)S(1)}, s32[896]{0:T(1024)}, u32[]{:S(2)}) copy-start(s32[896]{0:T(1024)} %param.15) | copy-start | bytes 10756
  74.1 18.9 %all-to-all-start.2 = ((bf16[8,16,4096]{2,1,0:T(8,128)(2,1)}), bf16[8,16,4096]{2,1,0:T(8,128)(2,1)S(1)}, u32[]{:S(2)}, u32[]{:S(2)}) async-start(bf16[8,16,4096]{2,1,0:T(8,128)(2,1)} %bitcast.16), calls=%async_computation.2 | async-start | bytes 2097152 | tf_op jit(solution)/shard_map/all_to_all | solution.py:166
  79.1 70.0 %reduce-scatter.2.cloned.1.call-start = ((), (), s32[]{:S(2)}) async-start(), calls=%async_computation.4 | async-start | bytes 1310720 | tf_op jit(solution)/shard_map/reduce_scatter | solution.py:186
  93.4 7.6 %collective-permute-start.2 = (bf16[16,4096]{1,0:T(8,128)(2,1)S(1)}, bf16[16,4096]{1,0:T(8,128)(2,1)S(1)}, u32[]{:S(2)}, u32[]{:S(2)}) collective-permute-start(bf16[16,4096]{1,0:T(8,128)(2,1)S(1)} %multiply_convert_fusion), channel_id=1, source_target_pairs={{0,3},{1,0},{2,1},{3,2},{4,7},{5,4},{6,5},{7,6},{8,11},{9,8},{10,9... | collective-permute-start | bytes 393224 | tf_op jit(solution)/shard_map/ppermute | solution.py:175
  97.1 11.6 %collective-permute-start.1 = (bf16[16,4096]{1,0:T(8,128)(2,1)S(1)}, bf16[16,4096]{1,0:T(8,128)(2,1)S(1)}, u32[]{:S(2)}, u32[]{:S(2)}) collective-permute-start(bf16[16,4096]{1,0:T(8,128)(2,1)S(1)} %multiply_convert_fusion), channel_id=1, source_target_pairs={{0,2},{1,3},{2,0},{3,1},{4,6},{5,7},{6,4},{7,5},{8,10},{9,11},{10,... | collective-permute-start | bytes 393224 | tf_op jit(solution)/shard_map/ppermute | solution.py:175
  97.1 11.6 %collective-permute-start = (bf16[16,4096]{1,0:T(8,128)(2,1)S(1)}, bf16[16,4096]{1,0:T(8,128)(2,1)S(1)}, u32[]{:S(2)}, u32[]{:S(2)}) collective-permute-start(bf16[16,4096]{1,0:T(8,128)(2,1)S(1)} %multiply_convert_fusion), channel_id=1, source_target_pairs={{0,1},{1,2},{2,3},{3,0},{4,5},{5,6},{6,7},{7,4},{8,9},{9,10},{10,1... | collective-permute-start | bytes 393224 | tf_op jit(solution)/shard_map/ppermute | solution.py:175
Sparse Core Ops, SparseCore 0:
  122.7 26.3 reduce-scatter.1

commit v6 on v5

--- a/solution.py
+++ b/solution.py
@@ -112,6 +112,21 @@
     )(weights, totals, hits, doc_piece)
 
 
+def line_reduce_scatter(parts, axis):
+    size = lax.axis_size(axis)
+    own = lax.axis_index(axis)
+    rightward = [(i, i + 1) for i in range(size - 1)]
+    leftward = [(i + 1, i) for i in range(size - 1)]
+    from_left = jnp.zeros_like(parts[0])
+    from_right = jnp.zeros_like(parts[0])
+    for step in range(1, size):
+        right_block = jnp.minimum(own + (size - step), size - 1)
+        left_block = jnp.maximum(own - (size - step), 0)
+        from_left = lax.ppermute(parts[right_block] + from_left, axis, rightward)
+        from_right = lax.ppermute(parts[left_block] + from_right, axis, leftward)
+    return parts[own] + from_left + from_right
+
+
 def on_device(
     spans, span_counts, session_ids, destinations, expert_weight, norm_gain, queries, positives
 ):
@@ -183,7 +198,9 @@
         jnp.bfloat16
     )
     loss_col, weights, totals, grad_part = scores(queries, doc_piece, hits)
-    grad_docs = lax.psum_scatter(grad_part, "blk", scatter_dimension=0, tiled=True)
+    grad_docs = line_reduce_scatter(
+        grad_part.reshape(cycle_size, doc_unit.shape[0], emb_width), "blk"
+    )
     grad_queries = query_grads(weights, totals, hits, doc_piece)
     loss_rows = loss_col.reshape(loss_col.shape[0])
     return (loss_rows, grad_queries, grad_docs)

time: 158 us -> 158 us (level)
  the two profiles are of different devices: /device:TPU:2 before, /device:TPU:26 now
where the time goes in v6:
time: 158 us; the launch traced here: 157 us
  waiting for transfers between devices  56.1 us (36%)
  starting transfers between devices  34.2 us (22%)
  Pallas kernels  20.4 us (13%)
  other arithmetic  18.4 us (12%)
  local copies, waits for them, and re-layouts  18.3 us (12%)
  matrix products  8.18 us (5%)
    all_to_all x1, waiting for transfers between devices, on_device(): lax.all_to_all(send_rows, 'dp', split_axis=0, concat_axis=0, tiled=True)  20.3 us
    all_to_all x1, waiting for transfers between devices, on_device(): lax.all_to_all(partial, 'dp', split_axis=0, concat_axis=0, tiled=True)  13 us
    ppermute x3, starting transfers between devices, line_reduce_scatter(): from_right = lax.ppermute(parts[left_block] + from_right, axis, leftward)  12.8 us
    pallas_call x1, Pallas kernels, scores(): pl.pallas_call(score_kernel, grid=(rows // tile,), in_specs=[pl.BlockSpec...  12.4 us
    ppermute x3, waiting for transfers between devices, line_reduce_scatter(): from_left = lax.ppermute(parts[right_block] + from_left, axis, rightward)  11.2 us
    ppermute x3, waiting for transfers between devices, on_device(): lax.ppermute(doc_unit, 'blk', [(i, (i + shift) % cycle_size) for i in ran...  9.12 us
    dot_general x1, matrix products, on_device(): partial = jnp.dot(selector, embedded, preferred_element_type=jnp.float32)  8.18 us
    pallas_call x1, Pallas kernels, query_grads(): pl.pallas_call(query_grad_kernel, grid=(rows // tile,), in_specs=[pl.Bloc...  8.02 us
  transfers between devices with their start and end apart: 12, of which 7 were waited for; matrix products, arithmetic and copies ran while one was open for 14% of the time, Pallas kernels for 5%

profile of v6, /device:TPU:26, one launch (start us, length us, event | category | flops | bytes accessed | tf_op | source)
XLA Modules:
  0.0 157.3 jit_solution(5504064711402464919)
XLA Ops:
  6.6 4.3 %all-to-all-start = ((s32[8,1,154]{2,1,0:T(1,128)}), s32[8,1,154]{2,1,0:T(1,128)S(1)}, u32[]{:S(2)}, u32[]{:S(2)}) async-start(s32[8,1,154]{2,1,0:T(1,128)} %copy.18), calls=%async_computation | async-start | bytes 16384 | tf_op jit(solution)/shard_map/all_to_all | solution.py:150
  10.9 3.2 %copy.19 = bf16[160,8,1024]{2,0,1:T(8,128)(2,1)S(1)} copy(bf16[160,8,1024]{2,1,0:T(8,128)(2,1)} %bitcast.61) | data formatting | bytes 5242880 | tf_op jit(solution)/shard_map/reshape | solution.py:142
  14.0 2.2 %gather_fusion.2 = bf16[8,160,1024]{2,1,0:T(8,128)(2,1)} fusion(bf16[160,8,1024]{2,0,1:T(8,128)(2,1)S(1)} %copy.19, s32[1024]{0:T(1024)S(1)} %pad_clamp_fusion.2), kind=kCustom, calls=%fused_computation.2 | custom fusion | bytes 5242912 | tf_op jit(solution)/shard_map/jit(_take)/gather | solution.py:143
  16.2 3.6 %slice_select_fusion = bf16[8,154,1024]{2,1,0:T(8,128)(2,1)} fusion(bf16[8,160,1024]{2,1,0:T(8,128)(2,1)} %gather_fusion.2, pred[8]{0:T(512)(128)(4,1)S(1)} %compare_and_fusion), kind=kLoop, calls=%fused_computation.17 | loop fusion | flops 1261568 | bytes 5046280 | tf_op jit(solution)/shard_map/jit(_take)/select_n | solution.py:143
  19.8 4.4 %all-to-all-start.1 = ((bf16[8,154,1024]{2,1,0:T(8,128)(2,1)}), bf16[8,154,1024]{2,1,0:T(8,128)(2,1)}, u32[]{:S(2)}, u32[]{:S(2)}) async-start(bf16[8,154,1024]{2,1,0:T(8,128)(2,1)} %slice_select_fusion), calls=%async_computation.1 | async-start | bytes 5242880 | tf_op jit(solution)/shard_map/all_to_all | solution.py:149
  26.0 4.4 %fusion.31 = (s32[320]{0:T(512)S(1)}, s32[320,1]{0,1:T(1,128)S(1)}) fusion(s32[]{:T(128)} %bitcast.7, s32[]{:T(128)} %bitcast.8, s32[]{:T(128)} %bitcast.9, s32[]{:T(128)} %bitcast.10, s32[]{:T(128)} %bitcast.11, s32[]{:T(128)} %bitcast.13, s32[]{:T(128)} %bitcast.12, s32[320]{0:T(512)S(1)} %get-tuple-element.21, s32[320]{0:T(512)S(1)} %get-tuple-element.20), kind=kLoop, calls=%fused_computation.81 | loop fusion | flops 4480 | bytes 5148 | tf_op jit(solution)/shard_map/gather | solution.py:158
  31.8 2.2 %gather_fusion.1 = s32[320]{0:T(512)S(1)} fusion(s32[1232]{0:T(1024)S(1)} %reshape.288, s32[1024]{0:T(1024)S(1)} %pad_clamp_fusion.1), kind=kCustom, calls=%fused_computation.1 | custom fusion | bytes 3840 | tf_op jit(solution)/shard_map/gather | solution.py:163
  34.7 20.3 %all-to-all-done.1 = bf16[8,154,1024]{2,1,0:T(8,128)(2,1)} async-done(((bf16[8,154,1024]{2,1,0:T(8,128)(2,1)}), bf16[8,154,1024]{2,1,0:T(8,128)(2,1)}, u32[]{:S(2)}, u32[]{:S(2)}) %all-to-all-start.1) | async-done | bytes 2523168 | tf_op jit(solution)/shard_map/all_to_all | solution.py:149
  55.0 2.1 %reshape.290 = bf16[1232,1024]{1,0:T(8,128)(2,1)S(1)} reshape(bf16[8,154,1024]{2,1,0:T(8,128)(2,1)} %all-to-all-done.1) | data formatting | bytes 5046272 | tf_op jit(solution)/shard_map/reshape | solution.py:161
  57.1 2.1 %gather_fusion.3 = bf16[320,1024]{1,0:T(8,128)(2,1)S(1)} fusion(bf16[1232,1024]{1,0:T(8,128)(2,1)S(1)} %reshape.290, s32[1024]{0:T(1024)S(1)} %pad_clamp_fusion.1), kind=kCustom, calls=%fused_computation.3 | custom fusion | bytes 1312000 | tf_op jit(solution)/shard_map/gather | solution.py:161
  59.4 8.2 %convolution_convert_fusion = bf16[128,4096]{1,0:T(8,128)(2,1)} fusion(bf16[1,1024,4096]{2,1,0:T(8,128)(2,1)} %param.12, bf16[320,1024]{1,0:T(8,128)(2,1)S(1)} %gather_fusion.3, f32[1024]{0:T(1024)S(1)} %copy-done.3, f32[320]{0:T(512)S(1)} %add_rsqrt_fusion, s32[320]{0:T(512)S(1)} %add_select_fusion), kind=kOutput, calls=%fused_computation.16 | convolution fusion | flops 3033571328 | bytes 10099200 | tf_op jit(solution)/shard_map/dot_general | solution.py:179
  67.6 5.0 %all-to-all-start.2 = ((bf16[8,16,4096]{2,1,0:T(8,128)(2,1)}), bf16[8,16,4096]{2,1,0:T(8,128)(2,1)S(1)}, u32[]{:S(2)}, u32[]{:S(2)}) async-start(bf16[8,16,4096]{2,1,0:T(8,128)(2,1)} %bitcast.16), calls=%async_computation.2 | async-start | bytes 2097152 | tf_op jit(solution)/shard_map/all_to_all | solution.py:181
  73.5 13.0 %all-to-all-done.2 = bf16[8,16,4096]{2,1,0:T(8,128)(2,1)S(1)} async-done(((bf16[8,16,4096]{2,1,0:T(8,128)(2,1)}), bf16[8,16,4096]{2,1,0:T(8,128)(2,1)S(1)}, u32[]{:S(2)}, u32[]{:S(2)}) %all-to-all-start.2) | async-done | bytes 1048608 | tf_op jit(solution)/shard_map/all_to_all | solution.py:181
  87.7 3.0 %collective-permute-start = (bf16[16,4096]{1,0:T(8,128)(2,1)S(1)}, bf16[16,4096]{1,0:T(8,128)(2,1)S(1)}, u32[]{:S(2)}, u32[]{:S(2)}) collective-permute-start(bf16[16,4096]{1,0:T(8,128)(2,1)S(1)} %multiply_convert_fusion), channel_id=1, source_target_pairs={{0,1},{1,2},{2,3},{3,0},{4,5},{5,6},{6,7},{7,4},{8,9},{9,10},{10,1... | collective-permute-start | bytes 393224 | tf_op jit(solution)/shard_map/ppermute | solution.py:190
  90.9 4.4 %collective-permute-done.2 = bf16[16,4096]{1,0:T(8,128)(2,1)S(1)} collective-permute-done((bf16[16,4096]{1,0:T(8,128)(2,1)S(1)}, bf16[16,4096]{1,0:T(8,128)(2,1)S(1)}, u32[]{:S(2)}, u32[]{:S(2)}) %collective-permute-start.2) | collective-permute-done | bytes 131104 | tf_op jit(solution)/shard_map/ppermute | solution.py:190
  95.2 4.7 %collective-permute-done.1 = bf16[16,4096]{1,0:T(8,128)(2,1)S(1)} collective-permute-done((bf16[16,4096]{1,0:T(8,128)(2,1)S(1)}, bf16[16,4096]{1,0:T(8,128)(2,1)S(1)}, u32[]{:S(2)}, u32[]{:S(2)}) %collective-permute-start.1) | collective-permute-done | bytes 131104 | tf_op jit(solution)/shard_map/ppermute | solution.py:190
  101.4 12.4 %shard_map.103 = (f32[896,1]{1,0:T(8,128)}, bf16[896,64]{1,0:T(8,128)(2,1)}, f32[896,1]{1,0:T(8,128)}, f32[64,4096]{1,0:T(8,128)}) custom-call(bf16[896,4096]{1,0:T(8,128)(2,1)} %q_ref.1, bf16[64,4096]{1,0:T(8,128)(2,1)} %bitcast.54, bf16[896,64]{1,0:T(8,128)(2,1)} %fusion.23.hit_ref), custom_call_target="tpu_custom_call" | custom-call | flops 939524096 | bytes 7340032 | tf_op jit(solution)/shard_map/pallas_call | solution.py:67
  116.4 5.1 %collective-permute-start.6 = (f32[16,4096]{1,0:T(8,128)S(1)}, f32[16,4096]{1,0:T(8,128)S(1)}, u32[]{:S(2)}, u32[]{:S(2)}) collective-permute-start(f32[16,4096]{1,0:T(8,128)S(1)} %get-tuple-element.19), channel_id=1, source_target_pairs={{1,0},{2,1},{3,2},{5,4},{6,5},{7,6},{9,8},{10,9},{11,10},{13,12},{... | collective-permute-start | bytes 786440 | tf_op jit(solution)/shard_map/ppermute | solution.py:126
  121.4 3.8 %collective-permute-done.3 = f32[16,4096]{1,0:T(8,128)S(1)} collective-permute-done((f32[16,4096]{1,0:T(8,128)S(1)}, f32[16,4096]{1,0:T(8,128)S(1)}, u32[]{:S(2)}, u32[]{:S(2)}) %collective-permute-start.3) | collective-permute-done | bytes 262176 | tf_op jit(solution)/shard_map/ppermute | solution.py:125
  127.5 7.4 %collective-permute-done.4 = f32[16,4096]{1,0:T(8,128)S(1)} collective-permute-done((f32[16,4096]{1,0:T(8,128)S(1)}, f32[16,4096]{1,0:T(8,128)S(1)}, u32[]{:S(2)}, u32[]{:S(2)}) %collective-permute-start.4) | collective-permute-done | bytes 262176 | tf_op jit(solution)/shard_map/ppermute | solution.py:125
  136.0 3.4 %collective-permute-start.7 = (f32[16,4096]{1,0:T(8,128)S(1)}, f32[16,4096]{1,0:T(8,128)S(1)}, u32[]{:S(2)}, u32[]{:S(2)}) collective-permute-start(f32[16,4096]{1,0:T(8,128)S(1)} %get-tuple-element.17), channel_id=1, source_target_pairs={{1,0},{2,1},{3,2},{5,4},{6,5},{7,6},{9,8},{10,9},{11,10},{13,12},{... | collective-permute-start | bytes 786440 | tf_op jit(solution)/shard_map/ppermute | solution.py:126
  140.7 2.6 %collective-permute-done.7 = f32[16,4096]{1,0:T(8,128)S(1)} collective-permute-done((f32[16,4096]{1,0:T(8,128)S(1)}, f32[16,4096]{1,0:T(8,128)S(1)}, u32[]{:S(2)}, u32[]{:S(2)}) %collective-permute-start.7) | collective-permute-done | bytes 262176 | tf_op jit(solution)/shard_map/ppermute | solution.py:126
  143.3 4.4 %collective-permute-start.8 = (f32[16,4096]{1,0:T(8,128)S(1)}, f32[16,4096]{1,0:T(8,128)S(1)}, u32[]{:S(2)}, u32[]{:S(2)}) collective-permute-start(f32[16,4096]{1,0:T(8,128)S(1)} %bitcast_add_fusion.1), channel_id=1, source_target_pairs={{1,0},{2,1},{3,2},{5,4},{6,5},{7,6},{9,8},{10,9},{11,10},{13,12},{... | collective-permute-start | bytes 786440 | tf_op jit(solution)/shard_map/ppermute | solution.py:126
  148.5 8.0 %shard_map.104 = bf16[896,4096]{1,0:T(8,128)(2,1)} custom-call(bf16[896,64]{1,0:T(8,128)(2,1)} %get-tuple-element.8.wb_ref, f32[896,1]{1,0:T(8,128)} %get-tuple-element.9.tot_ref, bf16[896,64]{1,0:T(8,128)(2,1)} %fusion.23.hit_ref, bf16[64,4096]{1,0:T(8,128)(2,1)} %bitcast.55), custom_call_target="tpu_custom_call" | custom-call | flops 939524096 | bytes 7340032 | tf_op jit(solution)/shard_map/pallas_call | solution.py:97
  (59 shorter events, 21.7 us)
Async XLA Ops:
  6.6 13.2 %all-to-all-start = ((s32[8,1,154]{2,1,0:T(1,128)}), s32[8,1,154]{2,1,0:T(1,128)S(1)}, u32[]{:S(2)}, u32[]{:S(2)}) async-start(s32[8,1,154]{2,1,0:T(1,128)} %copy.18), calls=%async_computation | async-start | bytes 16384 | tf_op jit(solution)/shard_map/all_to_all | solution.py:150
  19.8 35.2 %all-to-all-start.1 = ((bf16[8,154,1024]{2,1,0:T(8,128)(2,1)}), bf16[8,154,1024]{2,1,0:T(8,128)(2,1)}, u32[]{:S(2)}, u32[]{:S(2)}) async-start(bf16[8,154,1024]{2,1,0:T(8,128)(2,1)} %slice_select_fusion), calls=%async_computation.1 | async-start | bytes 5242880 | tf_op jit(solution)/shard_map/all_to_all | solution.py:149
  57.1 2.4 %copy-start.3 = (f32[1024]{0:T(1024)S(1)}, f32[1024]{0:T(1024)}, u32[]{:S(2)}) copy-start(f32[1024]{0:T(1024)} %param.13) | copy-start | bytes 12292
  59.4 13.2 %copy-start.2 = (s32[896]{0:T(1024)S(1)}, s32[896]{0:T(1024)}, u32[]{:S(2)}) copy-start(s32[896]{0:T(1024)} %param.15) | copy-start | bytes 10756
  67.6 18.9 %all-to-all-start.2 = ((bf16[8,16,4096]{2,1,0:T(8,128)(2,1)}), bf16[8,16,4096]{2,1,0:T(8,128)(2,1)S(1)}, u32[]{:S(2)}, u32[]{:S(2)}) async-start(bf16[8,16,4096]{2,1,0:T(8,128)(2,1)} %bitcast.16), calls=%async_computation.2 | async-start | bytes 2097152 | tf_op jit(solution)/shard_map/all_to_all | solution.py:181
  86.9 8.3 %collective-permute-start.2 = (bf16[16,4096]{1,0:T(8,128)(2,1)S(1)}, bf16[16,4096]{1,0:T(8,128)(2,1)S(1)}, u32[]{:S(2)}, u32[]{:S(2)}) collective-permute-start(bf16[16,4096]{1,0:T(8,128)(2,1)S(1)} %multiply_convert_fusion), channel_id=1, source_target_pairs={{0,3},{1,0},{2,1},{3,2},{4,7},{5,4},{6,5},{7,6},{8,11},{9,8},{10,9... | collective-permute-start | bytes 393224 | tf_op jit(solution)/shard_map/ppermute | solution.py:190
  87.4 12.6 %collective-permute-start.1 = (bf16[16,4096]{1,0:T(8,128)(2,1)S(1)}, bf16[16,4096]{1,0:T(8,128)(2,1)S(1)}, u32[]{:S(2)}, u32[]{:S(2)}) collective-permute-start(bf16[16,4096]{1,0:T(8,128)(2,1)S(1)} %multiply_convert_fusion), channel_id=1, source_target_pairs={{0,2},{1,3},{2,0},{3,1},{4,6},{5,7},{6,4},{7,5},{8,10},{9,11},{10,... | collective-permute-start | bytes 393224 | tf_op jit(solution)/shard_map/ppermute | solution.py:190
  87.7 12.2 %collective-permute-start = (bf16[16,4096]{1,0:T(8,128)(2,1)S(1)}, bf16[16,4096]{1,0:T(8,128)(2,1)S(1)}, u32[]{:S(2)}, u32[]{:S(2)}) collective-permute-start(bf16[16,4096]{1,0:T(8,128)(2,1)S(1)} %multiply_convert_fusion), channel_id=1, source_target_pairs={{0,1},{1,2},{2,3},{3,0},{4,5},{5,6},{6,7},{7,4},{8,9},{9,10},{10,1... | collective-permute-start | bytes 393224 | tf_op jit(solution)/shard_map/ppermute | solution.py:190
  113.8 29.4 %copy-start = (f32[64,4096]{1,0:T(8,128)S(1)}, f32[64,4096]{1,0:T(8,128)}, u32[]{:S(2)}) copy-start(f32[64,4096]{1,0:T(8,128)} %get-tuple-element.10) | copy-start | bytes 3145732
  113.9 33.8 %copy-start.1 = (f32[896,1]{1,0:T(8,128)S(1)}, f32[896,1]{1,0:T(8,128)}, u32[]{:S(2)}) copy-start(f32[896,1]{1,0:T(8,128)} %get-tuple-element.7) | copy-start | bytes 10756
  115.1 10.1 %collective-permute-start.3 = (f32[16,4096]{1,0:T(8,128)S(1)}, f32[16,4096]{1,0:T(8,128)S(1)}, u32[]{:S(2)}, u32[]{:S(2)}) collective-permute-start(f32[16,4096]{1,0:T(8,128)S(1)} %get-tuple-element.18), channel_id=1, source_target_pairs={{0,1},{1,2},{2,3},{4,5},{5,6},{6,7},{8,9},{9,10},{10,11},{12,13},{... | collective-permute-start | bytes 786440 | tf_op jit(solution)/shard_map/ppermute | solution.py:125
  116.4 11.1 %collective-permute-start.6 = (f32[16,4096]{1,0:T(8,128)S(1)}, f32[16,4096]{1,0:T(8,128)S(1)}, u32[]{:S(2)}, u32[]{:S(2)}) collective-permute-start(f32[16,4096]{1,0:T(8,128)S(1)} %get-tuple-element.19), channel_id=1, source_target_pairs={{1,0},{2,1},{3,2},{5,4},{6,5},{7,6},{9,8},{10,9},{11,10},{13,12},{... | collective-permute-start | bytes 786440 | tf_op jit(solution)/shard_map/ppermute | solution.py:126
  126.2 8.7 %collective-permute-start.4 = (f32[16,4096]{1,0:T(8,128)S(1)}, f32[16,4096]{1,0:T(8,128)S(1)}, u32[]{:S(2)}, u32[]{:S(2)}) collective-permute-start(f32[16,4096]{1,0:T(8,128)S(1)} %bitcast_add_fusion.2), channel_id=1, source_target_pairs={{0,1},{1,2},{2,3},{4,5},{5,6},{6,7},{8,9},{9,10},{10,11},{12,13},{... | collective-permute-start | bytes 786440 | tf_op jit(solution)/shard_map/ppermute | solution.py:125
  136.0 7.2 %collective-permute-start.7 = (f32[16,4096]{1,0:T(8,128)S(1)}, f32[16,4096]{1,0:T(8,128)S(1)}, u32[]{:S(2)}, u32[]{:S(2)}) collective-permute-start(f32[16,4096]{1,0:T(8,128)S(1)} %get-tuple-element.17), channel_id=1, source_target_pairs={{1,0},{2,1},{3,2},{5,4},{6,5},{7,6},{9,8},{10,9},{11,10},{13,12},{... | collective-permute-start | bytes 786440 | tf_op jit(solution)/shard_map/ppermute | solution.py:126
  139.4 17.1 %collective-permute-start.5 = (f32[16,4096]{1,0:T(8,128)S(1)}, f32[16,4096]{1,0:T(8,128)S(1)}, u32[]{:S(2)}, u32[]{:S(2)}) collective-permute-start(f32[16,4096]{1,0:T(8,128)S(1)} %get-tuple-element.16), channel_id=1, source_target_pairs={{0,1},{1,2},{2,3},{4,5},{5,6},{6,7},{8,9},{9,10},{10,11},{12,13},{... | collective-permute-start | bytes 786440 | tf_op jit(solution)/shard_map/ppermute | solution.py:125
  143.3 13.2 %collective-permute-start.8 = (f32[16,4096]{1,0:T(8,128)S(1)}, f32[16,4096]{1,0:T(8,128)S(1)}, u32[]{:S(2)}, u32[]{:S(2)}) collective-permute-start(f32[16,4096]{1,0:T(8,128)S(1)} %bitcast_add_fusion.1), channel_id=1, source_target_pairs={{1,0},{2,1},{3,2},{5,4},{6,5},{7,6},{9,8},{10,9},{11,10},{13,12},{... | collective-permute-start | bytes 786440 | tf_op jit(solution)/shard_map/ppermute | solution.py:126

commit v7 on v5

--- a/solution.py
+++ b/solution.py
@@ -36,10 +36,7 @@
     def _():
         gd_ref[...] = jnp.zeros_like(gd_ref)
 
-    widened = q_ref[...].astype(jnp.float32)
-    query_unit = (
-        widened * lax.rsqrt(jnp.sum(widened * widened, axis=-1, keepdims=True) + epsilon)
-    ).astype(jnp.bfloat16)
+    query_unit = q_ref[...]
     logits = logit_scale * contract_rows(query_unit, d_ref[...])
     weights = jnp.exp(logits)
     totals = jnp.sum(weights, axis=1, keepdims=True)
@@ -167,6 +164,7 @@
     pooled = jnp.sum(returned.astype(jnp.float32), axis=0)
 
     doc_unit = unit_rows(pooled)
+    query_unit = unit_rows(queries)
     cycle_size = lax.axis_size("blk")
     position = lax.axis_index("blk")
     arrived = jnp.stack(
@@ -182,7 +180,7 @@
     hits = (positives[:, None] == jnp.arange(piece_rows, dtype=jnp.int32)[None, :]).astype(
         jnp.bfloat16
     )
-    loss_col, weights, totals, grad_part = scores(queries, doc_piece, hits)
+    loss_col, weights, totals, grad_part = scores(query_unit, doc_piece, hits)
     grad_docs = lax.psum_scatter(grad_part, "blk", scatter_dimension=0, tiled=True)
     grad_queries = query_grads(weights, totals, hits, doc_piece)
     loss_rows = loss_col.reshape(loss_col.shape[0])

time: 158 us -> 160 us (1.013)
  other arithmetic: 16.6 us -> 30.3 us
  waiting for transfers between devices: 60.4 us -> 51.5 us
  local copies, waits for them, and re-layouts: 17.2 us -> 15.4 us
  Pallas kernels: 20.5 us -> 18.8 us
    convert_element_type x2 -> x3, other arithmetic: 0.18 us -> 9.12 us  [unit_rows(): return (widened * lax.rsqrt(jnp.sum(widened * widened, axis=-1, keepdims=...]
    all_to_all x1, waiting for transfers between devices: 13 us -> 4.97 us  [on_device(): lax.all_to_all(partial, 'dp', split_axis=0, concat_axis=0, tiled=True)]
    reduce_sum x1 -> x2, other arithmetic: 0.15 us -> 4.87 us  [unit_rows(): jnp.sum(widened * widened, axis=-1, keepdims=True) + epsilon]
    reshape x1, local copies, waits for them, and re-layouts: 3.18 us -> 1.44 us  [on_device(): by_lane = spans.reshape(cycle, groups, hidden_width)]
    pallas_call x1, Pallas kernels: 12.4 us -> 10.8 us  [scores(): pl.pallas_call(score_kernel, grid=(rows // tile,), in_specs=[pl.BlockSpec...]
  transfers between devices with their start and end apart: 7 -> 7, of which waited for: 5 -> 5; matrix products, arithmetic and copies ran while one was open for 14% -> 22% of each run, Pallas kernels for 5% -> 5%
where the time goes in v7:
time: 160 us; the launch traced here: 157 us
  waiting for transfers between devices  51.5 us (32%)
  other arithmetic  30.3 us (19%)
  Pallas kernels  18.8 us (12%)
  starting transfers between devices  18.3 us (11%)
  local copies, waits for them, and re-layouts  15.4 us (10%)
  between operations  14.9 us (9%)
  matrix products  8.19 us (5%)
    all_to_all x1, waiting for transfers between devices, on_device(): lax.all_to_all(send_rows, 'dp', split_axis=0, concat_axis=0, tiled=True)  19.4 us
    reduce_scatter x1, waiting for transfers between devices, on_device(): lax.psum_scatter(grad_part, 'blk', scatter_dimension=0, tiled=True)  16.6 us
    pallas_call x1, Pallas kernels, scores(): pl.pallas_call(score_kernel, grid=(rows // tile,), in_specs=[pl.BlockSpec...  10.8 us
    ppermute x3, waiting for transfers between devices, on_device(): lax.ppermute(doc_unit, 'blk', [(i, (i + shift) % cycle_size) for i in ran...  10.5 us
    convert_element_type x3, other arithmetic, unit_rows(): return (widened * lax.rsqrt(jnp.sum(widened * widened, axis=-1, keepdims=...  9.12 us
    dot_general x1, matrix products, on_device(): partial = jnp.dot(selector, embedded, preferred_element_type=jnp.float32)  8.19 us
    pallas_call x1, Pallas kernels, query_grads(): pl.pallas_call(query_grad_kernel, grid=(rows // tile,), in_specs=[pl.Bloc...  8.05 us
    gather x3, other arithmetic, on_device(): slot_of = source_of * capacity + packed_index - starts[source_of]  5.06 us
  transfers between devices with their start and end apart: 7, of which 5 were waited for; matrix products, arithmetic and copies ran while one was open for 22% of the time, Pallas kernels for 5%

profile of v7, /device:TPU:2, one launch (start us, length us, event | category | flops | bytes accessed | tf_op | source)
XLA Modules:
  0.0 157.3 jit_solution(6185986841525264949)
XLA Ops:
  7.2 1.2 slice.9
  13.1 4.3 %all-to-all-start = ((s32[8,1,154]{2,1,0:T(1,128)}), s32[8,1,154]{2,1,0:T(1,128)S(1)}, u32[]{:S(2)}, u32[]{:S(2)}) async-start(s32[8,1,154]{2,1,0:T(1,128)} %copy.18), calls=%async_computation | async-start | bytes 16384 | tf_op jit(solution)/shard_map/all_to_all | solution.py:132
  17.4 4.7 %fusion = f32[896]{0:T(1024)S(1)} fusion(bf16[896,4096]{1,0:T(8,128)(2,1)} %param.14), kind=kLoop, calls=%fused_computation.7 | loop fusion | flops 11009152 | bytes 7343616 | tf_op jit(solution)/shard_map/reduce_sum | solution.py:18
  22.1 1.4 copy.19
  23.6 2.2 %gather_fusion.2 = bf16[8,160,1024]{2,1,0:T(8,128)(2,1)} fusion(bf16[160,8,1024]{2,0,1:T(8,128)(2,1)S(1)} %copy.19, s32[1024]{0:T(1024)S(1)} %pad_clamp_fusion.2), kind=kCustom, calls=%fused_computation.2 | custom fusion | bytes 5242912 | tf_op jit(solution)/shard_map/jit(_take)/gather | solution.py:125
  25.8 3.6 %slice_select_fusion = bf16[8,154,1024]{2,1,0:T(8,128)(2,1)} fusion(bf16[8,160,1024]{2,1,0:T(8,128)(2,1)} %gather_fusion.2, pred[8]{0:T(512)(128)(4,1)S(1)} %compare_and_fusion), kind=kLoop, calls=%fused_computation.21 | loop fusion | flops 1261568 | bytes 5046280 | tf_op jit(solution)/shard_map/jit(_take)/select_n | solution.py:125
  29.4 4.4 %all-to-all-start.1 = ((bf16[8,154,1024]{2,1,0:T(8,128)(2,1)}), bf16[8,154,1024]{2,1,0:T(8,128)(2,1)}, u32[]{:S(2)}, u32[]{:S(2)}) async-start(bf16[8,154,1024]{2,1,0:T(8,128)(2,1)} %slice_select_fusion), calls=%async_computation.1 | async-start | bytes 5242880 | tf_op jit(solution)/shard_map/all_to_all | solution.py:131
  36.5 4.4 %fusion.32 = (s32[320]{0:T(512)S(1)}, s32[320,1]{0,1:T(1,128)S(1)}) fusion(s32[]{:T(128)} %bitcast.7, s32[]{:T(128)} %bitcast.8, s32[]{:T(128)} %bitcast.9, s32[]{:T(128)} %bitcast.10, s32[]{:T(128)} %bitcast.11, s32[]{:T(128)} %bitcast.13, s32[]{:T(128)} %bitcast.12, s32[320]{0:T(512)S(1)} %get-tuple-element.17, s32[320]{0:T(512)S(1)} %get-tuple-element.16), kind=kLoop, calls=%fused_computation.78 | loop fusion | flops 4480 | bytes 5148 | tf_op jit(solution)/shard_map/gather | solution.py:140
  42.2 2.2 %gather_fusion.1 = s32[320]{0:T(512)S(1)} fusion(s32[1232]{0:T(1024)S(1)} %reshape.291, s32[1024]{0:T(1024)S(1)} %pad_clamp_fusion.1), kind=kCustom, calls=%fused_computation.1 | custom fusion | bytes 3840 | tf_op jit(solution)/shard_map/gather | solution.py:145
  45.2 19.4 %all-to-all-done.1 = bf16[8,154,1024]{2,1,0:T(8,128)(2,1)} async-done(((bf16[8,154,1024]{2,1,0:T(8,128)(2,1)}), bf16[8,154,1024]{2,1,0:T(8,128)(2,1)}, u32[]{:S(2)}, u32[]{:S(2)}) %all-to-all-start.1) | async-done | bytes 2523168 | tf_op jit(solution)/shard_map/all_to_all | solution.py:131
  64.5 2.1 %reshape.293 = bf16[1232,1024]{1,0:T(8,128)(2,1)S(1)} reshape(bf16[8,154,1024]{2,1,0:T(8,128)(2,1)} %all-to-all-done.1) | data formatting | bytes 5046272 | tf_op jit(solution)/shard_map/reshape | solution.py:143
  66.6 2.1 %gather_fusion.3 = bf16[320,1024]{1,0:T(8,128)(2,1)S(1)} fusion(bf16[1232,1024]{1,0:T(8,128)(2,1)S(1)} %reshape.293, s32[1024]{0:T(1024)S(1)} %pad_clamp_fusion.1), kind=kCustom, calls=%fused_computation.3 | custom fusion | bytes 1312000 | tf_op jit(solution)/shard_map/gather | solution.py:143
  68.9 8.2 %convolution_convert_fusion = bf16[128,4096]{1,0:T(8,128)(2,1)} fusion(bf16[1,1024,4096]{2,1,0:T(8,128)(2,1)} %param.12, bf16[320,1024]{1,0:T(8,128)(2,1)S(1)} %gather_fusion.3, f32[1024]{0:T(1024)S(1)} %copy-done.2, f32[320]{0:T(512)S(1)} %add_rsqrt_fusion.1, s32[320]{0:T(512)S(1)} %add_select_fusion), kind=kOutput, calls=%fused_computation.20 | convolution fusion | flops 3033571328 | bytes 10099200 | tf_op jit(solution)/shard_map/dot_general | solution.py:161
  77.1 5.0 %all-to-all-start.2 = ((bf16[8,16,4096]{2,1,0:T(8,128)(2,1)}), bf16[8,16,4096]{2,1,0:T(8,128)(2,1)S(1)}, u32[]{:S(2)}, u32[]{:S(2)}) async-start(bf16[8,16,4096]{2,1,0:T(8,128)(2,1)} %bitcast.16), calls=%async_computation.2 | async-start | bytes 2097152 | tf_op jit(solution)/shard_map/all_to_all | solution.py:163
  82.1 8.9 %fusion.1.q_ref = bf16[896,4096]{1,0:T(8,128)(2,1)} fusion(bf16[896,4096]{1,0:T(8,128)(2,1)} %param.14, f32[896]{0:T(1024)S(1)} %add_rsqrt_fusion), kind=kLoop, calls=%fused_computation.8 | loop fusion | flops 11010048 | bytes 14683648 | tf_op jit(solution)/shard_map/convert_element_type | solution.py:19
  91.1 5.0 %all-to-all-done.2 = bf16[8,16,4096]{2,1,0:T(8,128)(2,1)S(1)} async-done(((bf16[8,16,4096]{2,1,0:T(8,128)(2,1)}), bf16[8,16,4096]{2,1,0:T(8,128)(2,1)S(1)}, u32[]{:S(2)}, u32[]{:S(2)}) %all-to-all-start.2) | async-done | bytes 1048608 | tf_op jit(solution)/shard_map/all_to_all | solution.py:163
  96.4 3.7 %collective-permute-start.2 = (bf16[16,4096]{1,0:T(8,128)(2,1)S(1)}, bf16[16,4096]{1,0:T(8,128)(2,1)S(1)}, u32[]{:S(2)}, u32[]{:S(2)}) collective-permute-start(bf16[16,4096]{1,0:T(8,128)(2,1)S(1)} %multiply_convert_fusion), channel_id=1, source_target_pairs={{0,3},{1,0},{2,1},{3,2},{4,7},{5,4},{6,5},{7,6},{8,11},{9,8},{10,9... | collective-permute-start | bytes 393224 | tf_op jit(solution)/shard_map/ppermute | solution.py:173
  101.2 2.8 %collective-permute-done.2 = bf16[16,4096]{1,0:T(8,128)(2,1)S(1)} collective-permute-done((bf16[16,4096]{1,0:T(8,128)(2,1)S(1)}, bf16[16,4096]{1,0:T(8,128)(2,1)S(1)}, u32[]{:S(2)}, u32[]{:S(2)}) %collective-permute-start.2) | collective-permute-done | bytes 131104 | tf_op jit(solution)/shard_map/ppermute | solution.py:173
  104.0 7.6 %collective-permute-done.1 = bf16[16,4096]{1,0:T(8,128)(2,1)S(1)} collective-permute-done((bf16[16,4096]{1,0:T(8,128)(2,1)S(1)}, bf16[16,4096]{1,0:T(8,128)(2,1)S(1)}, u32[]{:S(2)}, u32[]{:S(2)}) %collective-permute-start.1) | collective-permute-done | bytes 131104 | tf_op jit(solution)/shard_map/ppermute | solution.py:173
  111.7 1.4 gather_fusion.4
  113.1 10.8 %shard_map.103 = (f32[896,1]{1,0:T(8,128)}, bf16[896,64]{1,0:T(8,128)(2,1)}, f32[896,1]{1,0:T(8,128)}, f32[64,4096]{1,0:T(8,128)}) custom-call(bf16[896,4096]{1,0:T(8,128)(2,1)} %fusion.1.q_ref, bf16[64,4096]{1,0:T(8,128)(2,1)} %bitcast.37, bf16[896,64]{1,0:T(8,128)(2,1)} %fusion.25.hit_ref), custom_call_target="tpu_custom_call" | custom-call | flops 939524096 | bytes 7340032 | tf_op jit(solution)/shard_map/pallas_call | solution.py:64
  123.9 1.8 %reduce.7 = f32[896]{0:T(1024)} reduce(f32[896,1]{1,0:T(8,128)} %get-tuple-element.7, f32[]{:T(128)} %constant.113), dimensions={1}, to_apply=%get-tuple-element.7.reduce_sub_computation | reduce | bytes 7172 | tf_op jit(solution)/shard_map/pallas_call | solution.py:64
  125.8 8.0 %shard_map.104 = bf16[896,4096]{1,0:T(8,128)(2,1)} custom-call(bf16[896,64]{1,0:T(8,128)(2,1)} %get-tuple-element.8.wb_ref, f32[896,1]{1,0:T(8,128)} %get-tuple-element.9.tot_ref, bf16[896,64]{1,0:T(8,128)(2,1)} %fusion.25.hit_ref, bf16[64,4096]{1,0:T(8,128)(2,1)} %bitcast.38), custom_call_target="tpu_custom_call" | custom-call | flops 939524096 | bytes 7340032 | tf_op jit(solution)/shard_map/pallas_call | solution.py:94
  133.8 16.6 %reduce-scatter.2.cloned.1.call-done = f32[16,4096]{1,0:T(8,128)} async-done(((f32[64,4096]{1,0:T(8,128)}), f32[16,4096]{1,0:T(8,128)}) %reduce-scatter.2.cloned.1.call-update) | async-done | bytes 262160 | tf_op jit(solution)/shard_map/reduce_scatter | solution.py:184
  (46 shorter events, 10.6 us)
Async XLA Ops:
  13.1 16.2 %all-to-all-start = ((s32[8,1,154]{2,1,0:T(1,128)}), s32[8,1,154]{2,1,0:T(1,128)S(1)}, u32[]{:S(2)}, u32[]{:S(2)}) async-start(s32[8,1,154]{2,1,0:T(1,128)} %copy.18), calls=%async_computation | async-start | bytes 16384 | tf_op jit(solution)/shard_map/all_to_all | solution.py:132
  17.4 4.7 %copy-start = (bf16[1280,1024]{1,0:T(8,128)(2,1)S(1)}, bf16[1280,1024]{1,0:T(8,128)(2,1)}, u32[]{:S(2)}) copy-start(bf16[1280,1024]{1,0:T(8,128)(2,1)} %param.8) | copy-start | bytes 7864324
  25.8 8.0 %copy-start.1 = (s32[896]{0:T(1024)S(1)}, s32[896]{0:T(1024)}, u32[]{:S(2)}) copy-start(s32[896]{0:T(1024)} %param.15) | copy-start | bytes 10756
  29.4 35.2 %all-to-all-start.1 = ((bf16[8,154,1024]{2,1,0:T(8,128)(2,1)}), bf16[8,154,1024]{2,1,0:T(8,128)(2,1)}, u32[]{:S(2)}, u32[]{:S(2)}) async-start(bf16[8,154,1024]{2,1,0:T(8,128)(2,1)} %slice_select_fusion), calls=%async_computation.1 | async-start | bytes 5242880 | tf_op jit(solution)/shard_map/all_to_all | solution.py:131
  45.1 23.8 %copy-start.2 = (f32[1024]{0:T(1024)S(1)}, f32[1024]{0:T(1024)}, u32[]{:S(2)}) copy-start(f32[1024]{0:T(1024)} %param.13) | copy-start | bytes 12292
  77.1 18.9 %all-to-all-start.2 = ((bf16[8,16,4096]{2,1,0:T(8,128)(2,1)}), bf16[8,16,4096]{2,1,0:T(8,128)(2,1)S(1)}, u32[]{:S(2)}, u32[]{:S(2)}) async-start(bf16[8,16,4096]{2,1,0:T(8,128)(2,1)} %bitcast.16), calls=%async_computation.2 | async-start | bytes 2097152 | tf_op jit(solution)/shard_map/all_to_all | solution.py:163
  82.1 68.3 %reduce-scatter.2.cloned.1.call-start = ((), (), s32[]{:S(2)}) async-start(), calls=%async_computation.4 | async-start | bytes 1310720 | tf_op jit(solution)/shard_map/reduce_scatter | solution.py:184
  96.4 7.6 %collective-permute-start.2 = (bf16[16,4096]{1,0:T(8,128)(2,1)S(1)}, bf16[16,4096]{1,0:T(8,128)(2,1)S(1)}, u32[]{:S(2)}, u32[]{:S(2)}) collective-permute-start(bf16[16,4096]{1,0:T(8,128)(2,1)S(1)} %multiply_convert_fusion), channel_id=1, source_target_pairs={{0,3},{1,0},{2,1},{3,2},{4,7},{5,4},{6,5},{7,6},{8,11},{9,8},{10,9... | collective-permute-start | bytes 393224 | tf_op jit(solution)/shard_map/ppermute | solution.py:173
  100.1 11.6 %collective-permute-start.1 = (bf16[16,4096]{1,0:T(8,128)(2,1)S(1)}, bf16[16,4096]{1,0:T(8,128)(2,1)S(1)}, u32[]{:S(2)}, u32[]{:S(2)}) collective-permute-start(bf16[16,4096]{1,0:T(8,128)(2,1)S(1)} %multiply_convert_fusion), channel_id=1, source_target_pairs={{0,2},{1,3},{2,0},{3,1},{4,6},{5,7},{6,4},{7,5},{8,10},{9,11},{10,... | collective-permute-start | bytes 393224 | tf_op jit(solution)/shard_map/ppermute | solution.py:173
  100.1 11.6 %collective-permute-start = (bf16[16,4096]{1,0:T(8,128)(2,1)S(1)}, bf16[16,4096]{1,0:T(8,128)(2,1)S(1)}, u32[]{:S(2)}, u32[]{:S(2)}) collective-permute-start(bf16[16,4096]{1,0:T(8,128)(2,1)S(1)} %multiply_convert_fusion), channel_id=1, source_target_pairs={{0,1},{1,2},{2,3},{3,0},{4,5},{5,6},{6,7},{7,4},{8,9},{9,10},{10,1... | collective-permute-start | bytes 393224 | tf_op jit(solution)/shard_map/ppermute | solution.py:173
Sparse Core Ops, SparseCore 0:
  124.0 26.3 reduce-scatter.1

commit v8 on v7

--- a/solution.py
+++ b/solution.py
@@ -117,18 +117,23 @@
     groups = lax.axis_size("dp")
     capacity = (rows_dev - 3 * SESS_DEV) // groups
     received = rows_dev // 4
-    cycle = rows_dev // groups
     count = span_counts[0]
 
     lane_of = (jnp.arange(groups, dtype=jnp.int32) - destinations[0]) % groups
-    by_lane = spans.reshape(cycle, groups, hidden_width)
-    send_rows = jnp.swapaxes(jnp.take(by_lane, lane_of, axis=1), 0, 1)[:, :capacity]
     row_of = lane_of[:, None] + groups * jnp.arange(capacity, dtype=jnp.int32)[None, :]
-    ids_by_lane = session_ids.reshape(cycle, groups)
-    send_ids = jnp.where(
-        row_of < count, jnp.swapaxes(jnp.take(ids_by_lane, lane_of, axis=1), 0, 1)[:, :capacity], -1
+    row_of = jnp.where(row_of < count, row_of, -1).reshape(groups * capacity)
+    picker = (row_of[:, None] == jnp.arange(rows_dev, dtype=jnp.int32)[None, :]).astype(jnp.bfloat16)
+    send_rows = (
+        jnp.dot(picker, spans, preferred_element_type=jnp.float32)
+        .astype(jnp.bfloat16)
+        .reshape(groups, capacity, hidden_width)
+    )
+    send_ids = jnp.where(row_of >= 0, session_ids[jnp.maximum(row_of, 0)], -1).reshape(
+        groups, capacity
     )
     got_rows = lax.all_to_all(send_rows, "dp", split_axis=0, concat_axis=0, tiled=True)
+    query_unit = unit_rows(queries)
+    got_rows, query_unit = lax.optimization_barrier((got_rows, query_unit))
     got_ids = lax.all_to_all(send_ids, "dp", split_axis=0, concat_axis=0, tiled=True)
 
     got_counts = jnp.sum((got_ids >= 0).astype(jnp.int32), axis=1)
@@ -164,7 +169,6 @@
     pooled = jnp.sum(returned.astype(jnp.float32), axis=0)
 
     doc_unit = unit_rows(pooled)
-    query_unit = unit_rows(queries)
     cycle_size = lax.axis_size("blk")
     position = lax.axis_index("blk")
     arrived = jnp.stack(

time: 160 us -> 172 us (1.075)
  local copies, waits for them, and re-layouts: 15.4 us -> 24.2 us
  matrix products: 8.19 us -> 13.1 us
  other arithmetic: 30.3 us -> 27.1 us
    all_to_all x1, waiting for transfers between devices: 4.97 us -> 13.1 us  [on_device(): lax.all_to_all(partial, 'dp', split_axis=0, concat_axis=0, tiled=True)]
    all_to_all x1, waiting for transfers between devices: 19.4 us -> 11.4 us  [on_device(): lax.all_to_all(send_rows, 'dp', split_axis=0, concat_axis=0, tiled=True)]
    dot_general x0 -> x1, matrix products: none -> 4.89 us  [on_device(): jnp.dot(picker, spans, preferred_element_type=jnp.float32)]
    gather x2, local copies, waits for them, and re-layouts: 2.78 us -> 7.17 us  [on_device(): session_ids[jnp.maximum(row_of, 0)]]
    select_n x2, other arithmetic: 4.26 us -> 0.69 us  [the longest x1 0.68 us: on_device(): jnp.where(row_of >= 0, session_ids[jnp.maximum(row_of, 0)], -1)]
    gather x1, local copies, waits for them, and re-layouts: 2.09 us -> 4.82 us  [on_device(): packed = got_rows.reshape(groups * capacity, hidden_width)[slot_of]]
  transfers between devices with their start and end apart: 7 -> 7, of which waited for: 5 -> 5; matrix products, arithmetic and copies ran while one was open for 22% -> 21% of each run, Pallas kernels for 5% -> 5%
where the time goes in v8:
time: 172 us; the launch traced here: 169 us
  waiting for transfers between devices  51.6 us (30%)
  other arithmetic  27.1 us (16%)
  local copies, waits for them, and re-layouts  24.2 us (14%)
  starting transfers between devices  19.1 us (11%)
  Pallas kernels  18.8 us (11%)
  between operations  14.9 us (9%)
  matrix products  13.1 us (8%)
    reduce_scatter x1, waiting for transfers between devices, on_device(): lax.psum_scatter(grad_part, 'blk', scatter_dimension=0, tiled=True)  16.6 us
    all_to_all x1, waiting for transfers between devices, on_device(): lax.all_to_all(partial, 'dp', split_axis=0, concat_axis=0, tiled=True)  13.1 us
    all_to_all x1, waiting for transfers between devices, on_device(): lax.all_to_all(send_rows, 'dp', split_axis=0, concat_axis=0, tiled=True)  11.4 us
    pallas_call x1, Pallas kernels, scores(): pl.pallas_call(score_kernel, grid=(rows // tile,), in_specs=[pl.BlockSpec...  10.8 us
    ppermute x3, waiting for transfers between devices, on_device(): lax.ppermute(doc_unit, 'blk', [(i, (i + shift) % cycle_size) for i in ran...  10.5 us
    convert_element_type x3, other arithmetic, unit_rows(): return (widened * lax.rsqrt(jnp.sum(widened * widened, axis=-1, keepdims=...  9.12 us
    dot_general x1, matrix products, on_device(): partial = jnp.dot(selector, embedded, preferred_element_type=jnp.float32)  8.24 us
    pallas_call x1, Pallas kernels, query_grads(): pl.pallas_call(query_grad_kernel, grid=(rows // tile,), in_specs=[pl.Bloc...  8.05 us
  transfers between devices with their start and end apart: 7, of which 5 were waited for; matrix products, arithmetic and copies ran while one was open for 21% of the time, Pallas kernels for 5%

profile of v8, /device:TPU:2, one launch (start us, length us, event | category | flops | bytes accessed | tf_op | source)
XLA Modules:
  0.0 168.9 jit_solution(8892173111066275041)
XLA Ops:
  10.1 7.1 %gather_fusion = s32[1232]{0:T(1024)S(1)} fusion(s32[1280]{0:T(1024)S(1)} %copy-done.1, s32[2048]{0:T(1024)S(1)} %pad_clamp_fusion), kind=kCustom, calls=%fused_computation | custom fusion | bytes 14784 | tf_op jit(solution)/shard_map/gather | solution.py:131
  17.9 4.3 %all-to-all-start.1 = ((s32[8,1,154]{2,1,0:T(1,128)}), s32[8,1,154]{2,1,0:T(1,128)S(1)}, u32[]{:S(2)}, u32[]{:S(2)}) async-start(s32[8,1,154]{2,1,0:T(1,128)} %compare_select_fusion.1), calls=%async_computation.1 | async-start | bytes 16384 | tf_op jit(solution)/shard_map/all_to_all | solution.py:137
  22.3 4.6 %fusion = f32[896]{0:T(1024)S(1)} fusion(bf16[896,4096]{1,0:T(8,128)(2,1)} %param.14), kind=kLoop, calls=%fused_computation.6 | loop fusion | flops 11009152 | bytes 7343616 | tf_op jit(solution)/shard_map/reduce_sum | solution.py:18
  26.9 4.9 %fusion.15 = bf16[1232,1024]{1,0:T(8,128)(2,1)} fusion(bf16[1280,1024]{1,0:T(8,128)(2,1)S(1)} %copy-done, s32[1232]{0:T(1024)S(1)} %compare_select_fusion.3), kind=kOutput, calls=%fused_computation.22 | convolution fusion | flops 3232452608 | bytes 5149504 | tf_op jit(solution)/shard_map/dot_general | solution.py:127
  31.8 3.2 %reshape.345 = bf16[8,154,1024]{2,1,0:T(8,128)(2,1)} reshape(bf16[1232,1024]{1,0:T(8,128)(2,1)} %fusion.15) | data formatting | bytes 5046272 | tf_op jit(solution)/shard_map/reshape | solution.py:129
  34.9 4.5 %all-to-all-start = ((bf16[8,154,1024]{2,1,0:T(8,128)(2,1)}), bf16[8,154,1024]{2,1,0:T(8,128)(2,1)}, u32[]{:S(2)}, u32[]{:S(2)}) async-start(bf16[8,154,1024]{2,1,0:T(8,128)(2,1)} %reshape.345), calls=%async_computation | async-start | bytes 5242880 | tf_op jit(solution)/shard_map/all_to_all | solution.py:134
  39.5 8.9 %fusion.1.q_ref = bf16[896,4096]{1,0:T(8,128)(2,1)} fusion(bf16[896,4096]{1,0:T(8,128)(2,1)} %param.14, f32[896]{0:T(1024)S(1)} %add_rsqrt_fusion), kind=kLoop, calls=%fused_computation.7 | loop fusion | flops 11010048 | bytes 14683648 | tf_op jit(solution)/shard_map/convert_element_type | solution.py:19
  50.3 4.3 %fusion.35 = (s32[320]{0:T(512)S(1)}, s32[320,1]{0,1:T(1,128)S(1)}) fusion(s32[]{:T(128)} %bitcast.5, s32[]{:T(128)} %bitcast.6, s32[]{:T(128)} %bitcast.7, s32[]{:T(128)} %bitcast.8, s32[]{:T(128)} %bitcast.9, s32[]{:T(128)} %bitcast.11, s32[]{:T(128)} %bitcast.10, s32[320]{0:T(512)S(1)} %get-tuple-element.21, s32[320]{0:T(512)S(1)} %get-tuple-element.20), kind=kLoop, calls=%fused_computation.77 | loop fusion | flops 4480 | bytes 5148 | tf_op jit(solution)/shard_map/gather | solution.py:145
  56.0 2.2 %gather_fusion.1 = s32[320]{0:T(512)S(1)} fusion(s32[1232]{0:T(1024)S(1)} %reshape.348, s32[1024]{0:T(1024)S(1)} %pad_clamp_fusion.2), kind=kCustom, calls=%fused_computation.1 | custom fusion | bytes 3840 | tf_op jit(solution)/shard_map/gather | solution.py:150
  58.9 11.4 %all-to-all-done = bf16[8,154,1024]{2,1,0:T(8,128)(2,1)} async-done(((bf16[8,154,1024]{2,1,0:T(8,128)(2,1)}), bf16[8,154,1024]{2,1,0:T(8,128)(2,1)}, u32[]{:S(2)}, u32[]{:S(2)}) %all-to-all-start) | async-done | bytes 2523168 | tf_op jit(solution)/shard_map/all_to_all | solution.py:134
  70.3 3.1 %reshape.349 = bf16[1232,1024]{1,0:T(8,128)(2,1)} reshape(bf16[8,154,1024]{2,1,0:T(8,128)(2,1)} %all-to-all-done) | data formatting | bytes 5046272 | tf_op jit(solution)/shard_map/reshape | solution.py:148
  73.4 4.8 %gather_fusion.2 = bf16[320,1024]{1,0:T(8,128)(2,1)S(1)} fusion(bf16[1232,1024]{1,0:T(8,128)(2,1)} %reshape.349, s32[1024]{0:T(1024)S(1)} %pad_clamp_fusion.2), kind=kCustom, calls=%fused_computation.2 | custom fusion | bytes 1312000 | tf_op jit(solution)/shard_map/gather | solution.py:148
  78.5 8.2 %convolution_convert_fusion = bf16[128,4096]{1,0:T(8,128)(2,1)} fusion(bf16[1,1024,4096]{2,1,0:T(8,128)(2,1)} %param.12, bf16[320,1024]{1,0:T(8,128)(2,1)S(1)} %gather_fusion.2, f32[1024]{0:T(1024)S(1)} %copy-done.3, f32[320]{0:T(512)S(1)} %add_rsqrt_fusion.1, s32[320]{0:T(512)S(1)} %add_select_fusion), kind=kOutput, calls=%fused_computation.21 | convolution fusion | flops 3033571328 | bytes 10099200 | tf_op jit(solution)/shard_map/dot_general | solution.py:166
  86.7 5.6 %all-to-all-start.2 = ((bf16[8,16,4096]{2,1,0:T(8,128)(2,1)}), bf16[8,16,4096]{2,1,0:T(8,128)(2,1)}, u32[]{:S(2)}, u32[]{:S(2)}) async-start(bf16[8,16,4096]{2,1,0:T(8,128)(2,1)} %bitcast.37), calls=%async_computation.2 | async-start | bytes 2097152 | tf_op jit(solution)/shard_map/all_to_all | solution.py:168
  93.3 13.1 %all-to-all-done.2 = bf16[8,16,4096]{2,1,0:T(8,128)(2,1)} async-done(((bf16[8,16,4096]{2,1,0:T(8,128)(2,1)}), bf16[8,16,4096]{2,1,0:T(8,128)(2,1)}, u32[]{:S(2)}, u32[]{:S(2)}) %all-to-all-start.2) | async-done | bytes 1048608 | tf_op jit(solution)/shard_map/all_to_all | solution.py:168
  106.4 1.4 convert_reduce_fusion
  108.0 3.7 %collective-permute-start.2 = (bf16[16,4096]{1,0:T(8,128)(2,1)S(1)}, bf16[16,4096]{1,0:T(8,128)(2,1)S(1)}, u32[]{:S(2)}, u32[]{:S(2)}) collective-permute-start(bf16[16,4096]{1,0:T(8,128)(2,1)S(1)} %multiply_convert_fusion), channel_id=1, source_target_pairs={{0,3},{1,0},{2,1},{3,2},{4,7},{5,4},{6,5},{7,6},{8,11},{9,8},{10,9... | collective-permute-start | bytes 393224 | tf_op jit(solution)/shard_map/ppermute | solution.py:177
  112.8 2.8 %collective-permute-done.2 = bf16[16,4096]{1,0:T(8,128)(2,1)S(1)} collective-permute-done((bf16[16,4096]{1,0:T(8,128)(2,1)S(1)}, bf16[16,4096]{1,0:T(8,128)(2,1)S(1)}, u32[]{:S(2)}, u32[]{:S(2)}) %collective-permute-start.2) | collective-permute-done | bytes 131104 | tf_op jit(solution)/shard_map/ppermute | solution.py:177
  115.6 7.6 %collective-permute-done.1 = bf16[16,4096]{1,0:T(8,128)(2,1)S(1)} collective-permute-done((bf16[16,4096]{1,0:T(8,128)(2,1)S(1)}, bf16[16,4096]{1,0:T(8,128)(2,1)S(1)}, u32[]{:S(2)}, u32[]{:S(2)}) %collective-permute-start.1) | collective-permute-done | bytes 131104 | tf_op jit(solution)/shard_map/ppermute | solution.py:177
  123.3 1.4 gather_fusion.3
  124.7 10.8 %shard_map.103 = (f32[896,1]{1,0:T(8,128)}, bf16[896,64]{1,0:T(8,128)(2,1)}, f32[896,1]{1,0:T(8,128)}, f32[64,4096]{1,0:T(8,128)}) custom-call(bf16[896,4096]{1,0:T(8,128)(2,1)} %fusion.1.q_ref, bf16[64,4096]{1,0:T(8,128)(2,1)} %bitcast.35, bf16[896,64]{1,0:T(8,128)(2,1)} %fusion.28.hit_ref), custom_call_target="tpu_custom_call" | custom-call | flops 939524096 | bytes 7340032 | tf_op jit(solution)/shard_map/pallas_call | solution.py:64
  135.5 1.8 %reduce.8 = f32[896]{0:T(1024)} reduce(f32[896,1]{1,0:T(8,128)} %get-tuple-element.11, f32[]{:T(128)} %constant.89), dimensions={1}, to_apply=%get-tuple-element.11.reduce_sub_computation | reduce | bytes 7172 | tf_op jit(solution)/shard_map/pallas_call | solution.py:64
  137.4 8.0 %shard_map.104 = bf16[896,4096]{1,0:T(8,128)(2,1)} custom-call(bf16[896,64]{1,0:T(8,128)(2,1)} %get-tuple-element.12.wb_ref, f32[896,1]{1,0:T(8,128)} %get-tuple-element.13.tot_ref, bf16[896,64]{1,0:T(8,128)(2,1)} %fusion.28.hit_ref, bf16[64,4096]{1,0:T(8,128)(2,1)} %bitcast.36), custom_call_target="tpu_custom_call" | custom-call | flops 939524096 | bytes 7340032 | tf_op jit(solution)/shard_map/pallas_call | solution.py:94
  145.4 16.6 %reduce-scatter.2.cloned.1.call-done = f32[16,4096]{1,0:T(8,128)} async-done(((f32[64,4096]{1,0:T(8,128)}), f32[16,4096]{1,0:T(8,128)}) %reduce-scatter.2.cloned.1.call-update) | async-done | bytes 262160 | tf_op jit(solution)/shard_map/reduce_scatter | solution.py:188
  (48 shorter events, 9.5 us)
Async XLA Ops:
  7.2 19.7 %copy-start = (bf16[1280,1024]{1,0:T(8,128)(2,1)S(1)}, bf16[1280,1024]{1,0:T(8,128)(2,1)}, u32[]{:S(2)}) copy-start(bf16[1280,1024]{1,0:T(8,128)(2,1)} %param.8) | copy-start | bytes 7864324
  7.2 2.9 %copy-start.1 = (s32[1280]{0:T(1024)S(1)}, s32[1280]{0:T(1024)}, u32[]{:S(2)}) copy-start(s32[1280]{0:T(1024)} %param.10) | copy-start | bytes 15364
  17.9 17.0 %all-to-all-start.1 = ((s32[8,1,154]{2,1,0:T(1,128)}), s32[8,1,154]{2,1,0:T(1,128)S(1)}, u32[]{:S(2)}, u32[]{:S(2)}) async-start(s32[8,1,154]{2,1,0:T(1,128)} %compare_select_fusion.1), calls=%async_computation.1 | async-start | bytes 16384 | tf_op jit(solution)/shard_map/all_to_all | solution.py:137
  34.9 35.3 %all-to-all-start = ((bf16[8,154,1024]{2,1,0:T(8,128)(2,1)}), bf16[8,154,1024]{2,1,0:T(8,128)(2,1)}, u32[]{:S(2)}, u32[]{:S(2)}) async-start(bf16[8,154,1024]{2,1,0:T(8,128)(2,1)} %reshape.345), calls=%async_computation | async-start | bytes 5242880 | tf_op jit(solution)/shard_map/all_to_all | solution.py:134
  58.9 19.6 %copy-start.3 = (f32[1024]{0:T(1024)S(1)}, f32[1024]{0:T(1024)}, u32[]{:S(2)}) copy-start(f32[1024]{0:T(1024)} %param.13) | copy-start | bytes 12292
  78.5 13.9 %copy-start.2 = (s32[896]{0:T(1024)S(1)}, s32[896]{0:T(1024)}, u32[]{:S(2)}) copy-start(s32[896]{0:T(1024)} %param.15) | copy-start | bytes 10756
  86.7 19.6 %all-to-all-start.2 = ((bf16[8,16,4096]{2,1,0:T(8,128)(2,1)}), bf16[8,16,4096]{2,1,0:T(8,128)(2,1)}, u32[]{:S(2)}, u32[]{:S(2)}) async-start(bf16[8,16,4096]{2,1,0:T(8,128)(2,1)} %bitcast.37), calls=%async_computation.2 | async-start | bytes 2097152 | tf_op jit(solution)/shard_map/all_to_all | solution.py:168
  92.4 69.6 %reduce-scatter.2.cloned.1.call-start = ((), (), s32[]{:S(2)}) async-start(), calls=%async_computation.4 | async-start | bytes 1310720 | tf_op jit(solution)/shard_map/reduce_scatter | solution.py:188
  108.0 7.6 %collective-permute-start.2 = (bf16[16,4096]{1,0:T(8,128)(2,1)S(1)}, bf16[16,4096]{1,0:T(8,128)(2,1)S(1)}, u32[]{:S(2)}, u32[]{:S(2)}) collective-permute-start(bf16[16,4096]{1,0:T(8,128)(2,1)S(1)} %multiply_convert_fusion), channel_id=1, source_target_pairs={{0,3},{1,0},{2,1},{3,2},{4,7},{5,4},{6,5},{7,6},{8,11},{9,8},{10,9... | collective-permute-start | bytes 393224 | tf_op jit(solution)/shard_map/ppermute | solution.py:177
  111.7 11.6 %collective-permute-start.1 = (bf16[16,4096]{1,0:T(8,128)(2,1)S(1)}, bf16[16,4096]{1,0:T(8,128)(2,1)S(1)}, u32[]{:S(2)}, u32[]{:S(2)}) collective-permute-start(bf16[16,4096]{1,0:T(8,128)(2,1)S(1)} %multiply_convert_fusion), channel_id=1, source_target_pairs={{0,2},{1,3},{2,0},{3,1},{4,6},{5,7},{6,4},{7,5},{8,10},{9,11},{10,... | collective-permute-start | bytes 393224 | tf_op jit(solution)/shard_map/ppermute | solution.py:177
  111.7 11.6 %collective-permute-start = (bf16[16,4096]{1,0:T(8,128)(2,1)S(1)}, bf16[16,4096]{1,0:T(8,128)(2,1)S(1)}, u32[]{:S(2)}, u32[]{:S(2)}) collective-permute-start(bf16[16,4096]{1,0:T(8,128)(2,1)S(1)} %multiply_convert_fusion), channel_id=1, source_target_pairs={{0,1},{1,2},{2,3},{3,0},{4,5},{5,6},{6,7},{7,4},{8,9},{9,10},{10,1... | collective-permute-start | bytes 393224 | tf_op jit(solution)/shard_map/ppermute | solution.py:177
Sparse Core Ops, SparseCore 0:
  135.7 26.3 reduce-scatter.1

commit v9 on v5

--- a/solution.py
+++ b/solution.py
@@ -183,7 +183,14 @@
         jnp.bfloat16
     )
     loss_col, weights, totals, grad_part = scores(queries, doc_piece, hits)
-    grad_docs = lax.psum_scatter(grad_part, "blk", scatter_dimension=0, tiled=True)
+    grad_terms = lax.all_to_all(
+        grad_part.astype(jnp.bfloat16).reshape(cycle_size, doc_unit.shape[0], emb_width),
+        "blk",
+        split_axis=0,
+        concat_axis=0,
+        tiled=True,
+    )
+    grad_docs = jnp.sum(grad_terms.astype(jnp.float32), axis=0)
     grad_queries = query_grads(weights, totals, hits, doc_piece)
     loss_rows = loss_col.reshape(loss_col.shape[0])
     return (loss_rows, grad_queries, grad_docs)

time: 158 us -> 138 us (0.87)
  between operations: 14.8 us -> 1.46 us
  waiting for transfers between devices: 60.4 us -> 49 us
  starting transfers between devices: 18.3 us -> 22 us
  other arithmetic: 16.6 us -> 18.5 us
    reduce_scatter x1 -> x0, waiting for transfers between devices: 16.6 us -> none  [on_device(): lax.psum_scatter(grad_part, 'blk', scatter_dimension=0, tiled=True)]
    all_to_all x0 -> x1, waiting for transfers between devices: none -> 5.25 us  [on_device(): lax.all_to_all(grad_part.astype(jnp.bfloat16).reshape(cycle_size, doc_uni...]
    all_to_all x0 -> x1, starting transfers between devices: none -> 3.78 us  [on_device(): lax.all_to_all(grad_part.astype(jnp.bfloat16).reshape(cycle_size, doc_uni...]
    convert_element_type x0 -> x1, other arithmetic: none -> 2.14 us  [on_device(): grad_part.astype(jnp.bfloat16)]
  transfers between devices with their start and end apart: 7 -> 7, of which waited for: 5 -> 5; matrix products, arithmetic and copies ran while one was open for 14% -> 16% of each run, Pallas kernels for 5% -> 6%
where the time goes in v9:
time: 138 us; the launch traced here: 137 us
  waiting for transfers between devices  49 us (36%)
  starting transfers between devices  22 us (16%)
  Pallas kernels  20.4 us (15%)
  other arithmetic  18.5 us (13%)
  local copies, waits for them, and re-layouts  17.2 us (12%)
  matrix products  8.18 us (6%)
  between operations  1.46 us (1%)
    all_to_all x1, waiting for transfers between devices, on_device(): lax.all_to_all(send_rows, 'dp', split_axis=0, concat_axis=0, tiled=True)  20.3 us
    all_to_all x1, waiting for transfers between devices, on_device(): lax.all_to_all(partial, 'dp', split_axis=0, concat_axis=0, tiled=True)  13 us
    pallas_call x1, Pallas kernels, scores(): pl.pallas_call(score_kernel, grid=(rows // tile,), in_specs=[pl.BlockSpec...  12.4 us
    ppermute x3, waiting for transfers between devices, on_device(): lax.ppermute(doc_unit, 'blk', [(i, (i + shift) % cycle_size) for i in ran...  10.5 us
    dot_general x1, matrix products, on_device(): partial = jnp.dot(selector, embedded, preferred_element_type=jnp.float32)  8.18 us
    pallas_call x1, Pallas kernels, query_grads(): pl.pallas_call(query_grad_kernel, grid=(rows // tile,), in_specs=[pl.Bloc...  8.03 us
    all_to_all x1, waiting for transfers between devices, on_device(): lax.all_to_all(grad_part.astype(jnp.bfloat16).reshape(cycle_size, doc_uni...  5.25 us
    gather x3, other arithmetic, on_device(): slot_of = source_of * capacity + packed_index - starts[source_of]  5.09 us
  transfers between devices with their start and end apart: 7, of which 5 were waited for; matrix products, arithmetic and copies ran while one was open for 16% of the time, Pallas kernels for 6%

profile of v9, /device:TPU:2, one launch (start us, length us, event | category | flops | bytes accessed | tf_op | source)
XLA Modules:
  0.0 136.8 jit_solution(6441414660669410157)
XLA Ops:
  0.6 1.2 slice.9
  6.6 4.3 %all-to-all-start = ((s32[8,1,154]{2,1,0:T(1,128)}), s32[8,1,154]{2,1,0:T(1,128)S(1)}, u32[]{:S(2)}, u32[]{:S(2)}) async-start(s32[8,1,154]{2,1,0:T(1,128)} %copy.18), calls=%async_computation | async-start | bytes 16384 | tf_op jit(solution)/shard_map/all_to_all | solution.py:135
  10.9 3.2 %copy.19 = bf16[160,8,1024]{2,0,1:T(8,128)(2,1)S(1)} copy(bf16[160,8,1024]{2,1,0:T(8,128)(2,1)} %bitcast.40) | data formatting | bytes 5242880 | tf_op jit(solution)/shard_map/reshape | solution.py:127
  14.0 2.2 %gather_fusion.2 = bf16[8,160,1024]{2,1,0:T(8,128)(2,1)} fusion(bf16[160,8,1024]{2,0,1:T(8,128)(2,1)S(1)} %copy.19, s32[1024]{0:T(1024)S(1)} %pad_clamp_fusion.2), kind=kCustom, calls=%fused_computation.2 | custom fusion | bytes 5242912 | tf_op jit(solution)/shard_map/jit(_take)/gather | solution.py:128
  16.2 3.6 %slice_select_fusion = bf16[8,154,1024]{2,1,0:T(8,128)(2,1)} fusion(bf16[8,160,1024]{2,1,0:T(8,128)(2,1)} %gather_fusion.2, pred[8]{0:T(512)(128)(4,1)S(1)} %compare_and_fusion), kind=kLoop, calls=%fused_computation.17 | loop fusion | flops 1261568 | bytes 5046280 | tf_op jit(solution)/shard_map/jit(_take)/select_n | solution.py:128
  19.8 4.4 %all-to-all-start.1 = ((bf16[8,154,1024]{2,1,0:T(8,128)(2,1)}), bf16[8,154,1024]{2,1,0:T(8,128)(2,1)}, u32[]{:S(2)}, u32[]{:S(2)}) async-start(bf16[8,154,1024]{2,1,0:T(8,128)(2,1)} %slice_select_fusion), calls=%async_computation.1 | async-start | bytes 5242880 | tf_op jit(solution)/shard_map/all_to_all | solution.py:134
  26.0 4.4 %fusion.30 = (s32[320]{0:T(512)S(1)}, s32[320,1]{0,1:T(1,128)S(1)}) fusion(s32[]{:T(128)} %bitcast.7, s32[]{:T(128)} %bitcast.8, s32[]{:T(128)} %bitcast.9, s32[]{:T(128)} %bitcast.10, s32[]{:T(128)} %bitcast.11, s32[]{:T(128)} %bitcast.13, s32[]{:T(128)} %bitcast.12, s32[320]{0:T(512)S(1)} %get-tuple-element.17, s32[320]{0:T(512)S(1)} %get-tuple-element.16), kind=kLoop, calls=%fused_computation.74 | loop fusion | flops 4480 | bytes 5148 | tf_op jit(solution)/shard_map/gather | solution.py:143
  31.8 2.2 %gather_fusion.1 = s32[320]{0:T(512)S(1)} fusion(s32[1232]{0:T(1024)S(1)} %reshape.288, s32[1024]{0:T(1024)S(1)} %pad_clamp_fusion.1), kind=kCustom, calls=%fused_computation.1 | custom fusion | bytes 3840 | tf_op jit(solution)/shard_map/gather | solution.py:148
  34.7 20.3 %all-to-all-done.1 = bf16[8,154,1024]{2,1,0:T(8,128)(2,1)} async-done(((bf16[8,154,1024]{2,1,0:T(8,128)(2,1)}), bf16[8,154,1024]{2,1,0:T(8,128)(2,1)}, u32[]{:S(2)}, u32[]{:S(2)}) %all-to-all-start.1) | async-done | bytes 2523168 | tf_op jit(solution)/shard_map/all_to_all | solution.py:134
  55.0 2.1 %reshape.290 = bf16[1232,1024]{1,0:T(8,128)(2,1)S(1)} reshape(bf16[8,154,1024]{2,1,0:T(8,128)(2,1)} %all-to-all-done.1) | data formatting | bytes 5046272 | tf_op jit(solution)/shard_map/reshape | solution.py:146
  57.1 2.1 %gather_fusion.3 = bf16[320,1024]{1,0:T(8,128)(2,1)S(1)} fusion(bf16[1232,1024]{1,0:T(8,128)(2,1)S(1)} %reshape.290, s32[1024]{0:T(1024)S(1)} %pad_clamp_fusion.1), kind=kCustom, calls=%fused_computation.3 | custom fusion | bytes 1312000 | tf_op jit(solution)/shard_map/gather | solution.py:146
  59.4 8.2 %convolution_convert_fusion = bf16[128,4096]{1,0:T(8,128)(2,1)} fusion(bf16[1,1024,4096]{2,1,0:T(8,128)(2,1)} %param.12, bf16[320,1024]{1,0:T(8,128)(2,1)S(1)} %gather_fusion.3, f32[1024]{0:T(1024)S(1)} %copy-done.2, f32[320]{0:T(512)S(1)} %add_rsqrt_fusion, s32[320]{0:T(512)S(1)} %add_select_fusion), kind=kOutput, calls=%fused_computation.16 | convolution fusion | flops 3033571328 | bytes 10099200 | tf_op jit(solution)/shard_map/dot_general | solution.py:164
  67.6 5.0 %all-to-all-start.2 = ((bf16[8,16,4096]{2,1,0:T(8,128)(2,1)}), bf16[8,16,4096]{2,1,0:T(8,128)(2,1)S(1)}, u32[]{:S(2)}, u32[]{:S(2)}) async-start(bf16[8,16,4096]{2,1,0:T(8,128)(2,1)} %bitcast.16), calls=%async_computation.2 | async-start | bytes 2097152 | tf_op jit(solution)/shard_map/all_to_all | solution.py:166
  73.5 13.0 %all-to-all-done.2 = bf16[8,16,4096]{2,1,0:T(8,128)(2,1)S(1)} async-done(((bf16[8,16,4096]{2,1,0:T(8,128)(2,1)}), bf16[8,16,4096]{2,1,0:T(8,128)(2,1)S(1)}, u32[]{:S(2)}, u32[]{:S(2)}) %all-to-all-start.2) | async-done | bytes 1048608 | tf_op jit(solution)/shard_map/all_to_all | solution.py:166
  86.9 3.7 %collective-permute-start.2 = (bf16[16,4096]{1,0:T(8,128)(2,1)S(1)}, bf16[16,4096]{1,0:T(8,128)(2,1)S(1)}, u32[]{:S(2)}, u32[]{:S(2)}) collective-permute-start(bf16[16,4096]{1,0:T(8,128)(2,1)S(1)} %multiply_convert_fusion), channel_id=1, source_target_pairs={{0,3},{1,0},{2,1},{3,2},{4,7},{5,4},{6,5},{7,6},{8,11},{9,8},{10,9... | collective-permute-start | bytes 393224 | tf_op jit(solution)/shard_map/ppermute | solution.py:175
  90.6 1.0 collective-permute-start
  91.7 2.8 %collective-permute-done.2 = bf16[16,4096]{1,0:T(8,128)(2,1)S(1)} collective-permute-done((bf16[16,4096]{1,0:T(8,128)(2,1)S(1)}, bf16[16,4096]{1,0:T(8,128)(2,1)S(1)}, u32[]{:S(2)}, u32[]{:S(2)}) %collective-permute-start.2) | collective-permute-done | bytes 131104 | tf_op jit(solution)/shard_map/ppermute | solution.py:175
  94.5 7.6 %collective-permute-done.1 = bf16[16,4096]{1,0:T(8,128)(2,1)S(1)} collective-permute-done((bf16[16,4096]{1,0:T(8,128)(2,1)S(1)}, bf16[16,4096]{1,0:T(8,128)(2,1)S(1)}, u32[]{:S(2)}, u32[]{:S(2)}) %collective-permute-start.1) | collective-permute-done | bytes 131104 | tf_op jit(solution)/shard_map/ppermute | solution.py:175
  102.2 1.4 %gather_fusion.4 = bf16[4,16,4096]{2,1,0:T(8,128)(2,1)} fusion(bf16[4,16,4096]{2,1,0:T(8,128)(2,1)S(1)} %pad_maximum_fusion, s32[1024]{0:T(1024)S(1)} %pad_clamp_fusion), kind=kCustom, calls=%fused_computation.4 | custom fusion | bytes 1048592 | tf_op jit(solution)/shard_map/gather | solution.py:180
  103.6 12.4 %shard_map.103 = (f32[896,1]{1,0:T(8,128)}, bf16[896,64]{1,0:T(8,128)(2,1)}, f32[896,1]{1,0:T(8,128)}, f32[64,4096]{1,0:T(8,128)}) custom-call(bf16[896,4096]{1,0:T(8,128)(2,1)} %q_ref.1, bf16[64,4096]{1,0:T(8,128)(2,1)} %bitcast.38, bf16[896,64]{1,0:T(8,128)(2,1)} %fusion.23.hit_ref), custom_call_target="tpu_custom_call" | custom-call | flops 939524096 | bytes 7340032 | tf_op jit(solution)/shard_map/pallas_call | solution.py:67
  116.0 2.1 %convert_element_type.54 = bf16[64,4096]{1,0:T(8,128)(2,1)} convert(f32[64,4096]{1,0:T(8,128)} %get-tuple-element.10) | non-fusion elementwise | flops 262144 | bytes 1572864 | tf_op jit(solution)/shard_map/convert_element_type | solution.py:187
  118.1 3.8 %all-to-all-start.3 = ((bf16[4,16,4096]{2,1,0:T(8,128)(2,1)}), bf16[4,16,4096]{2,1,0:T(8,128)(2,1)S(1)}, u32[]{:S(2)}, u32[]{:S(2)}) async-start(bf16[4,16,4096]{2,1,0:T(8,128)(2,1)} %bitcast.23), calls=%async_computation.3 | async-start | bytes 1048576 | tf_op jit(solution)/shard_map/all_to_all | solution.py:186
  122.7 8.0 %shard_map.104 = bf16[896,4096]{1,0:T(8,128)(2,1)} custom-call(bf16[896,64]{1,0:T(8,128)(2,1)} %get-tuple-element.8.wb_ref, f32[896,1]{1,0:T(8,128)} %get-tuple-element.9.tot_ref, bf16[896,64]{1,0:T(8,128)(2,1)} %fusion.23.hit_ref, bf16[64,4096]{1,0:T(8,128)(2,1)} %bitcast.39), custom_call_target="tpu_custom_call" | custom-call | flops 939524096 | bytes 7340032 | tf_op jit(solution)/shard_map/pallas_call | solution.py:97
  130.8 5.3 %all-to-all-done.3 = bf16[4,16,4096]{2,1,0:T(8,128)(2,1)S(1)} async-done(((bf16[4,16,4096]{2,1,0:T(8,128)(2,1)}), bf16[4,16,4096]{2,1,0:T(8,128)(2,1)S(1)}, u32[]{:S(2)}, u32[]{:S(2)}) %all-to-all-start.3) | async-done | bytes 524320 | tf_op jit(solution)/shard_map/all_to_all | solution.py:186
  (44 shorter events, 11.2 us)
Async XLA Ops:
  6.6 13.2 %all-to-all-start = ((s32[8,1,154]{2,1,0:T(1,128)}), s32[8,1,154]{2,1,0:T(1,128)S(1)}, u32[]{:S(2)}, u32[]{:S(2)}) async-start(s32[8,1,154]{2,1,0:T(1,128)} %copy.18), calls=%async_computation | async-start | bytes 16384 | tf_op jit(solution)/shard_map/all_to_all | solution.py:135
  19.8 35.2 %all-to-all-start.1 = ((bf16[8,154,1024]{2,1,0:T(8,128)(2,1)}), bf16[8,154,1024]{2,1,0:T(8,128)(2,1)}, u32[]{:S(2)}, u32[]{:S(2)}) async-start(bf16[8,154,1024]{2,1,0:T(8,128)(2,1)} %slice_select_fusion), calls=%async_computation.1 | async-start | bytes 5242880 | tf_op jit(solution)/shard_map/all_to_all | solution.py:134
  57.1 2.4 %copy-start.2 = (f32[1024]{0:T(1024)S(1)}, f32[1024]{0:T(1024)}, u32[]{:S(2)}) copy-start(f32[1024]{0:T(1024)} %param.13) | copy-start | bytes 12292
  59.4 13.2 %copy-start.1 = (s32[896]{0:T(1024)S(1)}, s32[896]{0:T(1024)}, u32[]{:S(2)}) copy-start(s32[896]{0:T(1024)} %param.15) | copy-start | bytes 10756
  67.6 18.9 %all-to-all-start.2 = ((bf16[8,16,4096]{2,1,0:T(8,128)(2,1)}), bf16[8,16,4096]{2,1,0:T(8,128)(2,1)S(1)}, u32[]{:S(2)}, u32[]{:S(2)}) async-start(bf16[8,16,4096]{2,1,0:T(8,128)(2,1)} %bitcast.16), calls=%async_computation.2 | async-start | bytes 2097152 | tf_op jit(solution)/shard_map/all_to_all | solution.py:166
  86.9 7.6 %collective-permute-start.2 = (bf16[16,4096]{1,0:T(8,128)(2,1)S(1)}, bf16[16,4096]{1,0:T(8,128)(2,1)S(1)}, u32[]{:S(2)}, u32[]{:S(2)}) collective-permute-start(bf16[16,4096]{1,0:T(8,128)(2,1)S(1)} %multiply_convert_fusion), channel_id=1, source_target_pairs={{0,3},{1,0},{2,1},{3,2},{4,7},{5,4},{6,5},{7,6},{8,11},{9,8},{10,9... | collective-permute-start | bytes 393224 | tf_op jit(solution)/shard_map/ppermute | solution.py:175
  90.6 11.6 %collective-permute-start.1 = (bf16[16,4096]{1,0:T(8,128)(2,1)S(1)}, bf16[16,4096]{1,0:T(8,128)(2,1)S(1)}, u32[]{:S(2)}, u32[]{:S(2)}) collective-permute-start(bf16[16,4096]{1,0:T(8,128)(2,1)S(1)} %multiply_convert_fusion), channel_id=1, source_target_pairs={{0,2},{1,3},{2,0},{3,1},{4,6},{5,7},{6,4},{7,5},{8,10},{9,11},{10,... | collective-permute-start | bytes 393224 | tf_op jit(solution)/shard_map/ppermute | solution.py:175
  90.6 11.6 %collective-permute-start = (bf16[16,4096]{1,0:T(8,128)(2,1)S(1)}, bf16[16,4096]{1,0:T(8,128)(2,1)S(1)}, u32[]{:S(2)}, u32[]{:S(2)}) collective-permute-start(bf16[16,4096]{1,0:T(8,128)(2,1)S(1)} %multiply_convert_fusion), channel_id=1, source_target_pairs={{0,1},{1,2},{2,3},{3,0},{4,5},{5,6},{6,7},{7,4},{8,9},{9,10},{10,1... | collective-permute-start | bytes 393224 | tf_op jit(solution)/shard_map/ppermute | solution.py:175
  116.0 5.9 %copy-start = (f32[896,1]{1,0:T(8,128)S(1)}, f32[896,1]{1,0:T(8,128)}, u32[]{:S(2)}) copy-start(f32[896,1]{1,0:T(8,128)} %get-tuple-element.7) | copy-start | bytes 10756
  118.1 17.9 %all-to-all-start.3 = ((bf16[4,16,4096]{2,1,0:T(8,128)(2,1)}), bf16[4,16,4096]{2,1,0:T(8,128)(2,1)S(1)}, u32[]{:S(2)}, u32[]{:S(2)}) async-start(bf16[4,16,4096]{2,1,0:T(8,128)(2,1)} %bitcast.23), calls=%async_computation.3 | async-start | bytes 1048576 | tf_op jit(solution)/shard_map/all_to_all | solution.py:186

commit v10 on v9

--- a/solution.py
+++ b/solution.py
@@ -31,10 +31,10 @@
     )
 
 
-def score_kernel(q_ref, d_ref, hit_ref, loss_ref, wb_ref, tot_ref, gd_ref):
+def score_kernel(q_ref, d_ref, hit_ref, loss_ref, wb_ref, tot_ref, gd_ref, acc_ref):
     @pl.when(pl.program_id(0) == 0)
     def _():
-        gd_ref[...] = jnp.zeros_like(gd_ref)
+        acc_ref[...] = jnp.zeros_like(acc_ref)
 
     widened = q_ref[...].astype(jnp.float32)
     query_unit = (
@@ -49,9 +49,13 @@
     wb_ref[...] = weights.astype(jnp.bfloat16)
     tot_ref[...] = totals
     coefficient_t = (weights / totals - hits).T.astype(jnp.bfloat16)
-    gd_ref[...] += logit_scale * jnp.dot(
+    acc_ref[...] += logit_scale * jnp.dot(
         coefficient_t, query_unit, preferred_element_type=jnp.float32
     )
+
+    @pl.when(pl.program_id(0) == pl.num_programs(0) - 1)
+    def _():
+        gd_ref[...] = acc_ref[...].astype(jnp.bfloat16)
 
 
 def query_grad_kernel(wb_ref, tot_ref, hit_ref, d_ref, gq_ref):
@@ -82,8 +86,9 @@
             jax.ShapeDtypeStruct((rows, 1), jnp.float32),
             jax.ShapeDtypeStruct((rows, docs), jnp.bfloat16),
             jax.ShapeDtypeStruct((rows, 1), jnp.float32),
-            jax.ShapeDtypeStruct((docs, width), jnp.float32),
-        ],
+            jax.ShapeDtypeStruct((docs, width), jnp.bfloat16),
+        ],
+        scratch_shapes=[pltpu.VMEM((docs, width), jnp.float32)],
         compiler_params=pltpu.CompilerParams(dimension_semantics=("arbitrary",)),
         cost_estimate=pl.CostEstimate(
             flops=4 * rows * docs * width, transcendentals=rows * docs, bytes_accessed=2 * rows * width
@@ -125,11 +130,13 @@
 
     lane_of = (jnp.arange(groups, dtype=jnp.int32) - destinations[0]) % groups
     by_lane = spans.reshape(cycle, groups, hidden_width)
-    send_rows = jnp.swapaxes(jnp.take(by_lane, lane_of, axis=1), 0, 1)[:, :capacity]
+    send_rows = jnp.swapaxes(jnp.take(by_lane, lane_of, axis=1, mode="clip"), 0, 1)[
+        :, :capacity
+    ]
     row_of = lane_of[:, None] + groups * jnp.arange(capacity, dtype=jnp.int32)[None, :]
     ids_by_lane = session_ids.reshape(cycle, groups)
     send_ids = jnp.where(
-        row_of < count, jnp.swapaxes(jnp.take(ids_by_lane, lane_of, axis=1), 0, 1)[:, :capacity], -1
+        row_of < count, jnp.swapaxes(jnp.take(ids_by_lane, lane_of, axis=1, mode="clip"), 0, 1)[:, :capacity], -1
     )
     got_rows = lax.all_to_all(send_rows, "dp", split_axis=0, concat_axis=0, tiled=True)
     got_ids = lax.all_to_all(send_ids, "dp", split_axis=0, concat_axis=0, tiled=True)
@@ -143,7 +150,7 @@
     slot_of = source_of * capacity + packed_index - starts[source_of]
     packed_live = packed_index < jnp.sum(got_counts)
     slot_of = jnp.where(packed_live, slot_of, 0)
-    packed = got_rows.reshape(groups * capacity, hidden_width)[slot_of]
+    packed = got_rows[source_of, jnp.where(packed_live, packed_index - starts[source_of], 0)]
     packed_key = jnp.where(
         packed_live, source_of * SESS_DEV + got_ids.reshape(groups * capacity)[slot_of], -1
     )
@@ -184,7 +191,7 @@
     )
     loss_col, weights, totals, grad_part = scores(queries, doc_piece, hits)
     grad_terms = lax.all_to_all(
-        grad_part.astype(jnp.bfloat16).reshape(cycle_size, doc_unit.shape[0], emb_width),
+        grad_part.reshape(cycle_size, doc_unit.shape[0], emb_width),
         "blk",
         split_axis=0,
         concat_axis=0,

time: 138 us -> 137 us (level)
  local copies, waits for them, and re-layouts: 17.2 us -> 22.7 us
  other arithmetic: 18.5 us -> 13.2 us
    gather x3, local copies, waits for them, and re-layouts: 4.88 us -> 9.41 us  [the longest x1 6.63 us: on_device(): got_rows[source_of, jnp.where(packed_live, packed_index - starts[source_o...]
    select_n x2 -> x0, other arithmetic: 4.24 us -> none  [the longest x1 3.58 us: on_device(): jnp.take(by_lane, lane_of, axis=1)]
    all_to_all x0 -> x1, local copies, waits for them, and re-layouts: none -> 3.12 us  [on_device(): lax.all_to_all(send_rows, 'dp', split_axis=0, concat_axis=0, tiled=True)]
    convert_element_type x1 -> x0, other arithmetic: 2.14 us -> none  [on_device(): grad_part.astype(jnp.bfloat16)]
    reshape x1 -> x0, local copies, waits for them, and re-layouts: 2.06 us -> none  [on_device(): packed = got_rows.reshape(groups * capacity, hidden_width)[slot_of]]
  transfers between devices with their start and end apart: 7 -> 7, of which waited for: 5 -> 5; matrix products, arithmetic and copies ran while one was open for 16% -> 14% of each run, Pallas kernels for 6% -> 6%
where the time goes in v10:
time: 137 us; the launch traced here: 136 us
  waiting for transfers between devices  47.9 us (35%)
  local copies, waits for them, and re-layouts  22.7 us (17%)
  starting transfers between devices  22.1 us (16%)
  Pallas kernels  20.4 us (15%)
  other arithmetic  13.2 us (10%)
  matrix products  8.18 us (6%)
  between operations  1.44 us (1%)
    all_to_all x1, waiting for transfers between devices, on_device(): lax.all_to_all(send_rows, 'dp', split_axis=0, concat_axis=0, tiled=True)  20.2 us
    all_to_all x1, waiting for transfers between devices, on_device(): lax.all_to_all(partial, 'dp', split_axis=0, concat_axis=0, tiled=True)  13 us
    pallas_call x1, Pallas kernels, scores(): pl.pallas_call(score_kernel, grid=(rows // tile,), in_specs=[pl.BlockSpec...  12.4 us
    ppermute x3, waiting for transfers between devices, on_device(): lax.ppermute(doc_unit, 'blk', [(i, (i + shift) % cycle_size) for i in ran...  10.5 us
    dot_general x1, matrix products, on_device(): partial = jnp.dot(selector, embedded, preferred_element_type=jnp.float32)  8.18 us
    pallas_call x1, Pallas kernels, query_grads(): pl.pallas_call(query_grad_kernel, grid=(rows // tile,), in_specs=[pl.Bloc...  8.02 us
    gather x1, local copies, waits for them, and re-layouts, on_device(): got_rows[source_of, jnp.where(packed_live, packed_index - starts[source_o...  6.63 us
    gather x3, other arithmetic, on_device(): slot_of = source_of * capacity + packed_index - starts[source_of]  5.18 us
  transfers between devices with their start and end apart: 7, of which 5 were waited for; matrix products, arithmetic and copies ran while one was open for 14% of the time, Pallas kernels for 6%

profile of v10, /device:TPU:2, one launch (start us, length us, event | category | flops | bytes accessed | tf_op | source)
XLA Modules:
  0.0 136.0 jit_solution(10652800438077761291)
XLA Ops:
  0.6 1.2 slice.9
  5.9 4.3 %all-to-all-start = ((s32[8,1,154]{2,1,0:T(1,128)}), s32[8,1,154]{2,1,0:T(1,128)S(1)}, u32[]{:S(2)}, u32[]{:S(2)}) async-start(s32[8,1,154]{2,1,0:T(1,128)} %copy.21), calls=%async_computation | async-start | bytes 16384 | tf_op jit(solution)/shard_map/all_to_all | solution.py:142
  10.2 3.2 %copy.22 = bf16[160,8,1024]{2,0,1:T(8,128)(2,1)S(1)} copy(bf16[160,8,1024]{2,1,0:T(8,128)(2,1)} %bitcast.41) | data formatting | bytes 5242880 | tf_op jit(solution)/shard_map/reshape | solution.py:132
  13.4 2.2 %gather_fusion.2 = bf16[8,160,1024]{2,1,0:T(8,128)(2,1)} fusion(bf16[160,8,1024]{2,0,1:T(8,128)(2,1)S(1)} %copy.22, s32[1024]{0:T(1024)S(1)} %pad_clamp_fusion.2), kind=kCustom, calls=%fused_computation.2 | custom fusion | bytes 5242912 | tf_op jit(solution)/shard_map/jit(_take)/gather | solution.py:133
  15.6 4.4 %all-to-all-start.1 = ((bf16[8,154,1024]{2,1,0:T(8,128)(2,1)}), bf16[8,154,1024]{2,1,0:T(8,128)(2,1)}, u32[]{:S(2)}, u32[]{:S(2)}) async-start(bf16[8,154,1024]{2,1,0:T(8,128)(2,1)} %bitcast.37), calls=%async_computation.1 | async-start | bytes 5242880 | tf_op jit(solution)/shard_map/all_to_all | solution.py:141
  21.8 4.5 %fusion.29 = (s32[320]{0:T(512)S(1)}, s32[320,1]{0,1:T(1,128)S(1)}) fusion(s32[]{:T(128)} %bitcast.7, s32[]{:T(128)} %bitcast.8, s32[]{:T(128)} %bitcast.9, s32[]{:T(128)} %bitcast.10, s32[]{:T(128)} %bitcast.11, s32[]{:T(128)} %bitcast.13, s32[]{:T(128)} %bitcast.12, s32[320]{0:T(512)S(1)} %get-tuple-element.19, s32[320]{0:T(512)S(1)} %get-tuple-element.18), kind=kLoop, calls=%fused_computation.71 | loop fusion | flops 4480 | bytes 5148 | tf_op jit(solution)/shard_map/gather | solution.py:150
  27.7 2.2 %gather_fusion.1 = s32[320]{0:T(512)S(1)} fusion(s32[1232]{0:T(1024)S(1)} %reshape.293, s32[1024]{0:T(1024)S(1)} %pad_clamp_fusion.1), kind=kCustom, calls=%fused_computation.1 | custom fusion | bytes 3840 | tf_op jit(solution)/shard_map/gather | solution.py:155
  30.6 20.2 %all-to-all-done.1 = bf16[8,154,1024]{2,1,0:T(8,128)(2,1)} async-done(((bf16[8,154,1024]{2,1,0:T(8,128)(2,1)}), bf16[8,154,1024]{2,1,0:T(8,128)(2,1)}, u32[]{:S(2)}, u32[]{:S(2)}) %all-to-all-start.1) | async-done | bytes 2523168 | tf_op jit(solution)/shard_map/all_to_all | solution.py:141
  50.7 3.1 %copy.23 = bf16[8,154,1024]{2,0,1:T(8,128)(2,1)S(1)} copy(bf16[8,154,1024]{2,1,0:T(8,128)(2,1)} %all-to-all-done.1) | data formatting | bytes 5046272 | tf_op jit(solution)/shard_map/all_to_all | solution.py:141
  53.9 6.6 %gather_fusion.3 = bf16[320,1024]{1,0:T(8,128)(2,1)S(1)} fusion(bf16[8,154,1024]{2,0,1:T(8,128)(2,1)S(1)} %copy.23, s32[320]{0:T(512)S(1)} %get-tuple-element.15), kind=kCustom, calls=%fused_computation.3 | custom fusion | bytes 1313280 | tf_op jit(solution)/shard_map/gather | solution.py:153
  60.8 8.2 %convolution_convert_fusion = bf16[128,4096]{1,0:T(8,128)(2,1)} fusion(bf16[1,1024,4096]{2,1,0:T(8,128)(2,1)} %param.12, bf16[320,1024]{1,0:T(8,128)(2,1)S(1)} %gather_fusion.3, f32[1024]{0:T(1024)S(1)} %copy-done.1, f32[320]{0:T(512)S(1)} %add_rsqrt_fusion, s32[320]{0:T(512)S(1)} %add_select_fusion), kind=kOutput, calls=%fused_computation.16 | convolution fusion | flops 3033571328 | bytes 10099200 | tf_op jit(solution)/shard_map/dot_general | solution.py:171
  68.9 5.0 %all-to-all-start.2 = ((bf16[8,16,4096]{2,1,0:T(8,128)(2,1)}), bf16[8,16,4096]{2,1,0:T(8,128)(2,1)S(1)}, u32[]{:S(2)}, u32[]{:S(2)}) async-start(bf16[8,16,4096]{2,1,0:T(8,128)(2,1)} %bitcast.16), calls=%async_computation.2 | async-start | bytes 2097152 | tf_op jit(solution)/shard_map/all_to_all | solution.py:173
  74.0 0.9 fusion.23.hit_ref
  74.8 13.0 %all-to-all-done.2 = bf16[8,16,4096]{2,1,0:T(8,128)(2,1)S(1)} async-done(((bf16[8,16,4096]{2,1,0:T(8,128)(2,1)}), bf16[8,16,4096]{2,1,0:T(8,128)(2,1)S(1)}, u32[]{:S(2)}, u32[]{:S(2)}) %all-to-all-start.2) | async-done | bytes 1048608 | tf_op jit(solution)/shard_map/all_to_all | solution.py:173
  88.2 3.7 %collective-permute-start.2 = (bf16[16,4096]{1,0:T(8,128)(2,1)S(1)}, bf16[16,4096]{1,0:T(8,128)(2,1)S(1)}, u32[]{:S(2)}, u32[]{:S(2)}) collective-permute-start(bf16[16,4096]{1,0:T(8,128)(2,1)S(1)} %multiply_convert_fusion), channel_id=1, source_target_pairs={{0,3},{1,0},{2,1},{3,2},{4,7},{5,4},{6,5},{7,6},{8,11},{9,8},{10,9... | collective-permute-start | bytes 393224 | tf_op jit(solution)/shard_map/ppermute | solution.py:182
  91.9 1.0 collective-permute-start
  93.0 2.8 %collective-permute-done.2 = bf16[16,4096]{1,0:T(8,128)(2,1)S(1)} collective-permute-done((bf16[16,4096]{1,0:T(8,128)(2,1)S(1)}, bf16[16,4096]{1,0:T(8,128)(2,1)S(1)}, u32[]{:S(2)}, u32[]{:S(2)}) %collective-permute-start.2) | collective-permute-done | bytes 131104 | tf_op jit(solution)/shard_map/ppermute | solution.py:182
  95.8 7.6 %collective-permute-done.1 = bf16[16,4096]{1,0:T(8,128)(2,1)S(1)} collective-permute-done((bf16[16,4096]{1,0:T(8,128)(2,1)S(1)}, bf16[16,4096]{1,0:T(8,128)(2,1)S(1)}, u32[]{:S(2)}, u32[]{:S(2)}) %collective-permute-start.1) | collective-permute-done | bytes 131104 | tf_op jit(solution)/shard_map/ppermute | solution.py:182
  103.5 1.4 %gather_fusion.4 = bf16[4,16,4096]{2,1,0:T(8,128)(2,1)} fusion(bf16[4,16,4096]{2,1,0:T(8,128)(2,1)S(1)} %pad_maximum_fusion, s32[1024]{0:T(1024)S(1)} %pad_clamp_fusion), kind=kCustom, calls=%fused_computation.4 | custom fusion | bytes 1048592 | tf_op jit(solution)/shard_map/gather | solution.py:187
  104.9 12.4 %shard_map.103 = (f32[896,1]{1,0:T(8,128)}, bf16[896,64]{1,0:T(8,128)(2,1)}, f32[896,1]{1,0:T(8,128)}, bf16[64,4096]{1,0:T(8,128)(2,1)}) custom-call(bf16[896,4096]{1,0:T(8,128)(2,1)} %q_ref.1, bf16[64,4096]{1,0:T(8,128)(2,1)} %bitcast.39, bf16[896,64]{1,0:T(8,128)(2,1)} %fusion.23.hit_ref), custom_call_target="tpu_custom_call" | custom-call | flops 939524096 | bytes 7340032 | tf_op jit(solution)/shard_map/pallas_call | solution.py:71
  117.3 3.8 %all-to-all-start.3 = ((bf16[4,16,4096]{2,1,0:T(8,128)(2,1)}), bf16[4,16,4096]{2,1,0:T(8,128)(2,1)S(1)}, u32[]{:S(2)}, u32[]{:S(2)}) async-start(bf16[4,16,4096]{2,1,0:T(8,128)(2,1)} %bitcast.42), calls=%async_computation.3 | async-start | bytes 1048576 | tf_op jit(solution)/shard_map/all_to_all | solution.py:193
  121.1 1.8 %reduce.8 = f32[896]{0:T(1024)} reduce(f32[896,1]{1,0:T(8,128)} %get-tuple-element.7, f32[]{:T(128)} %constant.98), dimensions={1}, to_apply=%get-tuple-element.7.reduce_sub_computation | reduce | bytes 7172 | tf_op jit(solution)/shard_map/pallas_call | solution.py:71
  122.9 8.0 %shard_map.104 = bf16[896,4096]{1,0:T(8,128)(2,1)} custom-call(bf16[896,64]{1,0:T(8,128)(2,1)} %get-tuple-element.8.wb_ref, f32[896,1]{1,0:T(8,128)} %get-tuple-element.9.tot_ref, bf16[896,64]{1,0:T(8,128)(2,1)} %fusion.23.hit_ref, bf16[64,4096]{1,0:T(8,128)(2,1)} %bitcast.40), custom_call_target="tpu_custom_call" | custom-call | flops 939524096 | bytes 7340032 | tf_op jit(solution)/shard_map/pallas_call | solution.py:102
  130.9 4.2 %all-to-all-done.3 = bf16[4,16,4096]{2,1,0:T(8,128)(2,1)S(1)} async-done(((bf16[4,16,4096]{2,1,0:T(8,128)(2,1)}), bf16[4,16,4096]{2,1,0:T(8,128)(2,1)S(1)}, u32[]{:S(2)}, u32[]{:S(2)}) %all-to-all-start.3) | async-done | bytes 524320 | tf_op jit(solution)/shard_map/all_to_all | solution.py:193
  (39 shorter events, 8.8 us)
Async XLA Ops:
  5.9 9.6 %all-to-all-start = ((s32[8,1,154]{2,1,0:T(1,128)}), s32[8,1,154]{2,1,0:T(1,128)S(1)}, u32[]{:S(2)}, u32[]{:S(2)}) async-start(s32[8,1,154]{2,1,0:T(1,128)} %copy.21), calls=%async_computation | async-start | bytes 16384 | tf_op jit(solution)/shard_map/all_to_all | solution.py:142
  15.6 35.2 %all-to-all-start.1 = ((bf16[8,154,1024]{2,1,0:T(8,128)(2,1)}), bf16[8,154,1024]{2,1,0:T(8,128)(2,1)}, u32[]{:S(2)}, u32[]{:S(2)}) async-start(bf16[8,154,1024]{2,1,0:T(8,128)(2,1)} %bitcast.37), calls=%async_computation.1 | async-start | bytes 5242880 | tf_op jit(solution)/shard_map/all_to_all | solution.py:141
  30.6 30.2 %copy-start.1 = (f32[1024]{0:T(1024)S(1)}, f32[1024]{0:T(1024)}, u32[]{:S(2)}) copy-start(f32[1024]{0:T(1024)} %param.13) | copy-start | bytes 12292
  60.7 13.2 %copy-start = (s32[896]{0:T(1024)S(1)}, s32[896]{0:T(1024)}, u32[]{:S(2)}) copy-start(s32[896]{0:T(1024)} %param.15) | copy-start | bytes 10756
  68.9 18.9 %all-to-all-start.2 = ((bf16[8,16,4096]{2,1,0:T(8,128)(2,1)}), bf16[8,16,4096]{2,1,0:T(8,128)(2,1)S(1)}, u32[]{:S(2)}, u32[]{:S(2)}) async-start(bf16[8,16,4096]{2,1,0:T(8,128)(2,1)} %bitcast.16), calls=%async_computation.2 | async-start | bytes 2097152 | tf_op jit(solution)/shard_map/all_to_all | solution.py:173
  88.2 7.6 %collective-permute-start.2 = (bf16[16,4096]{1,0:T(8,128)(2,1)S(1)}, bf16[16,4096]{1,0:T(8,128)(2,1)S(1)}, u32[]{:S(2)}, u32[]{:S(2)}) collective-permute-start(bf16[16,4096]{1,0:T(8,128)(2,1)S(1)} %multiply_convert_fusion), channel_id=1, source_target_pairs={{0,3},{1,0},{2,1},{3,2},{4,7},{5,4},{6,5},{7,6},{8,11},{9,8},{10,9... | collective-permute-start | bytes 393224 | tf_op jit(solution)/shard_map/ppermute | solution.py:182
  91.9 11.6 %collective-permute-start.1 = (bf16[16,4096]{1,0:T(8,128)(2,1)S(1)}, bf16[16,4096]{1,0:T(8,128)(2,1)S(1)}, u32[]{:S(2)}, u32[]{:S(2)}) collective-permute-start(bf16[16,4096]{1,0:T(8,128)(2,1)S(1)} %multiply_convert_fusion), channel_id=1, source_target_pairs={{0,2},{1,3},{2,0},{3,1},{4,6},{5,7},{6,4},{7,5},{8,10},{9,11},{10,... | collective-permute-start | bytes 393224 | tf_op jit(solution)/shard_map/ppermute | solution.py:182
  91.9 11.6 %collective-permute-start = (bf16[16,4096]{1,0:T(8,128)(2,1)S(1)}, bf16[16,4096]{1,0:T(8,128)(2,1)S(1)}, u32[]{:S(2)}, u32[]{:S(2)}) collective-permute-start(bf16[16,4096]{1,0:T(8,128)(2,1)S(1)} %multiply_convert_fusion), channel_id=1, source_target_pairs={{0,1},{1,2},{2,3},{3,0},{4,5},{5,6},{6,7},{7,4},{8,9},{9,10},{10,1... | collective-permute-start | bytes 393224 | tf_op jit(solution)/shard_map/ppermute | solution.py:182
  117.3 17.9 %all-to-all-start.3 = ((bf16[4,16,4096]{2,1,0:T(8,128)(2,1)}), bf16[4,16,4096]{2,1,0:T(8,128)(2,1)S(1)}, u32[]{:S(2)}, u32[]{:S(2)}) async-start(bf16[4,16,4096]{2,1,0:T(8,128)(2,1)} %bitcast.42), calls=%async_computation.3 | async-start | bytes 1048576 | tf_op jit(solution)/shard_map/all_to_all | solution.py:193

commit v11 on v10

--- a/solution.py
+++ b/solution.py
@@ -150,7 +150,7 @@
     slot_of = source_of * capacity + packed_index - starts[source_of]
     packed_live = packed_index < jnp.sum(got_counts)
     slot_of = jnp.where(packed_live, slot_of, 0)
-    packed = got_rows[source_of, jnp.where(packed_live, packed_index - starts[source_of], 0)]
+    packed = got_rows.reshape(groups * capacity, hidden_width)[slot_of]
     packed_key = jnp.where(
         packed_live, source_of * SESS_DEV + got_ids.reshape(groups * capacity)[slot_of], -1
     )

time: 137 us -> 131 us (0.956)
  local copies, waits for them, and re-layouts: 22.7 us -> 17.1 us
    gather x1, local copies, waits for them, and re-layouts: 6.63 us -> 2.09 us  [on_device(): packed = got_rows.reshape(groups * capacity, hidden_width)[slot_of]]
    all_to_all x1 -> x0, local copies, waits for them, and re-layouts: 3.12 us -> none  [on_device(): lax.all_to_all(send_rows, 'dp', split_axis=0, concat_axis=0, tiled=True)]
    reshape x0 -> x1, local copies, waits for them, and re-layouts: none -> 2.06 us  [on_device(): packed = got_rows.reshape(groups * capacity, hidden_width)[slot_of]]
where the time goes in v11:
time: 131 us; the launch traced here: 130 us
  waiting for transfers between devices  47.9 us (37%)
  starting transfers between devices  22.1 us (17%)
  Pallas kernels  20.4 us (16%)
  local copies, waits for them, and re-layouts  17.1 us (13%)
  other arithmetic  13.2 us (10%)
  matrix products  8.18 us (6%)
  between operations  1.44 us (1%)
    all_to_all x1, waiting for transfers between devices, on_device(): lax.all_to_all(send_rows, 'dp', split_axis=0, concat_axis=0, tiled=True)  20.2 us
    all_to_all x1, waiting for transfers between devices, on_device(): lax.all_to_all(partial, 'dp', split_axis=0, concat_axis=0, tiled=True)  13 us
    pallas_call x1, Pallas kernels, scores(): pl.pallas_call(score_kernel, grid=(rows // tile,), in_specs=[pl.BlockSpec...  12.4 us
    ppermute x3, waiting for transfers between devices, on_device(): lax.ppermute(doc_unit, 'blk', [(i, (i + shift) % cycle_size) for i in ran...  10.5 us
    dot_general x1, matrix products, on_device(): partial = jnp.dot(selector, embedded, preferred_element_type=jnp.float32)  8.18 us
    pallas_call x1, Pallas kernels, query_grads(): pl.pallas_call(query_grad_kernel, grid=(rows // tile,), in_specs=[pl.Bloc...  8.02 us
    gather x3, other arithmetic, on_device(): slot_of = source_of * capacity + packed_index - starts[source_of]  5.18 us
    all_to_all x1, starting transfers between devices, on_device(): lax.all_to_all(partial, 'dp', split_axis=0, concat_axis=0, tiled=True)  4.99 us
  transfers between devices with their start and end apart: 7, of which 5 were waited for; matrix products, arithmetic and copies ran while one was open for 14% of the time, Pallas kernels for 6%

profile of v11, /device:TPU:2, one launch (start us, length us, event | category | flops | bytes accessed | tf_op | source)
XLA Modules:
  0.0 130.4 jit_solution(16168175284436985441)
XLA Ops:
  0.6 1.2 slice.9
  5.9 4.3 %all-to-all-start = ((s32[8,1,154]{2,1,0:T(1,128)}), s32[8,1,154]{2,1,0:T(1,128)S(1)}, u32[]{:S(2)}, u32[]{:S(2)}) async-start(s32[8,1,154]{2,1,0:T(1,128)} %copy.18), calls=%async_computation | async-start | bytes 16384 | tf_op jit(solution)/shard_map/all_to_all | solution.py:142
  10.2 3.2 %copy.19 = bf16[160,8,1024]{2,0,1:T(8,128)(2,1)S(1)} copy(bf16[160,8,1024]{2,1,0:T(8,128)(2,1)} %bitcast.41) | data formatting | bytes 5242880 | tf_op jit(solution)/shard_map/reshape | solution.py:132
  13.4 2.2 %gather_fusion.2 = bf16[8,160,1024]{2,1,0:T(8,128)(2,1)} fusion(bf16[160,8,1024]{2,0,1:T(8,128)(2,1)S(1)} %copy.19, s32[1024]{0:T(1024)S(1)} %pad_clamp_fusion.2), kind=kCustom, calls=%fused_computation.2 | custom fusion | bytes 5242912 | tf_op jit(solution)/shard_map/jit(_take)/gather | solution.py:133
  15.6 4.4 %all-to-all-start.1 = ((bf16[8,154,1024]{2,1,0:T(8,128)(2,1)}), bf16[8,154,1024]{2,1,0:T(8,128)(2,1)}, u32[]{:S(2)}, u32[]{:S(2)}) async-start(bf16[8,154,1024]{2,1,0:T(8,128)(2,1)} %bitcast.37), calls=%async_computation.1 | async-start | bytes 5242880 | tf_op jit(solution)/shard_map/all_to_all | solution.py:141
  21.8 4.5 %fusion.29 = (s32[320]{0:T(512)S(1)}, s32[320,1]{0,1:T(1,128)S(1)}) fusion(s32[]{:T(128)} %bitcast.7, s32[]{:T(128)} %bitcast.8, s32[]{:T(128)} %bitcast.9, s32[]{:T(128)} %bitcast.10, s32[]{:T(128)} %bitcast.11, s32[]{:T(128)} %bitcast.13, s32[]{:T(128)} %bitcast.12, s32[320]{0:T(512)S(1)} %get-tuple-element.17, s32[320]{0:T(512)S(1)} %get-tuple-element.16), kind=kLoop, calls=%fused_computation.69 | loop fusion | flops 4480 | bytes 5148 | tf_op jit(solution)/shard_map/gather | solution.py:150
  27.6 2.2 %gather_fusion.1 = s32[320]{0:T(512)S(1)} fusion(s32[1232]{0:T(1024)S(1)} %reshape.273, s32[1024]{0:T(1024)S(1)} %pad_clamp_fusion.1), kind=kCustom, calls=%fused_computation.1 | custom fusion | bytes 3840 | tf_op jit(solution)/shard_map/gather | solution.py:155
  30.6 20.2 %all-to-all-done.1 = bf16[8,154,1024]{2,1,0:T(8,128)(2,1)} async-done(((bf16[8,154,1024]{2,1,0:T(8,128)(2,1)}), bf16[8,154,1024]{2,1,0:T(8,128)(2,1)}, u32[]{:S(2)}, u32[]{:S(2)}) %all-to-all-start.1) | async-done | bytes 2523168 | tf_op jit(solution)/shard_map/all_to_all | solution.py:141
  50.7 2.1 %reshape.275 = bf16[1232,1024]{1,0:T(8,128)(2,1)S(1)} reshape(bf16[8,154,1024]{2,1,0:T(8,128)(2,1)} %all-to-all-done.1) | data formatting | bytes 5046272 | tf_op jit(solution)/shard_map/reshape | solution.py:153
  52.8 2.1 %gather_fusion.3 = bf16[320,1024]{1,0:T(8,128)(2,1)S(1)} fusion(bf16[1232,1024]{1,0:T(8,128)(2,1)S(1)} %reshape.275, s32[1024]{0:T(1024)S(1)} %pad_clamp_fusion.1), kind=kCustom, calls=%fused_computation.3 | custom fusion | bytes 1312000 | tf_op jit(solution)/shard_map/gather | solution.py:153
  55.2 8.2 %convolution_convert_fusion = bf16[128,4096]{1,0:T(8,128)(2,1)} fusion(bf16[1,1024,4096]{2,1,0:T(8,128)(2,1)} %param.12, bf16[320,1024]{1,0:T(8,128)(2,1)S(1)} %gather_fusion.3, f32[1024]{0:T(1024)S(1)} %copy-done.1, f32[320]{0:T(512)S(1)} %add_rsqrt_fusion, s32[320]{0:T(512)S(1)} %add_select_fusion), kind=kOutput, calls=%fused_computation.16 | convolution fusion | flops 3033571328 | bytes 10099200 | tf_op jit(solution)/shard_map/dot_general | solution.py:171
  63.3 5.0 %all-to-all-start.2 = ((bf16[8,16,4096]{2,1,0:T(8,128)(2,1)}), bf16[8,16,4096]{2,1,0:T(8,128)(2,1)S(1)}, u32[]{:S(2)}, u32[]{:S(2)}) async-start(bf16[8,16,4096]{2,1,0:T(8,128)(2,1)} %bitcast.16), calls=%async_computation.2 | async-start | bytes 2097152 | tf_op jit(solution)/shard_map/all_to_all | solution.py:173
  68.4 0.9 fusion.23.hit_ref
  69.2 13.0 %all-to-all-done.2 = bf16[8,16,4096]{2,1,0:T(8,128)(2,1)S(1)} async-done(((bf16[8,16,4096]{2,1,0:T(8,128)(2,1)}), bf16[8,16,4096]{2,1,0:T(8,128)(2,1)S(1)}, u32[]{:S(2)}, u32[]{:S(2)}) %all-to-all-start.2) | async-done | bytes 1048608 | tf_op jit(solution)/shard_map/all_to_all | solution.py:173
  82.6 3.7 %collective-permute-start.2 = (bf16[16,4096]{1,0:T(8,128)(2,1)S(1)}, bf16[16,4096]{1,0:T(8,128)(2,1)S(1)}, u32[]{:S(2)}, u32[]{:S(2)}) collective-permute-start(bf16[16,4096]{1,0:T(8,128)(2,1)S(1)} %multiply_convert_fusion), channel_id=1, source_target_pairs={{0,3},{1,0},{2,1},{3,2},{4,7},{5,4},{6,5},{7,6},{8,11},{9,8},{10,9... | collective-permute-start | bytes 393224 | tf_op jit(solution)/shard_map/ppermute | solution.py:182
  86.3 1.0 collective-permute-start
  87.4 2.8 %collective-permute-done.2 = bf16[16,4096]{1,0:T(8,128)(2,1)S(1)} collective-permute-done((bf16[16,4096]{1,0:T(8,128)(2,1)S(1)}, bf16[16,4096]{1,0:T(8,128)(2,1)S(1)}, u32[]{:S(2)}, u32[]{:S(2)}) %collective-permute-start.2) | collective-permute-done | bytes 131104 | tf_op jit(solution)/shard_map/ppermute | solution.py:182
  90.2 7.6 %collective-permute-done.1 = bf16[16,4096]{1,0:T(8,128)(2,1)S(1)} collective-permute-done((bf16[16,4096]{1,0:T(8,128)(2,1)S(1)}, bf16[16,4096]{1,0:T(8,128)(2,1)S(1)}, u32[]{:S(2)}, u32[]{:S(2)}) %collective-permute-start.1) | collective-permute-done | bytes 131104 | tf_op jit(solution)/shard_map/ppermute | solution.py:182
  97.9 1.4 %gather_fusion.4 = bf16[4,16,4096]{2,1,0:T(8,128)(2,1)} fusion(bf16[4,16,4096]{2,1,0:T(8,128)(2,1)S(1)} %pad_maximum_fusion, s32[1024]{0:T(1024)S(1)} %pad_clamp_fusion), kind=kCustom, calls=%fused_computation.4 | custom fusion | bytes 1048592 | tf_op jit(solution)/shard_map/gather | solution.py:187
  99.3 12.4 %shard_map.103 = (f32[896,1]{1,0:T(8,128)}, bf16[896,64]{1,0:T(8,128)(2,1)}, f32[896,1]{1,0:T(8,128)}, bf16[64,4096]{1,0:T(8,128)(2,1)}) custom-call(bf16[896,4096]{1,0:T(8,128)(2,1)} %q_ref.1, bf16[64,4096]{1,0:T(8,128)(2,1)} %bitcast.39, bf16[896,64]{1,0:T(8,128)(2,1)} %fusion.23.hit_ref), custom_call_target="tpu_custom_call" | custom-call | flops 939524096 | bytes 7340032 | tf_op jit(solution)/shard_map/pallas_call | solution.py:71
  111.7 3.8 %all-to-all-start.3 = ((bf16[4,16,4096]{2,1,0:T(8,128)(2,1)}), bf16[4,16,4096]{2,1,0:T(8,128)(2,1)S(1)}, u32[]{:S(2)}, u32[]{:S(2)}) async-start(bf16[4,16,4096]{2,1,0:T(8,128)(2,1)} %bitcast.42), calls=%async_computation.3 | async-start | bytes 1048576 | tf_op jit(solution)/shard_map/all_to_all | solution.py:193
  115.5 1.8 %reduce.7 = f32[896]{0:T(1024)} reduce(f32[896,1]{1,0:T(8,128)} %get-tuple-element.7, f32[]{:T(128)} %constant.84), dimensions={1}, to_apply=%get-tuple-element.7.reduce_sub_computation | reduce | bytes 7172 | tf_op jit(solution)/shard_map/pallas_call | solution.py:71
  117.3 8.0 %shard_map.104 = bf16[896,4096]{1,0:T(8,128)(2,1)} custom-call(bf16[896,64]{1,0:T(8,128)(2,1)} %get-tuple-element.8.wb_ref, f32[896,1]{1,0:T(8,128)} %get-tuple-element.9.tot_ref, bf16[896,64]{1,0:T(8,128)(2,1)} %fusion.23.hit_ref, bf16[64,4096]{1,0:T(8,128)(2,1)} %bitcast.40), custom_call_target="tpu_custom_call" | custom-call | flops 939524096 | bytes 7340032 | tf_op jit(solution)/shard_map/pallas_call | solution.py:102
  125.3 4.2 %all-to-all-done.3 = bf16[4,16,4096]{2,1,0:T(8,128)(2,1)S(1)} async-done(((bf16[4,16,4096]{2,1,0:T(8,128)(2,1)}), bf16[4,16,4096]{2,1,0:T(8,128)(2,1)S(1)}, u32[]{:S(2)}, u32[]{:S(2)}) %all-to-all-start.3) | async-done | bytes 524320 | tf_op jit(solution)/shard_map/all_to_all | solution.py:193
  (39 shorter events, 8.8 us)
Async XLA Ops:
  5.9 9.6 %all-to-all-start = ((s32[8,1,154]{2,1,0:T(1,128)}), s32[8,1,154]{2,1,0:T(1,128)S(1)}, u32[]{:S(2)}, u32[]{:S(2)}) async-start(s32[8,1,154]{2,1,0:T(1,128)} %copy.18), calls=%async_computation | async-start | bytes 16384 | tf_op jit(solution)/shard_map/all_to_all | solution.py:142
  15.6 35.2 %all-to-all-start.1 = ((bf16[8,154,1024]{2,1,0:T(8,128)(2,1)}), bf16[8,154,1024]{2,1,0:T(8,128)(2,1)}, u32[]{:S(2)}, u32[]{:S(2)}) async-start(bf16[8,154,1024]{2,1,0:T(8,128)(2,1)} %bitcast.37), calls=%async_computation.1 | async-start | bytes 5242880 | tf_op jit(solution)/shard_map/all_to_all | solution.py:141
  30.5 24.6 %copy-start.1 = (f32[1024]{0:T(1024)S(1)}, f32[1024]{0:T(1024)}, u32[]{:S(2)}) copy-start(f32[1024]{0:T(1024)} %param.13) | copy-start | bytes 12292
  55.2 13.2 %copy-start = (s32[896]{0:T(1024)S(1)}, s32[896]{0:T(1024)}, u32[]{:S(2)}) copy-start(s32[896]{0:T(1024)} %param.15) | copy-start | bytes 10756
  63.3 18.9 %all-to-all-start.2 = ((bf16[8,16,4096]{2,1,0:T(8,128)(2,1)}), bf16[8,16,4096]{2,1,0:T(8,128)(2,1)S(1)}, u32[]{:S(2)}, u32[]{:S(2)}) async-start(bf16[8,16,4096]{2,1,0:T(8,128)(2,1)} %bitcast.16), calls=%async_computation.2 | async-start | bytes 2097152 | tf_op jit(solution)/shard_map/all_to_all | solution.py:173
  82.6 7.6 %collective-permute-start.2 = (bf16[16,4096]{1,0:T(8,128)(2,1)S(1)}, bf16[16,4096]{1,0:T(8,128)(2,1)S(1)}, u32[]{:S(2)}, u32[]{:S(2)}) collective-permute-start(bf16[16,4096]{1,0:T(8,128)(2,1)S(1)} %multiply_convert_fusion), channel_id=1, source_target_pairs={{0,3},{1,0},{2,1},{3,2},{4,7},{5,4},{6,5},{7,6},{8,11},{9,8},{10,9... | collective-permute-start | bytes 393224 | tf_op jit(solution)/shard_map/ppermute | solution.py:182
  86.3 11.6 %collective-permute-start.1 = (bf16[16,4096]{1,0:T(8,128)(2,1)S(1)}, bf16[16,4096]{1,0:T(8,128)(2,1)S(1)}, u32[]{:S(2)}, u32[]{:S(2)}) collective-permute-start(bf16[16,4096]{1,0:T(8,128)(2,1)S(1)} %multiply_convert_fusion), channel_id=1, source_target_pairs={{0,2},{1,3},{2,0},{3,1},{4,6},{5,7},{6,4},{7,5},{8,10},{9,11},{10,... | collective-permute-start | bytes 393224 | tf_op jit(solution)/shard_map/ppermute | solution.py:182
  86.3 11.6 %collective-permute-start = (bf16[16,4096]{1,0:T(8,128)(2,1)S(1)}, bf16[16,4096]{1,0:T(8,128)(2,1)S(1)}, u32[]{:S(2)}, u32[]{:S(2)}) collective-permute-start(bf16[16,4096]{1,0:T(8,128)(2,1)S(1)} %multiply_convert_fusion), channel_id=1, source_target_pairs={{0,1},{1,2},{2,3},{3,0},{4,5},{5,6},{6,7},{7,4},{8,9},{9,10},{10,1... | collective-permute-start | bytes 393224 | tf_op jit(solution)/shard_map/ppermute | solution.py:182
  111.7 17.9 %all-to-all-start.3 = ((bf16[4,16,4096]{2,1,0:T(8,128)(2,1)}), bf16[4,16,4096]{2,1,0:T(8,128)(2,1)S(1)}, u32[]{:S(2)}, u32[]{:S(2)}) async-start(bf16[4,16,4096]{2,1,0:T(8,128)(2,1)} %bitcast.42), calls=%async_computation.3 | async-start | bytes 1048576 | tf_op jit(solution)/shard_map/all_to_all | solution.py:193

commit v12 on v11

--- a/solution.py
+++ b/solution.py
@@ -175,16 +175,13 @@
 
     doc_unit = unit_rows(pooled)
     cycle_size = lax.axis_size("blk")
-    position = lax.axis_index("blk")
-    arrived = jnp.stack(
-        [doc_unit]
-        + [
-            lax.ppermute(doc_unit, "blk", [(i, (i + shift) % cycle_size) for i in range(cycle_size)])
-            for shift in range(1, cycle_size)
-        ]
-    )
-    arrival_of = (position - jnp.arange(cycle_size, dtype=jnp.int32)) % cycle_size
-    doc_piece = arrived[arrival_of].reshape(cycle_size * doc_unit.shape[0], emb_width)
+    doc_piece = lax.all_to_all(
+        jnp.broadcast_to(doc_unit[None], (cycle_size,) + doc_unit.shape),
+        "blk",
+        split_axis=0,
+        concat_axis=0,
+        tiled=True,
+    ).reshape(cycle_size * doc_unit.shape[0], emb_width)
     piece_rows = doc_piece.shape[0]
     hits = (positives[:, None] == jnp.arange(piece_rows, dtype=jnp.int32)[None, :]).astype(
         jnp.bfloat16

time: 131 us -> 135 us (1.031)
  the two profiles are of different devices: /device:TPU:2 before, /device:TPU:0 now
where the time goes in v12:
time: 135 us; the launch traced here: 134 us
  waiting for transfers between devices  38.7 us (29%)
  Pallas kernels  20.4 us (15%)
  starting transfers between devices  17.9 us (13%)
  blocking collectives  17.8 us (13%)
  local copies, waits for them, and re-layouts  17.4 us (13%)
  other arithmetic  13.1 us (10%)
  matrix products  7.21 us (5%)
  between operations  1.44 us (1%)
    all_to_all x1, waiting for transfers between devices, on_device(): lax.all_to_all(send_rows, 'dp', split_axis=0, concat_axis=0, tiled=True)  21.7 us
    all_to_all x1, blocking collectives, on_device(): lax.all_to_all(partial, 'dp', split_axis=0, concat_axis=0, tiled=True)  17.8 us
    all_to_all x1, waiting for transfers between devices, on_device(): lax.all_to_all(jnp.broadcast_to(doc_unit[None], (cycle_size,) + doc_unit....  13 us
    pallas_call x1, Pallas kernels, scores(): pl.pallas_call(score_kernel, grid=(rows // tile,), in_specs=[pl.BlockSpec...  12.4 us
    pallas_call x1, Pallas kernels, query_grads(): pl.pallas_call(query_grad_kernel, grid=(rows // tile,), in_specs=[pl.Bloc...  8.03 us
    dot_general x1, matrix products, on_device(): partial = jnp.dot(selector, embedded, preferred_element_type=jnp.float32)  7.21 us
    gather x3, other arithmetic, on_device(): slot_of = source_of * capacity + packed_index - starts[source_of]  5.18 us
    all_to_all x1, starting transfers between devices, on_device(): lax.all_to_all(send_ids, 'dp', split_axis=0, concat_axis=0, tiled=True)  5.17 us
  transfers between devices with their start and end apart: 4, of which 3 were waited for; matrix products, arithmetic and copies ran while one was open for 14% of the time, Pallas kernels for 6%

profile of v12, /device:TPU:0, one launch (start us, length us, event | category | flops | bytes accessed | tf_op | source)
XLA Modules:
  0.0 133.9 jit_solution(9910701984375320101)
XLA Ops:
  0.6 1.2 slice.9
  3.8 0.8 reshape.208
  5.9 5.2 %all-to-all-start = ((s32[8,1,154]{2,1,0:T(1,128)}), s32[8,1,154]{2,1,0:T(1,128)S(1)}, u32[]{:S(2)}, u32[]{:S(2)}) async-start(s32[8,1,154]{2,1,0:T(1,128)} %copy.18), calls=%async_computation | async-start | bytes 16384 | tf_op jit(solution)/shard_map/all_to_all | solution.py:142
  11.1 3.2 %copy.19 = bf16[160,8,1024]{2,0,1:T(8,128)(2,1)S(1)} copy(bf16[160,8,1024]{2,1,0:T(8,128)(2,1)} %bitcast.32) | data formatting | bytes 5242880 | tf_op jit(solution)/shard_map/reshape | solution.py:132
  14.3 2.2 %gather_fusion.2 = bf16[8,160,1024]{2,1,0:T(8,128)(2,1)} fusion(bf16[160,8,1024]{2,0,1:T(8,128)(2,1)S(1)} %copy.19, s32[1024]{0:T(1024)S(1)} %pad_clamp_fusion.1), kind=kCustom, calls=%fused_computation.2 | custom fusion | bytes 5242912 | tf_op jit(solution)/shard_map/jit(_take)/gather | solution.py:133
  16.5 4.4 %all-to-all-start.1 = ((bf16[8,154,1024]{2,1,0:T(8,128)(2,1)}), bf16[8,154,1024]{2,1,0:T(8,128)(2,1)}, u32[]{:S(2)}, u32[]{:S(2)}) async-start(bf16[8,154,1024]{2,1,0:T(8,128)(2,1)} %bitcast.28), calls=%async_computation.1 | async-start | bytes 5242880 | tf_op jit(solution)/shard_map/all_to_all | solution.py:141
  20.9 0.8 fusion.37
  22.7 4.5 %fusion.28 = (s32[320]{0:T(512)S(1)}, s32[320,1]{0,1:T(1,128)S(1)}) fusion(s32[]{:T(128)} %bitcast.7, s32[]{:T(128)} %bitcast.8, s32[]{:T(128)} %bitcast.9, s32[]{:T(128)} %bitcast.10, s32[]{:T(128)} %bitcast.11, s32[]{:T(128)} %bitcast.13, s32[]{:T(128)} %bitcast.12, s32[320]{0:T(512)S(1)} %get-tuple-element.17, s32[320]{0:T(512)S(1)} %get-tuple-element.16), kind=kLoop, calls=%fused_computation.60 | loop fusion | flops 4480 | bytes 5148 | tf_op jit(solution)/shard_map/gather | solution.py:150
  28.6 2.2 %gather_fusion.1 = s32[320]{0:T(512)S(1)} fusion(s32[1232]{0:T(1024)S(1)} %reshape.211, s32[1024]{0:T(1024)S(1)} %pad_clamp_fusion), kind=kCustom, calls=%fused_computation.1 | custom fusion | bytes 3840 | tf_op jit(solution)/shard_map/gather | solution.py:155
  31.5 21.7 %all-to-all-done.1 = bf16[8,154,1024]{2,1,0:T(8,128)(2,1)} async-done(((bf16[8,154,1024]{2,1,0:T(8,128)(2,1)}), bf16[8,154,1024]{2,1,0:T(8,128)(2,1)}, u32[]{:S(2)}, u32[]{:S(2)}) %all-to-all-start.1) | async-done | bytes 2523168 | tf_op jit(solution)/shard_map/all_to_all | solution.py:141
  53.2 2.1 %reshape.213 = bf16[1232,1024]{1,0:T(8,128)(2,1)S(1)} reshape(bf16[8,154,1024]{2,1,0:T(8,128)(2,1)} %all-to-all-done.1) | data formatting | bytes 5046272 | tf_op jit(solution)/shard_map/reshape | solution.py:153
  55.2 2.1 %gather_fusion.3 = bf16[320,1024]{1,0:T(8,128)(2,1)S(1)} fusion(bf16[1232,1024]{1,0:T(8,128)(2,1)S(1)} %reshape.213, s32[1024]{0:T(1024)S(1)} %pad_clamp_fusion), kind=kCustom, calls=%fused_computation.3 | custom fusion | bytes 1312000 | tf_op jit(solution)/shard_map/gather | solution.py:153
  57.6 7.2 %convolution_convert_fusion = bf16[128,4096]{1,0:T(8,128)(2,1)S(1)} fusion(bf16[1,1024,4096]{2,1,0:T(8,128)(2,1)} %param.12, bf16[320,1024]{1,0:T(8,128)(2,1)S(1)} %gather_fusion.3, f32[1024]{0:T(1024)S(1)} %copy-done.2, f32[320]{0:T(512)S(1)} %add_rsqrt_fusion, s32[320]{0:T(512)S(1)} %add_select_fusion), kind=kOutput, calls=%fused_computation.15 | convolution fusion | flops 3033571328 | bytes 10099200 | tf_op jit(solution)/shard_map/dot_general | solution.py:171
  64.8 17.8 %all_to_all.29 = bf16[8,16,4096]{2,1,0:T(8,128)(2,1)S(1)} all-to-all(bf16[8,16,4096]{2,1,0:T(8,128)(2,1)S(1)} %bitcast.33), channel_id=1, replica_groups=mesh['dp'=8,'blk'=4] {'dp'}, dimensions={0} | all-to-all | bytes 2097152 | tf_op jit(solution)/shard_map/all_to_all | solution.py:173
  83.0 0.8 broadcast_in_dim.14
  83.8 4.9 %all-to-all-start.3 = ((bf16[4,16,4096]{2,1,0:T(8,128)(2,1)}), bf16[4,16,4096]{2,1,0:T(8,128)(2,1)S(1)}, u32[]{:S(2)}, u32[]{:S(2)}) async-start(bf16[4,16,4096]{2,1,0:T(8,128)(2,1)} %broadcast_in_dim.14), calls=%async_computation.3 | async-start | bytes 1048576 | tf_op jit(solution)/shard_map/all_to_all | solution.py:178
  88.7 0.9 fusion.23.hit_ref
  89.6 13.0 %all-to-all-done.3 = bf16[4,16,4096]{2,1,0:T(8,128)(2,1)S(1)} async-done(((bf16[4,16,4096]{2,1,0:T(8,128)(2,1)}), bf16[4,16,4096]{2,1,0:T(8,128)(2,1)S(1)}, u32[]{:S(2)}, u32[]{:S(2)}) %all-to-all-start.3) | async-done | bytes 524320 | tf_op jit(solution)/shard_map/all_to_all | solution.py:178
  102.5 0.8 copy-done
  103.3 12.4 %shard_map.103 = (f32[896,1]{1,0:T(8,128)}, bf16[896,64]{1,0:T(8,128)(2,1)}, f32[896,1]{1,0:T(8,128)}, bf16[64,4096]{1,0:T(8,128)(2,1)}) custom-call(bf16[896,4096]{1,0:T(8,128)(2,1)} %q_ref.1, bf16[64,4096]{1,0:T(8,128)(2,1)} %bitcast.30, bf16[896,64]{1,0:T(8,128)(2,1)} %fusion.23.hit_ref), custom_call_target="tpu_custom_call" | custom-call | flops 939524096 | bytes 7340032 | tf_op jit(solution)/shard_map/pallas_call | solution.py:71
  115.7 3.5 %all-to-all-start.4 = ((bf16[4,16,4096]{2,1,0:T(8,128)(2,1)}), bf16[4,16,4096]{2,1,0:T(8,128)(2,1)S(1)}, u32[]{:S(2)}, u32[]{:S(2)}) async-start(bf16[4,16,4096]{2,1,0:T(8,128)(2,1)} %bitcast.34), calls=%async_computation.4 | async-start | bytes 1048576 | tf_op jit(solution)/shard_map/all_to_all | solution.py:190
  119.2 1.8 %reduce.7 = f32[896]{0:T(1024)} reduce(f32[896,1]{1,0:T(8,128)} %get-tuple-element.7, f32[]{:T(128)} %constant.64), dimensions={1}, to_apply=%get-tuple-element.7.reduce_sub_computation | reduce | bytes 7172 | tf_op jit(solution)/shard_map/pallas_call | solution.py:71
  121.0 8.0 %shard_map.104 = bf16[896,4096]{1,0:T(8,128)(2,1)} custom-call(bf16[896,64]{1,0:T(8,128)(2,1)} %get-tuple-element.8.wb_ref, f32[896,1]{1,0:T(8,128)} %get-tuple-element.9.tot_ref, bf16[896,64]{1,0:T(8,128)(2,1)} %fusion.23.hit_ref, bf16[64,4096]{1,0:T(8,128)(2,1)} %bitcast.31), custom_call_target="tpu_custom_call" | custom-call | flops 939524096 | bytes 7340032 | tf_op jit(solution)/shard_map/pallas_call | solution.py:102
  129.0 4.1 %all-to-all-done.4 = bf16[4,16,4096]{2,1,0:T(8,128)(2,1)S(1)} async-done(((bf16[4,16,4096]{2,1,0:T(8,128)(2,1)}), bf16[4,16,4096]{2,1,0:T(8,128)(2,1)S(1)}, u32[]{:S(2)}, u32[]{:S(2)}) %all-to-all-start.4) | async-done | bytes 524320 | tf_op jit(solution)/shard_map/all_to_all | solution.py:190
  (32 shorter events, 7.1 us)
Async XLA Ops:
  5.9 10.6 %all-to-all-start = ((s32[8,1,154]{2,1,0:T(1,128)}), s32[8,1,154]{2,1,0:T(1,128)S(1)}, u32[]{:S(2)}, u32[]{:S(2)}) async-start(s32[8,1,154]{2,1,0:T(1,128)} %copy.18), calls=%async_computation | async-start | bytes 16384 | tf_op jit(solution)/shard_map/all_to_all | solution.py:142
  16.5 36.7 %all-to-all-start.1 = ((bf16[8,154,1024]{2,1,0:T(8,128)(2,1)}), bf16[8,154,1024]{2,1,0:T(8,128)(2,1)}, u32[]{:S(2)}, u32[]{:S(2)}) async-start(bf16[8,154,1024]{2,1,0:T(8,128)(2,1)} %bitcast.28), calls=%async_computation.1 | async-start | bytes 5242880 | tf_op jit(solution)/shard_map/all_to_all | solution.py:141
  31.5 26.1 %copy-start.2 = (f32[1024]{0:T(1024)S(1)}, f32[1024]{0:T(1024)}, u32[]{:S(2)}) copy-start(f32[1024]{0:T(1024)} %param.13) | copy-start | bytes 12292
  64.8 23.9 %copy-start.1 = (s32[896]{0:T(1024)S(1)}, s32[896]{0:T(1024)}, u32[]{:S(2)}) copy-start(s32[896]{0:T(1024)} %param.15) | copy-start | bytes 10756
  83.8 18.7 %all-to-all-start.3 = ((bf16[4,16,4096]{2,1,0:T(8,128)(2,1)}), bf16[4,16,4096]{2,1,0:T(8,128)(2,1)S(1)}, u32[]{:S(2)}, u32[]{:S(2)}) async-start(bf16[4,16,4096]{2,1,0:T(8,128)(2,1)} %broadcast_in_dim.14), calls=%async_computation.3 | async-start | bytes 1048576 | tf_op jit(solution)/shard_map/all_to_all | solution.py:178
  102.5 0.8 copy-start
  115.7 17.4 %all-to-all-start.4 = ((bf16[4,16,4096]{2,1,0:T(8,128)(2,1)}), bf16[4,16,4096]{2,1,0:T(8,128)(2,1)S(1)}, u32[]{:S(2)}, u32[]{:S(2)}) async-start(bf16[4,16,4096]{2,1,0:T(8,128)(2,1)} %bitcast.34), calls=%async_computation.4 | async-start | bytes 1048576 | tf_op jit(solution)/shard_map/all_to_all | solution.py:190

commit v13 on v11

--- a/solution.py
+++ b/solution.py
@@ -150,7 +150,14 @@
     slot_of = source_of * capacity + packed_index - starts[source_of]
     packed_live = packed_index < jnp.sum(got_counts)
     slot_of = jnp.where(packed_live, slot_of, 0)
-    packed = got_rows.reshape(groups * capacity, hidden_width)[slot_of]
+    packer = (
+        (jnp.arange(groups, dtype=jnp.int32)[None, :, None] == source_of[:, None, None])
+        & (jnp.arange(capacity, dtype=jnp.int32)[None, None, :] == (packed_index - starts[source_of])[:, None, None])
+        & packed_live[:, None, None]
+    ).astype(jnp.bfloat16)
+    packed = lax.dot_general(
+        packer, got_rows, (((1, 2), (0, 1)), ((), ())), preferred_element_type=jnp.float32
+    ).astype(jnp.bfloat16)
     packed_key = jnp.where(
         packed_live, source_of * SESS_DEV + got_ids.reshape(groups * capacity)[slot_of], -1
     )

time: 131 us -> 128 us (0.977)
  local copies, waits for them, and re-layouts: 17.1 us -> 13 us
    gather x1 -> x0, local copies, waits for them, and re-layouts: 2.09 us -> none  [on_device(): packed = got_rows.reshape(groups * capacity, hidden_width)[slot_of]]
    reshape x1 -> x0, local copies, waits for them, and re-layouts: 2.06 us -> none  [on_device(): packed = got_rows.reshape(groups * capacity, hidden_width)[slot_of]]
    gather x3 -> x2, other arithmetic: 5.18 us -> 4.34 us  [on_device(): slot_of = source_of * capacity + packed_index - starts[source_of]]
  transfers between devices with their start and end apart: 7 -> 7, of which waited for: 5 -> 5; matrix products, arithmetic and copies ran while one was open for 14% -> 15% of each run, Pallas kernels for 6% -> 6%
where the time goes in v13:
time: 128 us; the launch traced here: 127 us
  waiting for transfers between devices  47.3 us (37%)
  starting transfers between devices  21.9 us (17%)
  Pallas kernels  20.4 us (16%)
  other arithmetic  13.5 us (11%)
  local copies, waits for them, and re-layouts  13 us (10%)
  matrix products  9.35 us (7%)
  between operations  1.44 us (1%)
    all_to_all x1, waiting for transfers between devices, on_device(): lax.all_to_all(send_rows, 'dp', split_axis=0, concat_axis=0, tiled=True)  19.6 us
    all_to_all x1, waiting for transfers between devices, on_device(): lax.all_to_all(partial, 'dp', split_axis=0, concat_axis=0, tiled=True)  13 us
    pallas_call x1, Pallas kernels, scores(): pl.pallas_call(score_kernel, grid=(rows // tile,), in_specs=[pl.BlockSpec...  12.4 us
    ppermute x3, waiting for transfers between devices, on_device(): lax.ppermute(doc_unit, 'blk', [(i, (i + shift) % cycle_size) for i in ran...  10.5 us
    dot_general x1, matrix products, on_device(): partial = jnp.dot(selector, embedded, preferred_element_type=jnp.float32)  8.18 us
    pallas_call x1, Pallas kernels, query_grads(): pl.pallas_call(query_grad_kernel, grid=(rows // tile,), in_specs=[pl.Bloc...  8.02 us
    all_to_all x1, starting transfers between devices, on_device(): lax.all_to_all(partial, 'dp', split_axis=0, concat_axis=0, tiled=True)  4.98 us
    ppermute x3, starting transfers between devices, on_device(): lax.ppermute(doc_unit, 'blk', [(i, (i + shift) % cycle_size) for i in ran...  4.67 us
  transfers between devices with their start and end apart: 7, of which 5 were waited for; matrix products, arithmetic and copies ran while one was open for 15% of the time, Pallas kernels for 6%

profile of v13, /device:TPU:2, one launch (start us, length us, event | category | flops | bytes accessed | tf_op | source)
XLA Modules:
  0.0 126.9 jit_solution(3103254399446830847)
XLA Ops:
  0.6 1.2 slice.9
  3.8 0.8 reshape.326
  5.9 4.3 %all-to-all-start = ((s32[8,1,154]{2,1,0:T(1,128)}), s32[8,1,154]{2,1,0:T(1,128)S(1)}, u32[]{:S(2)}, u32[]{:S(2)}) async-start(s32[8,1,154]{2,1,0:T(1,128)} %copy.18), calls=%async_computation | async-start | bytes 16384 | tf_op jit(solution)/shard_map/all_to_all | solution.py:142
  10.2 3.2 %copy.19 = bf16[160,8,1024]{2,0,1:T(8,128)(2,1)S(1)} copy(bf16[160,8,1024]{2,1,0:T(8,128)(2,1)} %bitcast.46) | data formatting | bytes 5242880 | tf_op jit(solution)/shard_map/reshape | solution.py:132
  13.4 2.2 %gather_fusion.2 = bf16[8,160,1024]{2,1,0:T(8,128)(2,1)} fusion(bf16[160,8,1024]{2,0,1:T(8,128)(2,1)S(1)} %copy.19, s32[1024]{0:T(1024)S(1)} %pad_clamp_fusion.2), kind=kCustom, calls=%fused_computation.2 | custom fusion | bytes 5242912 | tf_op jit(solution)/shard_map/jit(_take)/gather | solution.py:133
  15.6 4.2 %all-to-all-start.1 = ((bf16[8,154,1024]{2,1,0:T(8,128)(2,1)}), bf16[8,154,1024]{2,1,0:T(8,128)(2,1)S(1)}, u32[]{:S(2)}, u32[]{:S(2)}) async-start(bf16[8,154,1024]{2,1,0:T(8,128)(2,1)} %bitcast.42), calls=%async_computation.1 | async-start | bytes 5242880 | tf_op jit(solution)/shard_map/all_to_all | solution.py:141
  21.6 4.3 %fusion.41 = (s32[320]{0:T(512)S(1)}, s32[320,1]{0,1:T(1,128)S(1)}) fusion(s32[]{:T(128)} %bitcast.7, s32[]{:T(128)} %bitcast.8, s32[]{:T(128)} %bitcast.9, s32[]{:T(128)} %bitcast.10, s32[]{:T(128)} %bitcast.11, s32[]{:T(128)} %bitcast.13, s32[]{:T(128)} %bitcast.12, s32[320]{0:T(512)S(1)} %get-tuple-element.19, s32[320]{0:T(512)S(1)} %get-tuple-element.18), kind=kLoop, calls=%fused_computation.79 | loop fusion | flops 4480 | bytes 5148 | tf_op jit(solution)/shard_map/gather | solution.py:150
  27.3 2.2 %gather_fusion.1 = s32[320]{0:T(512)S(1)} fusion(s32[1232]{0:T(1024)S(1)} %reshape.329, s32[1024]{0:T(1024)S(1)} %pad_clamp_fusion.1), kind=kCustom, calls=%fused_computation.1 | custom fusion | bytes 3840 | tf_op jit(solution)/shard_map/gather | solution.py:162
  30.9 19.6 %all-to-all-done.1 = bf16[8,154,1024]{2,1,0:T(8,128)(2,1)S(1)} async-done(((bf16[8,154,1024]{2,1,0:T(8,128)(2,1)}), bf16[8,154,1024]{2,1,0:T(8,128)(2,1)S(1)}, u32[]{:S(2)}, u32[]{:S(2)}) %all-to-all-start.1) | async-done | bytes 2523168 | tf_op jit(solution)/shard_map/all_to_all | solution.py:141
  50.5 1.2 fusion.23
  51.7 8.2 %convolution_convert_fusion = bf16[128,4096]{1,0:T(8,128)(2,1)} fusion(bf16[1,1024,4096]{2,1,0:T(8,128)(2,1)} %param.12, bf16[320,1024]{1,0:T(8,128)(2,1)S(1)} %get-tuple-element.29, f32[1024]{0:T(1024)S(1)} %copy-done.1, f32[320]{0:T(512)S(1)} %add_rsqrt_fusion, s32[320]{0:T(512)S(1)} %add_select_fusion), kind=kOutput, calls=%fused_computation.15 | convolution fusion | flops 3033571328 | bytes 10099200 | tf_op jit(solution)/shard_map/dot_general | solution.py:178
  59.9 5.0 %all-to-all-start.2 = ((bf16[8,16,4096]{2,1,0:T(8,128)(2,1)}), bf16[8,16,4096]{2,1,0:T(8,128)(2,1)S(1)}, u32[]{:S(2)}, u32[]{:S(2)}) async-start(bf16[8,16,4096]{2,1,0:T(8,128)(2,1)} %bitcast.17), calls=%async_computation.2 | async-start | bytes 2097152 | tf_op jit(solution)/shard_map/all_to_all | solution.py:180
  64.9 0.9 fusion.35.hit_ref
  65.8 13.0 %all-to-all-done.2 = bf16[8,16,4096]{2,1,0:T(8,128)(2,1)S(1)} async-done(((bf16[8,16,4096]{2,1,0:T(8,128)(2,1)}), bf16[8,16,4096]{2,1,0:T(8,128)(2,1)S(1)}, u32[]{:S(2)}, u32[]{:S(2)}) %all-to-all-start.2) | async-done | bytes 1048608 | tf_op jit(solution)/shard_map/all_to_all | solution.py:180
  79.2 3.7 %collective-permute-start.2 = (bf16[16,4096]{1,0:T(8,128)(2,1)S(1)}, bf16[16,4096]{1,0:T(8,128)(2,1)S(1)}, u32[]{:S(2)}, u32[]{:S(2)}) collective-permute-start(bf16[16,4096]{1,0:T(8,128)(2,1)S(1)} %multiply_convert_fusion), channel_id=1, source_target_pairs={{0,3},{1,0},{2,1},{3,2},{4,7},{5,4},{6,5},{7,6},{8,11},{9,8},{10,9... | collective-permute-start | bytes 393224 | tf_op jit(solution)/shard_map/ppermute | solution.py:189
  82.9 1.0 collective-permute-start
  84.0 2.8 %collective-permute-done.2 = bf16[16,4096]{1,0:T(8,128)(2,1)S(1)} collective-permute-done((bf16[16,4096]{1,0:T(8,128)(2,1)S(1)}, bf16[16,4096]{1,0:T(8,128)(2,1)S(1)}, u32[]{:S(2)}, u32[]{:S(2)}) %collective-permute-start.2) | collective-permute-done | bytes 131104 | tf_op jit(solution)/shard_map/ppermute | solution.py:189
  86.8 7.6 %collective-permute-done.1 = bf16[16,4096]{1,0:T(8,128)(2,1)S(1)} collective-permute-done((bf16[16,4096]{1,0:T(8,128)(2,1)S(1)}, bf16[16,4096]{1,0:T(8,128)(2,1)S(1)}, u32[]{:S(2)}, u32[]{:S(2)}) %collective-permute-start.1) | collective-permute-done | bytes 131104 | tf_op jit(solution)/shard_map/ppermute | solution.py:189
  94.5 1.4 %gather_fusion.3 = bf16[4,16,4096]{2,1,0:T(8,128)(2,1)} fusion(bf16[4,16,4096]{2,1,0:T(8,128)(2,1)S(1)} %pad_maximum_fusion, s32[1024]{0:T(1024)S(1)} %pad_clamp_fusion), kind=kCustom, calls=%fused_computation.3 | custom fusion | bytes 1048592 | tf_op jit(solution)/shard_map/gather | solution.py:194
  95.9 12.4 %shard_map.103 = (f32[896,1]{1,0:T(8,128)}, bf16[896,64]{1,0:T(8,128)(2,1)}, f32[896,1]{1,0:T(8,128)}, bf16[64,4096]{1,0:T(8,128)(2,1)}) custom-call(bf16[896,4096]{1,0:T(8,128)(2,1)} %q_ref.1, bf16[64,4096]{1,0:T(8,128)(2,1)} %bitcast.44, bf16[896,64]{1,0:T(8,128)(2,1)} %fusion.35.hit_ref), custom_call_target="tpu_custom_call" | custom-call | flops 939524096 | bytes 7340032 | tf_op jit(solution)/shard_map/pallas_call | solution.py:71
  108.3 3.8 %all-to-all-start.3 = ((bf16[4,16,4096]{2,1,0:T(8,128)(2,1)}), bf16[4,16,4096]{2,1,0:T(8,128)(2,1)S(1)}, u32[]{:S(2)}, u32[]{:S(2)}) async-start(bf16[4,16,4096]{2,1,0:T(8,128)(2,1)} %bitcast.47), calls=%async_computation.3 | async-start | bytes 1048576 | tf_op jit(solution)/shard_map/all_to_all | solution.py:200
  112.1 1.8 %reduce.7 = f32[896]{0:T(1024)} reduce(f32[896,1]{1,0:T(8,128)} %get-tuple-element.7, f32[]{:T(128)} %constant.84), dimensions={1}, to_apply=%get-tuple-element.7.reduce_sub_computation | reduce | bytes 7172 | tf_op jit(solution)/shard_map/pallas_call | solution.py:71
  113.9 8.0 %shard_map.104 = bf16[896,4096]{1,0:T(8,128)(2,1)} custom-call(bf16[896,64]{1,0:T(8,128)(2,1)} %get-tuple-element.8.wb_ref, f32[896,1]{1,0:T(8,128)} %get-tuple-element.9.tot_ref, bf16[896,64]{1,0:T(8,128)(2,1)} %fusion.35.hit_ref, bf16[64,4096]{1,0:T(8,128)(2,1)} %bitcast.45), custom_call_target="tpu_custom_call" | custom-call | flops 939524096 | bytes 7340032 | tf_op jit(solution)/shard_map/pallas_call | solution.py:102
  121.9 4.2 %all-to-all-done.3 = bf16[4,16,4096]{2,1,0:T(8,128)(2,1)S(1)} async-done(((bf16[4,16,4096]{2,1,0:T(8,128)(2,1)}), bf16[4,16,4096]{2,1,0:T(8,128)(2,1)S(1)}, u32[]{:S(2)}, u32[]{:S(2)}) %all-to-all-start.3) | async-done | bytes 524320 | tf_op jit(solution)/shard_map/all_to_all | solution.py:200
  (40 shorter events, 8.5 us)
Async XLA Ops:
  5.9 9.6 %all-to-all-start = ((s32[8,1,154]{2,1,0:T(1,128)}), s32[8,1,154]{2,1,0:T(1,128)S(1)}, u32[]{:S(2)}, u32[]{:S(2)}) async-start(s32[8,1,154]{2,1,0:T(1,128)} %copy.18), calls=%async_computation | async-start | bytes 16384 | tf_op jit(solution)/shard_map/all_to_all | solution.py:142
  15.6 35.0 %all-to-all-start.1 = ((bf16[8,154,1024]{2,1,0:T(8,128)(2,1)}), bf16[8,154,1024]{2,1,0:T(8,128)(2,1)S(1)}, u32[]{:S(2)}, u32[]{:S(2)}) async-start(bf16[8,154,1024]{2,1,0:T(8,128)(2,1)} %bitcast.42), calls=%async_computation.1 | async-start | bytes 5242880 | tf_op jit(solution)/shard_map/all_to_all | solution.py:141
  30.9 20.8 %copy-start.1 = (f32[1024]{0:T(1024)S(1)}, f32[1024]{0:T(1024)}, u32[]{:S(2)}) copy-start(f32[1024]{0:T(1024)} %param.13) | copy-start | bytes 12292
  51.7 13.2 %copy-start = (s32[896]{0:T(1024)S(1)}, s32[896]{0:T(1024)}, u32[]{:S(2)}) copy-start(s32[896]{0:T(1024)} %param.15) | copy-start | bytes 10756
  59.9 18.9 %all-to-all-start.2 = ((bf16[8,16,4096]{2,1,0:T(8,128)(2,1)}), bf16[8,16,4096]{2,1,0:T(8,128)(2,1)S(1)}, u32[]{:S(2)}, u32[]{:S(2)}) async-start(bf16[8,16,4096]{2,1,0:T(8,128)(2,1)} %bitcast.17), calls=%async_computation.2 | async-start | bytes 2097152 | tf_op jit(solution)/shard_map/all_to_all | solution.py:180
  79.2 7.6 %collective-permute-start.2 = (bf16[16,4096]{1,0:T(8,128)(2,1)S(1)}, bf16[16,4096]{1,0:T(8,128)(2,1)S(1)}, u32[]{:S(2)}, u32[]{:S(2)}) collective-permute-start(bf16[16,4096]{1,0:T(8,128)(2,1)S(1)} %multiply_convert_fusion), channel_id=1, source_target_pairs={{0,3},{1,0},{2,1},{3,2},{4,7},{5,4},{6,5},{7,6},{8,11},{9,8},{10,9... | collective-permute-start | bytes 393224 | tf_op jit(solution)/shard_map/ppermute | solution.py:189
  82.9 11.6 %collective-permute-start.1 = (bf16[16,4096]{1,0:T(8,128)(2,1)S(1)}, bf16[16,4096]{1,0:T(8,128)(2,1)S(1)}, u32[]{:S(2)}, u32[]{:S(2)}) collective-permute-start(bf16[16,4096]{1,0:T(8,128)(2,1)S(1)} %multiply_convert_fusion), channel_id=1, source_target_pairs={{0,2},{1,3},{2,0},{3,1},{4,6},{5,7},{6,4},{7,5},{8,10},{9,11},{10,... | collective-permute-start | bytes 393224 | tf_op jit(solution)/shard_map/ppermute | solution.py:189
  82.9 11.6 %collective-permute-start = (bf16[16,4096]{1,0:T(8,128)(2,1)S(1)}, bf16[16,4096]{1,0:T(8,128)(2,1)S(1)}, u32[]{:S(2)}, u32[]{:S(2)}) collective-permute-start(bf16[16,4096]{1,0:T(8,128)(2,1)S(1)} %multiply_convert_fusion), channel_id=1, source_target_pairs={{0,1},{1,2},{2,3},{3,0},{4,5},{5,6},{6,7},{7,4},{8,9},{9,10},{10,1... | collective-permute-start | bytes 393224 | tf_op jit(solution)/shard_map/ppermute | solution.py:189
  108.3 17.9 %all-to-all-start.3 = ((bf16[4,16,4096]{2,1,0:T(8,128)(2,1)}), bf16[4,16,4096]{2,1,0:T(8,128)(2,1)S(1)}, u32[]{:S(2)}, u32[]{:S(2)}) async-start(bf16[4,16,4096]{2,1,0:T(8,128)(2,1)} %bitcast.47), calls=%async_computation.3 | async-start | bytes 1048576 | tf_op jit(solution)/shard_map/all_to_all | solution.py:200

commit v14 on v13

--- a/solution.py
+++ b/solution.py
@@ -36,10 +36,7 @@
     def _():
         acc_ref[...] = jnp.zeros_like(acc_ref)
 
-    widened = q_ref[...].astype(jnp.float32)
-    query_unit = (
-        widened * lax.rsqrt(jnp.sum(widened * widened, axis=-1, keepdims=True) + epsilon)
-    ).astype(jnp.bfloat16)
+    query_unit = q_ref[...]
     logits = logit_scale * contract_rows(query_unit, d_ref[...])
     weights = jnp.exp(logits)
     totals = jnp.sum(weights, axis=1, keepdims=True)
@@ -58,6 +55,27 @@
         gd_ref[...] = acc_ref[...].astype(jnp.bfloat16)
 
 
+def unit_query_kernel(q_ref, qu_ref):
+    widened = q_ref[...].astype(jnp.float32)
+    qu_ref[...] = (
+        widened * lax.rsqrt(jnp.sum(widened * widened, axis=-1, keepdims=True) + epsilon)
+    ).astype(jnp.bfloat16)
+
+
+def unit_queries(queries, tile=128):
+    rows, width = queries.shape
+    return pl.pallas_call(
+        unit_query_kernel,
+        grid=(rows // tile,),
+        in_specs=[pl.BlockSpec((tile, width), lambda i: (i, 0))],
+        out_specs=pl.BlockSpec((tile, width), lambda i: (i, 0)),
+        out_shape=jax.ShapeDtypeStruct((rows, width), jnp.bfloat16),
+        cost_estimate=pl.CostEstimate(
+            flops=4 * rows * width, transcendentals=rows, bytes_accessed=4 * rows * width
+        ),
+    )(queries)
+
+
 def query_grad_kernel(wb_ref, tot_ref, hit_ref, d_ref, gq_ref):
     docs = d_ref[...]
     numerator = jnp.dot(wb_ref[...], docs, preferred_element_type=jnp.float32)
@@ -139,6 +157,7 @@
         row_of < count, jnp.swapaxes(jnp.take(ids_by_lane, lane_of, axis=1, mode="clip"), 0, 1)[:, :capacity], -1
     )
     got_rows = lax.all_to_all(send_rows, "dp", split_axis=0, concat_axis=0, tiled=True)
+    got_rows, queries = lax.optimization_barrier((got_rows, queries))
     got_ids = lax.all_to_all(send_ids, "dp", split_axis=0, concat_axis=0, tiled=True)
 
     got_counts = jnp.sum((got_ids >= 0).astype(jnp.int32), axis=1)
@@ -181,6 +200,7 @@
     pooled = jnp.sum(returned.astype(jnp.float32), axis=0)
 
     doc_unit = unit_rows(pooled)
+    query_unit = unit_queries(queries)
     cycle_size = lax.axis_size("blk")
     position = lax.axis_index("blk")
     arrived = jnp.stack(
@@ -196,7 +216,7 @@
     hits = (positives[:, None] == jnp.arange(piece_rows, dtype=jnp.int32)[None, :]).astype(
         jnp.bfloat16
     )
-    loss_col, weights, totals, grad_part = scores(queries, doc_piece, hits)
+    loss_col, weights, totals, grad_part = scores(query_unit, doc_piece, hits)
     grad_terms = lax.all_to_all(
         grad_part.reshape(cycle_size, doc_unit.shape[0], emb_width),
         "blk",

time: 128 us -> 127 us (level)
  waiting for transfers between devices: 47.3 us -> 37.4 us
  Pallas kernels: 20.4 us -> 28.8 us
    all_to_all x1, waiting for transfers between devices: 13 us -> 3.1 us  [on_device(): lax.all_to_all(partial, 'dp', split_axis=0, concat_axis=0, tiled=True)]
    pallas_call x0 -> x1, Pallas kernels: none -> 9.9 us  [unit_queries(): pl.pallas_call(unit_query_kernel, grid=(rows // tile,), in_specs=[pl.Bloc...]
    pallas_call x1, Pallas kernels: 12.4 us -> 10.9 us  [scores(): pl.pallas_call(score_kernel, grid=(rows // tile,), in_specs=[pl.BlockSpec...]
  transfers between devices with their start and end apart: 7 -> 7, of which waited for: 5 -> 5; matrix products, arithmetic and copies ran while one was open for 15% -> 15% of each run, Pallas kernels for 6% -> 14%
where the time goes in v14:
time: 127 us; the launch traced here: 125 us
  waiting for transfers between devices  37.4 us (29%)
  Pallas kernels  28.8 us (23%)
  starting transfers between devices  21.9 us (17%)
  other arithmetic  13.5 us (11%)
  local copies, waits for them, and re-layouts  13 us (10%)
  matrix products  9.37 us (7%)
  between operations  1.44 us (1%)
    all_to_all x1, waiting for transfers between devices, on_device(): lax.all_to_all(send_rows, 'dp', split_axis=0, concat_axis=0, tiled=True)  19.6 us
    pallas_call x1, Pallas kernels, scores(): pl.pallas_call(score_kernel, grid=(rows // tile,), in_specs=[pl.BlockSpec...  10.9 us
    ppermute x3, waiting for transfers between devices, on_device(): lax.ppermute(doc_unit, 'blk', [(i, (i + shift) % cycle_size) for i in ran...  10.5 us
    pallas_call x1, Pallas kernels, unit_queries(): pl.pallas_call(unit_query_kernel, grid=(rows // tile,), in_specs=[pl.Bloc...  9.9 us
    dot_general x1, matrix products, on_device(): partial = jnp.dot(selector, embedded, preferred_element_type=jnp.float32)  8.2 us
    pallas_call x1, Pallas kernels, query_grads(): pl.pallas_call(query_grad_kernel, grid=(rows // tile,), in_specs=[pl.Bloc...  8.03 us
    all_to_all x1, starting transfers between devices, on_device(): lax.all_to_all(partial, 'dp', split_axis=0, concat_axis=0, tiled=True)  4.98 us
    ppermute x3, starting transfers between devices, on_device(): lax.ppermute(doc_unit, 'blk', [(i, (i + shift) % cycle_size) for i in ran...  4.67 us
  transfers between devices with their start and end apart: 7, of which 5 were waited for; matrix products, arithmetic and copies ran while one was open for 15% of the time, Pallas kernels for 14%

profile of v14, /device:TPU:2, one launch (start us, length us, event | category | flops | bytes accessed | tf_op | source)
XLA Modules:
  0.0 125.4 jit_solution(5195558928873268600)
XLA Ops:
  0.6 1.2 slice.9
  5.9 4.3 %all-to-all-start.1 = ((s32[8,1,154]{2,1,0:T(1,128)}), s32[8,1,154]{2,1,0:T(1,128)S(1)}, u32[]{:S(2)}, u32[]{:S(2)}) async-start(s32[8,1,154]{2,1,0:T(1,128)} %copy.19), calls=%async_computation.1 | async-start | bytes 16384 | tf_op jit(solution)/shard_map/all_to_all | solution.py:161
  10.2 3.2 %copy.17 = bf16[160,8,1024]{2,0,1:T(8,128)(2,1)S(1)} copy(bf16[160,8,1024]{2,1,0:T(8,128)(2,1)} %bitcast.46) | data formatting | bytes 5242880 | tf_op jit(solution)/shard_map/reshape | solution.py:150
  13.4 2.2 %gather_fusion = bf16[8,160,1024]{2,1,0:T(8,128)(2,1)} fusion(bf16[160,8,1024]{2,0,1:T(8,128)(2,1)S(1)} %copy.17, s32[1024]{0:T(1024)S(1)} %pad_clamp_fusion.2), kind=kCustom, calls=%fused_computation | custom fusion | bytes 5242912 | tf_op jit(solution)/shard_map/jit(_take)/gather | solution.py:151
  15.6 4.2 %all-to-all-start = ((bf16[8,154,1024]{2,1,0:T(8,128)(2,1)}), bf16[8,154,1024]{2,1,0:T(8,128)(2,1)S(1)}, u32[]{:S(2)}, u32[]{:S(2)}) async-start(bf16[8,154,1024]{2,1,0:T(8,128)(2,1)} %bitcast.42), calls=%async_computation | async-start | bytes 5242880 | tf_op jit(solution)/shard_map/all_to_all | solution.py:159
  21.6 4.3 %fusion.41 = (s32[320]{0:T(512)S(1)}, s32[320,1]{0,1:T(1,128)S(1)}) fusion(s32[]{:T(128)} %bitcast.8, s32[]{:T(128)} %bitcast.9, s32[]{:T(128)} %bitcast.10, s32[]{:T(128)} %bitcast.11, s32[]{:T(128)} %bitcast.12, s32[]{:T(128)} %bitcast.14, s32[]{:T(128)} %bitcast.13, s32[320]{0:T(512)S(1)} %get-tuple-element.23, s32[320]{0:T(512)S(1)} %get-tuple-element.22), kind=kLoop, calls=%fused_computation.79 | loop fusion | flops 4480 | bytes 5148 | tf_op jit(solution)/shard_map/gather | solution.py:169
  27.3 2.2 %gather_fusion.2 = s32[320]{0:T(512)S(1)} fusion(s32[1232]{0:T(1024)S(1)} %reshape.330, s32[1024]{0:T(1024)S(1)} %pad_clamp_fusion.1), kind=kCustom, calls=%fused_computation.2 | custom fusion | bytes 3840 | tf_op jit(solution)/shard_map/gather | solution.py:181
  30.9 19.6 %all-to-all-done = bf16[8,154,1024]{2,1,0:T(8,128)(2,1)S(1)} async-done(((bf16[8,154,1024]{2,1,0:T(8,128)(2,1)}), bf16[8,154,1024]{2,1,0:T(8,128)(2,1)S(1)}, u32[]{:S(2)}, u32[]{:S(2)}) %all-to-all-start) | async-done | bytes 2523168 | tf_op jit(solution)/shard_map/all_to_all | solution.py:159
  50.5 1.2 fusion.23
  51.7 8.2 %convolution_convert_fusion = bf16[128,4096]{1,0:T(8,128)(2,1)} fusion(bf16[1,1024,4096]{2,1,0:T(8,128)(2,1)} %param.12, bf16[320,1024]{1,0:T(8,128)(2,1)S(1)} %get-tuple-element.33, f32[1024]{0:T(1024)S(1)} %copy-done.1, f32[320]{0:T(512)S(1)} %add_rsqrt_fusion, s32[320]{0:T(512)S(1)} %add_select_fusion), kind=kOutput, calls=%fused_computation.15 | convolution fusion | flops 3033571328 | bytes 10099200 | tf_op jit(solution)/shard_map/dot_general | solution.py:197
  59.9 5.0 %all-to-all-start.2 = ((bf16[8,16,4096]{2,1,0:T(8,128)(2,1)}), bf16[8,16,4096]{2,1,0:T(8,128)(2,1)S(1)}, u32[]{:S(2)}, u32[]{:S(2)}) async-start(bf16[8,16,4096]{2,1,0:T(8,128)(2,1)} %bitcast.17), calls=%async_computation.2 | async-start | bytes 2097152 | tf_op jit(solution)/shard_map/all_to_all | solution.py:199
  65.0 0.9 fusion.35.hit_ref
  65.8 9.9 %shard_map.103.q_ref = bf16[896,4096]{1,0:T(8,128)(2,1)} custom-call(bf16[896,4096]{1,0:T(8,128)(2,1)} %q_ref), custom_call_target="tpu_custom_call" | custom-call | flops 14680064 | bytes 14680064 | tf_op jit(solution)/shard_map/pallas_call | solution.py:67
  75.7 3.1 %all-to-all-done.2 = bf16[8,16,4096]{2,1,0:T(8,128)(2,1)S(1)} async-done(((bf16[8,16,4096]{2,1,0:T(8,128)(2,1)}), bf16[8,16,4096]{2,1,0:T(8,128)(2,1)S(1)}, u32[]{:S(2)}, u32[]{:S(2)}) %all-to-all-start.2) | async-done | bytes 1048608 | tf_op jit(solution)/shard_map/all_to_all | solution.py:199
  79.2 3.7 %collective-permute-start.2 = (bf16[16,4096]{1,0:T(8,128)(2,1)S(1)}, bf16[16,4096]{1,0:T(8,128)(2,1)S(1)}, u32[]{:S(2)}, u32[]{:S(2)}) collective-permute-start(bf16[16,4096]{1,0:T(8,128)(2,1)S(1)} %multiply_convert_fusion), channel_id=1, source_target_pairs={{0,3},{1,0},{2,1},{3,2},{4,7},{5,4},{6,5},{7,6},{8,11},{9,8},{10,9... | collective-permute-start | bytes 393224 | tf_op jit(solution)/shard_map/ppermute | solution.py:209
  82.9 1.0 collective-permute-start
  84.0 2.8 %collective-permute-done.2 = bf16[16,4096]{1,0:T(8,128)(2,1)S(1)} collective-permute-done((bf16[16,4096]{1,0:T(8,128)(2,1)S(1)}, bf16[16,4096]{1,0:T(8,128)(2,1)S(1)}, u32[]{:S(2)}, u32[]{:S(2)}) %collective-permute-start.2) | collective-permute-done | bytes 131104 | tf_op jit(solution)/shard_map/ppermute | solution.py:209
  86.8 7.6 %collective-permute-done.1 = bf16[16,4096]{1,0:T(8,128)(2,1)S(1)} collective-permute-done((bf16[16,4096]{1,0:T(8,128)(2,1)S(1)}, bf16[16,4096]{1,0:T(8,128)(2,1)S(1)}, u32[]{:S(2)}, u32[]{:S(2)}) %collective-permute-start.1) | collective-permute-done | bytes 131104 | tf_op jit(solution)/shard_map/ppermute | solution.py:209
  94.5 1.4 %gather_fusion.3 = bf16[4,16,4096]{2,1,0:T(8,128)(2,1)} fusion(bf16[4,16,4096]{2,1,0:T(8,128)(2,1)S(1)} %pad_maximum_fusion, s32[1024]{0:T(1024)S(1)} %pad_clamp_fusion), kind=kCustom, calls=%fused_computation.3 | custom fusion | bytes 1048592 | tf_op jit(solution)/shard_map/gather | solution.py:214
  95.9 10.9 %shard_map.104 = (f32[896,1]{1,0:T(8,128)}, bf16[896,64]{1,0:T(8,128)(2,1)}, f32[896,1]{1,0:T(8,128)}, bf16[64,4096]{1,0:T(8,128)(2,1)}) custom-call(bf16[896,4096]{1,0:T(8,128)(2,1)} %shard_map.103.q_ref, bf16[64,4096]{1,0:T(8,128)(2,1)} %bitcast.44, bf16[896,64]{1,0:T(8,128)(2,1)} %fusion.35.hit_ref), custom_call_target="tpu_custom_call" | custom-call | flops 939524096 | bytes 7340032 | tf_op jit(solution)/shard_map/pallas_call | solution.py:89
  106.8 3.8 %all-to-all-start.3 = ((bf16[4,16,4096]{2,1,0:T(8,128)(2,1)}), bf16[4,16,4096]{2,1,0:T(8,128)(2,1)S(1)}, u32[]{:S(2)}, u32[]{:S(2)}) async-start(bf16[4,16,4096]{2,1,0:T(8,128)(2,1)} %bitcast.47), calls=%async_computation.3 | async-start | bytes 1048576 | tf_op jit(solution)/shard_map/all_to_all | solution.py:220
  110.6 1.8 %reduce.7 = f32[896]{0:T(1024)} reduce(f32[896,1]{1,0:T(8,128)} %get-tuple-element.11, f32[]{:T(128)} %constant.84), dimensions={1}, to_apply=%get-tuple-element.11.reduce_sub_computation | reduce | bytes 7172 | tf_op jit(solution)/shard_map/pallas_call | solution.py:89
  112.4 8.0 %shard_map.105 = bf16[896,4096]{1,0:T(8,128)(2,1)} custom-call(bf16[896,64]{1,0:T(8,128)(2,1)} %get-tuple-element.12.wb_ref, f32[896,1]{1,0:T(8,128)} %get-tuple-element.13.tot_ref, bf16[896,64]{1,0:T(8,128)(2,1)} %fusion.35.hit_ref, bf16[64,4096]{1,0:T(8,128)(2,1)} %bitcast.45), custom_call_target="tpu_custom_call" | custom-call | flops 939524096 | bytes 7340032 | tf_op jit(solution)/shard_map/pallas_call | solution.py:120
  120.4 4.2 %all-to-all-done.3 = bf16[4,16,4096]{2,1,0:T(8,128)(2,1)S(1)} async-done(((bf16[4,16,4096]{2,1,0:T(8,128)(2,1)}), bf16[4,16,4096]{2,1,0:T(8,128)(2,1)S(1)}, u32[]{:S(2)}, u32[]{:S(2)}) %all-to-all-start.3) | async-done | bytes 524320 | tf_op jit(solution)/shard_map/all_to_all | solution.py:220
  (41 shorter events, 9.3 us)
Async XLA Ops:
  5.9 9.6 %all-to-all-start.1 = ((s32[8,1,154]{2,1,0:T(1,128)}), s32[8,1,154]{2,1,0:T(1,128)S(1)}, u32[]{:S(2)}, u32[]{:S(2)}) async-start(s32[8,1,154]{2,1,0:T(1,128)} %copy.19), calls=%async_computation.1 | async-start | bytes 16384 | tf_op jit(solution)/shard_map/all_to_all | solution.py:161
  15.6 35.0 %all-to-all-start = ((bf16[8,154,1024]{2,1,0:T(8,128)(2,1)}), bf16[8,154,1024]{2,1,0:T(8,128)(2,1)S(1)}, u32[]{:S(2)}, u32[]{:S(2)}) async-start(bf16[8,154,1024]{2,1,0:T(8,128)(2,1)} %bitcast.42), calls=%async_computation | async-start | bytes 5242880 | tf_op jit(solution)/shard_map/all_to_all | solution.py:159
  30.9 20.8 %copy-start.1 = (f32[1024]{0:T(1024)S(1)}, f32[1024]{0:T(1024)}, u32[]{:S(2)}) copy-start(f32[1024]{0:T(1024)} %param.13) | copy-start | bytes 12292
  51.7 13.2 %copy-start = (s32[896]{0:T(1024)S(1)}, s32[896]{0:T(1024)}, u32[]{:S(2)}) copy-start(s32[896]{0:T(1024)} %param.15) | copy-start | bytes 10756
  59.9 18.9 %all-to-all-start.2 = ((bf16[8,16,4096]{2,1,0:T(8,128)(2,1)}), bf16[8,16,4096]{2,1,0:T(8,128)(2,1)S(1)}, u32[]{:S(2)}, u32[]{:S(2)}) async-start(bf16[8,16,4096]{2,1,0:T(8,128)(2,1)} %bitcast.17), calls=%async_computation.2 | async-start | bytes 2097152 | tf_op jit(solution)/shard_map/all_to_all | solution.py:199
  79.2 7.6 %collective-permute-start.2 = (bf16[16,4096]{1,0:T(8,128)(2,1)S(1)}, bf16[16,4096]{1,0:T(8,128)(2,1)S(1)}, u32[]{:S(2)}, u32[]{:S(2)}) collective-permute-start(bf16[16,4096]{1,0:T(8,128)(2,1)S(1)} %multiply_convert_fusion), channel_id=1, source_target_pairs={{0,3},{1,0},{2,1},{3,2},{4,7},{5,4},{6,5},{7,6},{8,11},{9,8},{10,9... | collective-permute-start | bytes 393224 | tf_op jit(solution)/shard_map/ppermute | solution.py:209
  82.9 11.6 %collective-permute-start.1 = (bf16[16,4096]{1,0:T(8,128)(2,1)S(1)}, bf16[16,4096]{1,0:T(8,128)(2,1)S(1)}, u32[]{:S(2)}, u32[]{:S(2)}) collective-permute-start(bf16[16,4096]{1,0:T(8,128)(2,1)S(1)} %multiply_convert_fusion), channel_id=1, source_target_pairs={{0,2},{1,3},{2,0},{3,1},{4,6},{5,7},{6,4},{7,5},{8,10},{9,11},{10,... | collective-permute-start | bytes 393224 | tf_op jit(solution)/shard_map/ppermute | solution.py:209
  82.9 11.6 %collective-permute-start = (bf16[16,4096]{1,0:T(8,128)(2,1)S(1)}, bf16[16,4096]{1,0:T(8,128)(2,1)S(1)}, u32[]{:S(2)}, u32[]{:S(2)}) collective-permute-start(bf16[16,4096]{1,0:T(8,128)(2,1)S(1)} %multiply_convert_fusion), channel_id=1, source_target_pairs={{0,1},{1,2},{2,3},{3,0},{4,5},{5,6},{6,7},{7,4},{8,9},{9,10},{10,1... | collective-permute-start | bytes 393224 | tf_op jit(solution)/shard_map/ppermute | solution.py:209
  106.8 17.9 %all-to-all-start.3 = ((bf16[4,16,4096]{2,1,0:T(8,128)(2,1)}), bf16[4,16,4096]{2,1,0:T(8,128)(2,1)S(1)}, u32[]{:S(2)}, u32[]{:S(2)}) async-start(bf16[4,16,4096]{2,1,0:T(8,128)(2,1)} %bitcast.47), calls=%async_computation.3 | async-start | bytes 1048576 | tf_op jit(solution)/shard_map/all_to_all | solution.py:220

commit v15 on v14

--- a/solution.py
+++ b/solution.py
@@ -83,7 +83,7 @@
     gq_ref[...] = (logit_scale * (numerator / tot_ref[...] - chosen_doc)).astype(jnp.bfloat16)
 
 
-def scores(queries, doc_piece, hits, tile=128):
+def scores(queries, doc_piece, hits, tile=224):
     rows, width = queries.shape
     docs = doc_piece.shape[0]
     return pl.pallas_call(
@@ -114,7 +114,7 @@
     )(queries, doc_piece, hits)
 
 
-def query_grads(weights, totals, hits, doc_piece, tile=128):
+def query_grads(weights, totals, hits, doc_piece, tile=224):
     rows, docs = weights.shape
     width = doc_piece.shape[1]
     return pl.pallas_call(

time: 127 us -> 125 us (0.984)
  Pallas kernels: 28.8 us -> 26.1 us
    pallas_call x1, Pallas kernels: 10.9 us -> 9.15 us  [scores(): pl.pallas_call(score_kernel, grid=(rows // tile,), in_specs=[pl.BlockSpec...]
  transfers between devices with their start and end apart: 7 -> 7, of which waited for: 5 -> 5; matrix products, arithmetic and copies ran while one was open for 15% -> 16% of each run, Pallas kernels for 14% -> 14%
where the time goes in v15:
time: 125 us; the launch traced here: 124 us
  waiting for transfers between devices  38.4 us (31%)
  Pallas kernels  26.1 us (21%)
  starting transfers between devices  21.9 us (18%)
  other arithmetic  13.5 us (11%)
  local copies, waits for them, and re-layouts  13 us (10%)
  matrix products  9.37 us (7%)
  between operations  1.44 us (1%)
    all_to_all x1, waiting for transfers between devices, on_device(): lax.all_to_all(send_rows, 'dp', split_axis=0, concat_axis=0, tiled=True)  19.6 us
    ppermute x3, waiting for transfers between devices, on_device(): lax.ppermute(doc_unit, 'blk', [(i, (i + shift) % cycle_size) for i in ran...  10.5 us
    pallas_call x1, Pallas kernels, unit_queries(): pl.pallas_call(unit_query_kernel, grid=(rows // tile,), in_specs=[pl.Bloc...  9.9 us
    pallas_call x1, Pallas kernels, scores(): pl.pallas_call(score_kernel, grid=(rows // tile,), in_specs=[pl.BlockSpec...  9.15 us
    dot_general x1, matrix products, on_device(): partial = jnp.dot(selector, embedded, preferred_element_type=jnp.float32)  8.2 us
    pallas_call x1, Pallas kernels, query_grads(): pl.pallas_call(query_grad_kernel, grid=(rows // tile,), in_specs=[pl.Bloc...  7.06 us
    all_to_all x1, waiting for transfers between devices, on_device(): lax.all_to_all(grad_part.reshape(cycle_size, doc_unit.shape[0], emb_width...  5.22 us
    all_to_all x1, starting transfers between devices, on_device(): lax.all_to_all(partial, 'dp', split_axis=0, concat_axis=0, tiled=True)  4.98 us
  transfers between devices with their start and end apart: 7, of which 5 were waited for; matrix products, arithmetic and copies ran while one was open for 16% of the time, Pallas kernels for 14%

profile of v15, /device:TPU:2, one launch (start us, length us, event | category | flops | bytes accessed | tf_op | source)
XLA Modules:
  0.0 123.7 jit_solution(13639411475359915039)
XLA Ops:
  0.6 1.2 slice.9
  5.9 4.3 %all-to-all-start.1 = ((s32[8,1,154]{2,1,0:T(1,128)}), s32[8,1,154]{2,1,0:T(1,128)S(1)}, u32[]{:S(2)}, u32[]{:S(2)}) async-start(s32[8,1,154]{2,1,0:T(1,128)} %copy.19), calls=%async_computation.1 | async-start | bytes 16384 | tf_op jit(solution)/shard_map/all_to_all | solution.py:161
  10.2 3.2 %copy.17 = bf16[160,8,1024]{2,0,1:T(8,128)(2,1)S(1)} copy(bf16[160,8,1024]{2,1,0:T(8,128)(2,1)} %bitcast.46) | data formatting | bytes 5242880 | tf_op jit(solution)/shard_map/reshape | solution.py:150
  13.4 2.2 %gather_fusion = bf16[8,160,1024]{2,1,0:T(8,128)(2,1)} fusion(bf16[160,8,1024]{2,0,1:T(8,128)(2,1)S(1)} %copy.17, s32[1024]{0:T(1024)S(1)} %pad_clamp_fusion.2), kind=kCustom, calls=%fused_computation | custom fusion | bytes 5242912 | tf_op jit(solution)/shard_map/jit(_take)/gather | solution.py:151
  15.6 4.2 %all-to-all-start = ((bf16[8,154,1024]{2,1,0:T(8,128)(2,1)}), bf16[8,154,1024]{2,1,0:T(8,128)(2,1)S(1)}, u32[]{:S(2)}, u32[]{:S(2)}) async-start(bf16[8,154,1024]{2,1,0:T(8,128)(2,1)} %bitcast.42), calls=%async_computation | async-start | bytes 5242880 | tf_op jit(solution)/shard_map/all_to_all | solution.py:159
  21.6 4.3 %fusion.41 = (s32[320]{0:T(512)S(1)}, s32[320,1]{0,1:T(1,128)S(1)}) fusion(s32[]{:T(128)} %bitcast.8, s32[]{:T(128)} %bitcast.9, s32[]{:T(128)} %bitcast.10, s32[]{:T(128)} %bitcast.11, s32[]{:T(128)} %bitcast.12, s32[]{:T(128)} %bitcast.14, s32[]{:T(128)} %bitcast.13, s32[320]{0:T(512)S(1)} %get-tuple-element.23, s32[320]{0:T(512)S(1)} %get-tuple-element.22), kind=kLoop, calls=%fused_computation.79 | loop fusion | flops 4480 | bytes 5148 | tf_op jit(solution)/shard_map/gather | solution.py:169
  27.3 2.2 %gather_fusion.2 = s32[320]{0:T(512)S(1)} fusion(s32[1232]{0:T(1024)S(1)} %reshape.330, s32[1024]{0:T(1024)S(1)} %pad_clamp_fusion.1), kind=kCustom, calls=%fused_computation.2 | custom fusion | bytes 3840 | tf_op jit(solution)/shard_map/gather | solution.py:181
  30.9 19.6 %all-to-all-done = bf16[8,154,1024]{2,1,0:T(8,128)(2,1)S(1)} async-done(((bf16[8,154,1024]{2,1,0:T(8,128)(2,1)}), bf16[8,154,1024]{2,1,0:T(8,128)(2,1)S(1)}, u32[]{:S(2)}, u32[]{:S(2)}) %all-to-all-start) | async-done | bytes 2523168 | tf_op jit(solution)/shard_map/all_to_all | solution.py:159
  50.5 1.2 fusion.23
  51.7 8.2 %convolution_convert_fusion = bf16[128,4096]{1,0:T(8,128)(2,1)} fusion(bf16[1,1024,4096]{2,1,0:T(8,128)(2,1)} %param.12, bf16[320,1024]{1,0:T(8,128)(2,1)S(1)} %get-tuple-element.33, f32[1024]{0:T(1024)S(1)} %copy-done.1, f32[320]{0:T(512)S(1)} %add_rsqrt_fusion, s32[320]{0:T(512)S(1)} %add_select_fusion), kind=kOutput, calls=%fused_computation.15 | convolution fusion | flops 3033571328 | bytes 10099200 | tf_op jit(solution)/shard_map/dot_general | solution.py:197
  59.9 5.0 %all-to-all-start.2 = ((bf16[8,16,4096]{2,1,0:T(8,128)(2,1)}), bf16[8,16,4096]{2,1,0:T(8,128)(2,1)S(1)}, u32[]{:S(2)}, u32[]{:S(2)}) async-start(bf16[8,16,4096]{2,1,0:T(8,128)(2,1)} %bitcast.17), calls=%async_computation.2 | async-start | bytes 2097152 | tf_op jit(solution)/shard_map/all_to_all | solution.py:199
  65.0 0.9 fusion.35.hit_ref
  65.8 9.9 %shard_map.103.q_ref = bf16[896,4096]{1,0:T(8,128)(2,1)} custom-call(bf16[896,4096]{1,0:T(8,128)(2,1)} %q_ref), custom_call_target="tpu_custom_call" | custom-call | flops 14680064 | bytes 14680064 | tf_op jit(solution)/shard_map/pallas_call | solution.py:67
  75.7 3.1 %all-to-all-done.2 = bf16[8,16,4096]{2,1,0:T(8,128)(2,1)S(1)} async-done(((bf16[8,16,4096]{2,1,0:T(8,128)(2,1)}), bf16[8,16,4096]{2,1,0:T(8,128)(2,1)S(1)}, u32[]{:S(2)}, u32[]{:S(2)}) %all-to-all-start.2) | async-done | bytes 1048608 | tf_op jit(solution)/shard_map/all_to_all | solution.py:199
  79.2 3.7 %collective-permute-start.2 = (bf16[16,4096]{1,0:T(8,128)(2,1)S(1)}, bf16[16,4096]{1,0:T(8,128)(2,1)S(1)}, u32[]{:S(2)}, u32[]{:S(2)}) collective-permute-start(bf16[16,4096]{1,0:T(8,128)(2,1)S(1)} %multiply_convert_fusion), channel_id=1, source_target_pairs={{0,3},{1,0},{2,1},{3,2},{4,7},{5,4},{6,5},{7,6},{8,11},{9,8},{10,9... | collective-permute-start | bytes 393224 | tf_op jit(solution)/shard_map/ppermute | solution.py:209
  82.9 1.0 collective-permute-start
  84.0 2.8 %collective-permute-done.2 = bf16[16,4096]{1,0:T(8,128)(2,1)S(1)} collective-permute-done((bf16[16,4096]{1,0:T(8,128)(2,1)S(1)}, bf16[16,4096]{1,0:T(8,128)(2,1)S(1)}, u32[]{:S(2)}, u32[]{:S(2)}) %collective-permute-start.2) | collective-permute-done | bytes 131104 | tf_op jit(solution)/shard_map/ppermute | solution.py:209
  86.8 7.6 %collective-permute-done.1 = bf16[16,4096]{1,0:T(8,128)(2,1)S(1)} collective-permute-done((bf16[16,4096]{1,0:T(8,128)(2,1)S(1)}, bf16[16,4096]{1,0:T(8,128)(2,1)S(1)}, u32[]{:S(2)}, u32[]{:S(2)}) %collective-permute-start.1) | collective-permute-done | bytes 131104 | tf_op jit(solution)/shard_map/ppermute | solution.py:209
  94.5 1.4 %gather_fusion.3 = bf16[4,16,4096]{2,1,0:T(8,128)(2,1)} fusion(bf16[4,16,4096]{2,1,0:T(8,128)(2,1)S(1)} %pad_maximum_fusion, s32[1024]{0:T(1024)S(1)} %pad_clamp_fusion), kind=kCustom, calls=%fused_computation.3 | custom fusion | bytes 1048592 | tf_op jit(solution)/shard_map/gather | solution.py:214
  95.9 9.2 %shard_map.104 = (f32[896,1]{1,0:T(8,128)}, bf16[896,64]{1,0:T(8,128)(2,1)}, f32[896,1]{1,0:T(8,128)}, bf16[64,4096]{1,0:T(8,128)(2,1)}) custom-call(bf16[896,4096]{1,0:T(8,128)(2,1)} %shard_map.103.q_ref, bf16[64,4096]{1,0:T(8,128)(2,1)} %bitcast.44, bf16[896,64]{1,0:T(8,128)(2,1)} %fusion.35.hit_ref), custom_call_target="tpu_custom_call" | custom-call | flops 939524096 | bytes 7340032 | tf_op jit(solution)/shard_map/pallas_call | solution.py:89
  105.1 3.8 %all-to-all-start.3 = ((bf16[4,16,4096]{2,1,0:T(8,128)(2,1)}), bf16[4,16,4096]{2,1,0:T(8,128)(2,1)S(1)}, u32[]{:S(2)}, u32[]{:S(2)}) async-start(bf16[4,16,4096]{2,1,0:T(8,128)(2,1)} %bitcast.47), calls=%async_computation.3 | async-start | bytes 1048576 | tf_op jit(solution)/shard_map/all_to_all | solution.py:220
  108.8 1.8 %reduce.7 = f32[896]{0:T(1024)} reduce(f32[896,1]{1,0:T(8,128)} %get-tuple-element.11, f32[]{:T(128)} %constant.84), dimensions={1}, to_apply=%get-tuple-element.11.reduce_sub_computation | reduce | bytes 7172 | tf_op jit(solution)/shard_map/pallas_call | solution.py:89
  110.7 7.1 %shard_map.105 = bf16[896,4096]{1,0:T(8,128)(2,1)} custom-call(bf16[896,64]{1,0:T(8,128)(2,1)} %get-tuple-element.12.wb_ref, f32[896,1]{1,0:T(8,128)} %get-tuple-element.13.tot_ref, bf16[896,64]{1,0:T(8,128)(2,1)} %fusion.35.hit_ref, bf16[64,4096]{1,0:T(8,128)(2,1)} %bitcast.45), custom_call_target="tpu_custom_call" | custom-call | flops 939524096 | bytes 7340032 | tf_op jit(solution)/shard_map/pallas_call | solution.py:120
  117.7 5.2 %all-to-all-done.3 = bf16[4,16,4096]{2,1,0:T(8,128)(2,1)S(1)} async-done(((bf16[4,16,4096]{2,1,0:T(8,128)(2,1)}), bf16[4,16,4096]{2,1,0:T(8,128)(2,1)S(1)}, u32[]{:S(2)}, u32[]{:S(2)}) %all-to-all-start.3) | async-done | bytes 524320 | tf_op jit(solution)/shard_map/all_to_all | solution.py:220
  (41 shorter events, 9.3 us)
Async XLA Ops:
  5.9 9.6 %all-to-all-start.1 = ((s32[8,1,154]{2,1,0:T(1,128)}), s32[8,1,154]{2,1,0:T(1,128)S(1)}, u32[]{:S(2)}, u32[]{:S(2)}) async-start(s32[8,1,154]{2,1,0:T(1,128)} %copy.19), calls=%async_computation.1 | async-start | bytes 16384 | tf_op jit(solution)/shard_map/all_to_all | solution.py:161
  15.6 35.0 %all-to-all-start = ((bf16[8,154,1024]{2,1,0:T(8,128)(2,1)}), bf16[8,154,1024]{2,1,0:T(8,128)(2,1)S(1)}, u32[]{:S(2)}, u32[]{:S(2)}) async-start(bf16[8,154,1024]{2,1,0:T(8,128)(2,1)} %bitcast.42), calls=%async_computation | async-start | bytes 5242880 | tf_op jit(solution)/shard_map/all_to_all | solution.py:159
  30.9 20.8 %copy-start.1 = (f32[1024]{0:T(1024)S(1)}, f32[1024]{0:T(1024)}, u32[]{:S(2)}) copy-start(f32[1024]{0:T(1024)} %param.13) | copy-start | bytes 12292
  51.7 13.2 %copy-start = (s32[896]{0:T(1024)S(1)}, s32[896]{0:T(1024)}, u32[]{:S(2)}) copy-start(s32[896]{0:T(1024)} %param.15) | copy-start | bytes 10756
  59.9 18.9 %all-to-all-start.2 = ((bf16[8,16,4096]{2,1,0:T(8,128)(2,1)}), bf16[8,16,4096]{2,1,0:T(8,128)(2,1)S(1)}, u32[]{:S(2)}, u32[]{:S(2)}) async-start(bf16[8,16,4096]{2,1,0:T(8,128)(2,1)} %bitcast.17), calls=%async_computation.2 | async-start | bytes 2097152 | tf_op jit(solution)/shard_map/all_to_all | solution.py:199
  79.2 7.6 %collective-permute-start.2 = (bf16[16,4096]{1,0:T(8,128)(2,1)S(1)}, bf16[16,4096]{1,0:T(8,128)(2,1)S(1)}, u32[]{:S(2)}, u32[]{:S(2)}) collective-permute-start(bf16[16,4096]{1,0:T(8,128)(2,1)S(1)} %multiply_convert_fusion), channel_id=1, source_target_pairs={{0,3},{1,0},{2,1},{3,2},{4,7},{5,4},{6,5},{7,6},{8,11},{9,8},{10,9... | collective-permute-start | bytes 393224 | tf_op jit(solution)/shard_map/ppermute | solution.py:209
  82.9 11.6 %collective-permute-start.1 = (bf16[16,4096]{1,0:T(8,128)(2,1)S(1)}, bf16[16,4096]{1,0:T(8,128)(2,1)S(1)}, u32[]{:S(2)}, u32[]{:S(2)}) collective-permute-start(bf16[16,4096]{1,0:T(8,128)(2,1)S(1)} %multiply_convert_fusion), channel_id=1, source_target_pairs={{0,2},{1,3},{2,0},{3,1},{4,6},{5,7},{6,4},{7,5},{8,10},{9,11},{10,... | collective-permute-start | bytes 393224 | tf_op jit(solution)/shard_map/ppermute | solution.py:209
  82.9 11.6 %collective-permute-start = (bf16[16,4096]{1,0:T(8,128)(2,1)S(1)}, bf16[16,4096]{1,0:T(8,128)(2,1)S(1)}, u32[]{:S(2)}, u32[]{:S(2)}) collective-permute-start(bf16[16,4096]{1,0:T(8,128)(2,1)S(1)} %multiply_convert_fusion), channel_id=1, source_target_pairs={{0,1},{1,2},{2,3},{3,0},{4,5},{5,6},{6,7},{7,4},{8,9},{9,10},{10,1... | collective-permute-start | bytes 393224 | tf_op jit(solution)/shard_map/ppermute | solution.py:209
  105.1 17.9 %all-to-all-start.3 = ((bf16[4,16,4096]{2,1,0:T(8,128)(2,1)}), bf16[4,16,4096]{2,1,0:T(8,128)(2,1)S(1)}, u32[]{:S(2)}, u32[]{:S(2)}) async-start(bf16[4,16,4096]{2,1,0:T(8,128)(2,1)} %bitcast.47), calls=%async_computation.3 | async-start | bytes 1048576 | tf_op jit(solution)/shard_map/all_to_all | solution.py:220

commit v16 on v15

--- a/solution.py
+++ b/solution.py
@@ -83,7 +83,7 @@
     gq_ref[...] = (logit_scale * (numerator / tot_ref[...] - chosen_doc)).astype(jnp.bfloat16)
 
 
-def scores(queries, doc_piece, hits, tile=224):
+def scores(queries, doc_piece, hits, tile=448):
     rows, width = queries.shape
     docs = doc_piece.shape[0]
     return pl.pallas_call(

time: 125 us -> 126 us (level)
  transfers between devices with their start and end apart: 7 -> 7, of which waited for: 5 -> 5; matrix products, arithmetic and copies ran while one was open for 16% -> 15% of each run, Pallas kernels for 14% -> 14%
where the time goes in v16:
time: 126 us; the launch traced here: 125 us
  waiting for transfers between devices  38.4 us (30%)
  Pallas kernels  27 us (21%)
  starting transfers between devices  21.9 us (17%)
  other arithmetic  13.5 us (11%)
  local copies, waits for them, and re-layouts  13 us (10%)
  matrix products  9.37 us (7%)
  between operations  1.44 us (1%)
    all_to_all x1, waiting for transfers between devices, on_device(): lax.all_to_all(send_rows, 'dp', split_axis=0, concat_axis=0, tiled=True)  19.6 us
    ppermute x3, waiting for transfers between devices, on_device(): lax.ppermute(doc_unit, 'blk', [(i, (i + shift) % cycle_size) for i in ran...  10.5 us
    pallas_call x1, Pallas kernels, scores(): pl.pallas_call(score_kernel, grid=(rows // tile,), in_specs=[pl.BlockSpec...  10 us
    pallas_call x1, Pallas kernels, unit_queries(): pl.pallas_call(unit_query_kernel, grid=(rows // tile,), in_specs=[pl.Bloc...  9.9 us
    dot_general x1, matrix products, on_device(): partial = jnp.dot(selector, embedded, preferred_element_type=jnp.float32)  8.2 us
    pallas_call x1, Pallas kernels, query_grads(): pl.pallas_call(query_grad_kernel, grid=(rows // tile,), in_specs=[pl.Bloc...  7.05 us
    all_to_all x1, waiting for transfers between devices, on_device(): lax.all_to_all(grad_part.reshape(cycle_size, doc_unit.shape[0], emb_width...  5.22 us
    all_to_all x1, starting transfers between devices, on_device(): lax.all_to_all(partial, 'dp', split_axis=0, concat_axis=0, tiled=True)  4.98 us
  transfers between devices with their start and end apart: 7, of which 5 were waited for; matrix products, arithmetic and copies ran while one was open for 15% of the time, Pallas kernels for 14%

profile of v16, /device:TPU:2, one launch (start us, length us, event | category | flops | bytes accessed | tf_op | source)
XLA Modules:
  0.0 124.6 jit_solution(4946071287849780283)
XLA Ops:
  0.6 1.2 slice.9
  5.9 4.3 %all-to-all-start.1 = ((s32[8,1,154]{2,1,0:T(1,128)}), s32[8,1,154]{2,1,0:T(1,128)S(1)}, u32[]{:S(2)}, u32[]{:S(2)}) async-start(s32[8,1,154]{2,1,0:T(1,128)} %copy.19), calls=%async_computation.1 | async-start | bytes 16384 | tf_op jit(solution)/shard_map/all_to_all | solution.py:161
  10.2 3.2 %copy.17 = bf16[160,8,1024]{2,0,1:T(8,128)(2,1)S(1)} copy(bf16[160,8,1024]{2,1,0:T(8,128)(2,1)} %bitcast.46) | data formatting | bytes 5242880 | tf_op jit(solution)/shard_map/reshape | solution.py:150
  13.4 2.2 %gather_fusion = bf16[8,160,1024]{2,1,0:T(8,128)(2,1)} fusion(bf16[160,8,1024]{2,0,1:T(8,128)(2,1)S(1)} %copy.17, s32[1024]{0:T(1024)S(1)} %pad_clamp_fusion.2), kind=kCustom, calls=%fused_computation | custom fusion | bytes 5242912 | tf_op jit(solution)/shard_map/jit(_take)/gather | solution.py:151
  15.6 4.2 %all-to-all-start = ((bf16[8,154,1024]{2,1,0:T(8,128)(2,1)}), bf16[8,154,1024]{2,1,0:T(8,128)(2,1)S(1)}, u32[]{:S(2)}, u32[]{:S(2)}) async-start(bf16[8,154,1024]{2,1,0:T(8,128)(2,1)} %bitcast.42), calls=%async_computation | async-start | bytes 5242880 | tf_op jit(solution)/shard_map/all_to_all | solution.py:159
  21.6 4.3 %fusion.41 = (s32[320]{0:T(512)S(1)}, s32[320,1]{0,1:T(1,128)S(1)}) fusion(s32[]{:T(128)} %bitcast.8, s32[]{:T(128)} %bitcast.9, s32[]{:T(128)} %bitcast.10, s32[]{:T(128)} %bitcast.11, s32[]{:T(128)} %bitcast.12, s32[]{:T(128)} %bitcast.14, s32[]{:T(128)} %bitcast.13, s32[320]{0:T(512)S(1)} %get-tuple-element.23, s32[320]{0:T(512)S(1)} %get-tuple-element.22), kind=kLoop, calls=%fused_computation.79 | loop fusion | flops 4480 | bytes 5148 | tf_op jit(solution)/shard_map/gather | solution.py:169
  27.3 2.2 %gather_fusion.2 = s32[320]{0:T(512)S(1)} fusion(s32[1232]{0:T(1024)S(1)} %reshape.330, s32[1024]{0:T(1024)S(1)} %pad_clamp_fusion.1), kind=kCustom, calls=%fused_computation.2 | custom fusion | bytes 3840 | tf_op jit(solution)/shard_map/gather | solution.py:181
  30.9 19.6 %all-to-all-done = bf16[8,154,1024]{2,1,0:T(8,128)(2,1)S(1)} async-done(((bf16[8,154,1024]{2,1,0:T(8,128)(2,1)}), bf16[8,154,1024]{2,1,0:T(8,128)(2,1)S(1)}, u32[]{:S(2)}, u32[]{:S(2)}) %all-to-all-start) | async-done | bytes 2523168 | tf_op jit(solution)/shard_map/all_to_all | solution.py:159
  50.5 1.2 fusion.23
  51.7 8.2 %convolution_convert_fusion = bf16[128,4096]{1,0:T(8,128)(2,1)} fusion(bf16[1,1024,4096]{2,1,0:T(8,128)(2,1)} %param.12, bf16[320,1024]{1,0:T(8,128)(2,1)S(1)} %get-tuple-element.33, f32[1024]{0:T(1024)S(1)} %copy-done.1, f32[320]{0:T(512)S(1)} %add_rsqrt_fusion, s32[320]{0:T(512)S(1)} %add_select_fusion), kind=kOutput, calls=%fused_computation.15 | convolution fusion | flops 3033571328 | bytes 10099200 | tf_op jit(solution)/shard_map/dot_general | solution.py:197
  59.9 5.0 %all-to-all-start.2 = ((bf16[8,16,4096]{2,1,0:T(8,128)(2,1)}), bf16[8,16,4096]{2,1,0:T(8,128)(2,1)S(1)}, u32[]{:S(2)}, u32[]{:S(2)}) async-start(bf16[8,16,4096]{2,1,0:T(8,128)(2,1)} %bitcast.17), calls=%async_computation.2 | async-start | bytes 2097152 | tf_op jit(solution)/shard_map/all_to_all | solution.py:199
  65.0 0.9 fusion.35.hit_ref
  65.8 9.9 %shard_map.103.q_ref = bf16[896,4096]{1,0:T(8,128)(2,1)} custom-call(bf16[896,4096]{1,0:T(8,128)(2,1)} %q_ref), custom_call_target="tpu_custom_call" | custom-call | flops 14680064 | bytes 14680064 | tf_op jit(solution)/shard_map/pallas_call | solution.py:67
  75.7 3.1 %all-to-all-done.2 = bf16[8,16,4096]{2,1,0:T(8,128)(2,1)S(1)} async-done(((bf16[8,16,4096]{2,1,0:T(8,128)(2,1)}), bf16[8,16,4096]{2,1,0:T(8,128)(2,1)S(1)}, u32[]{:S(2)}, u32[]{:S(2)}) %all-to-all-start.2) | async-done | bytes 1048608 | tf_op jit(solution)/shard_map/all_to_all | solution.py:199
  79.2 3.7 %collective-permute-start.2 = (bf16[16,4096]{1,0:T(8,128)(2,1)S(1)}, bf16[16,4096]{1,0:T(8,128)(2,1)S(1)}, u32[]{:S(2)}, u32[]{:S(2)}) collective-permute-start(bf16[16,4096]{1,0:T(8,128)(2,1)S(1)} %multiply_convert_fusion), channel_id=1, source_target_pairs={{0,3},{1,0},{2,1},{3,2},{4,7},{5,4},{6,5},{7,6},{8,11},{9,8},{10,9... | collective-permute-start | bytes 393224 | tf_op jit(solution)/shard_map/ppermute | solution.py:209
  82.9 1.0 collective-permute-start
  84.0 2.8 %collective-permute-done.2 = bf16[16,4096]{1,0:T(8,128)(2,1)S(1)} collective-permute-done((bf16[16,4096]{1,0:T(8,128)(2,1)S(1)}, bf16[16,4096]{1,0:T(8,128)(2,1)S(1)}, u32[]{:S(2)}, u32[]{:S(2)}) %collective-permute-start.2) | collective-permute-done | bytes 131104 | tf_op jit(solution)/shard_map/ppermute | solution.py:209
  86.8 7.6 %collective-permute-done.1 = bf16[16,4096]{1,0:T(8,128)(2,1)S(1)} collective-permute-done((bf16[16,4096]{1,0:T(8,128)(2,1)S(1)}, bf16[16,4096]{1,0:T(8,128)(2,1)S(1)}, u32[]{:S(2)}, u32[]{:S(2)}) %collective-permute-start.1) | collective-permute-done | bytes 131104 | tf_op jit(solution)/shard_map/ppermute | solution.py:209
  94.5 1.4 %gather_fusion.3 = bf16[4,16,4096]{2,1,0:T(8,128)(2,1)} fusion(bf16[4,16,4096]{2,1,0:T(8,128)(2,1)S(1)} %pad_maximum_fusion, s32[1024]{0:T(1024)S(1)} %pad_clamp_fusion), kind=kCustom, calls=%fused_computation.3 | custom fusion | bytes 1048592 | tf_op jit(solution)/shard_map/gather | solution.py:214
  95.9 10.0 %shard_map.104 = (f32[896,1]{1,0:T(8,128)}, bf16[896,64]{1,0:T(8,128)(2,1)}, f32[896,1]{1,0:T(8,128)}, bf16[64,4096]{1,0:T(8,128)(2,1)}) custom-call(bf16[896,4096]{1,0:T(8,128)(2,1)} %shard_map.103.q_ref, bf16[64,4096]{1,0:T(8,128)(2,1)} %bitcast.44, bf16[896,64]{1,0:T(8,128)(2,1)} %fusion.35.hit_ref), custom_call_target="tpu_custom_call" | custom-call | flops 939524096 | bytes 7340032 | tf_op jit(solution)/shard_map/pallas_call | solution.py:89
  105.9 3.8 %all-to-all-start.3 = ((bf16[4,16,4096]{2,1,0:T(8,128)(2,1)}), bf16[4,16,4096]{2,1,0:T(8,128)(2,1)S(1)}, u32[]{:S(2)}, u32[]{:S(2)}) async-start(bf16[4,16,4096]{2,1,0:T(8,128)(2,1)} %bitcast.47), calls=%async_computation.3 | async-start | bytes 1048576 | tf_op jit(solution)/shard_map/all_to_all | solution.py:220
  109.7 1.8 %reduce.7 = f32[896]{0:T(1024)} reduce(f32[896,1]{1,0:T(8,128)} %get-tuple-element.11, f32[]{:T(128)} %constant.84), dimensions={1}, to_apply=%get-tuple-element.11.reduce_sub_computation | reduce | bytes 7172 | tf_op jit(solution)/shard_map/pallas_call | solution.py:89
  111.6 7.0 %shard_map.105 = bf16[896,4096]{1,0:T(8,128)(2,1)} custom-call(bf16[896,64]{1,0:T(8,128)(2,1)} %get-tuple-element.12.wb_ref, f32[896,1]{1,0:T(8,128)} %get-tuple-element.13.tot_ref, bf16[896,64]{1,0:T(8,128)(2,1)} %fusion.35.hit_ref, bf16[64,4096]{1,0:T(8,128)(2,1)} %bitcast.45), custom_call_target="tpu_custom_call" | custom-call | flops 939524096 | bytes 7340032 | tf_op jit(solution)/shard_map/pallas_call | solution.py:120
  118.6 5.2 %all-to-all-done.3 = bf16[4,16,4096]{2,1,0:T(8,128)(2,1)S(1)} async-done(((bf16[4,16,4096]{2,1,0:T(8,128)(2,1)}), bf16[4,16,4096]{2,1,0:T(8,128)(2,1)S(1)}, u32[]{:S(2)}, u32[]{:S(2)}) %all-to-all-start.3) | async-done | bytes 524320 | tf_op jit(solution)/shard_map/all_to_all | solution.py:220
  (41 shorter events, 9.3 us)
Async XLA Ops:
  5.9 9.6 %all-to-all-start.1 = ((s32[8,1,154]{2,1,0:T(1,128)}), s32[8,1,154]{2,1,0:T(1,128)S(1)}, u32[]{:S(2)}, u32[]{:S(2)}) async-start(s32[8,1,154]{2,1,0:T(1,128)} %copy.19), calls=%async_computation.1 | async-start | bytes 16384 | tf_op jit(solution)/shard_map/all_to_all | solution.py:161
  15.6 35.0 %all-to-all-start = ((bf16[8,154,1024]{2,1,0:T(8,128)(2,1)}), bf16[8,154,1024]{2,1,0:T(8,128)(2,1)S(1)}, u32[]{:S(2)}, u32[]{:S(2)}) async-start(bf16[8,154,1024]{2,1,0:T(8,128)(2,1)} %bitcast.42), calls=%async_computation | async-start | bytes 5242880 | tf_op jit(solution)/shard_map/all_to_all | solution.py:159
  30.9 20.8 %copy-start.1 = (f32[1024]{0:T(1024)S(1)}, f32[1024]{0:T(1024)}, u32[]{:S(2)}) copy-start(f32[1024]{0:T(1024)} %param.13) | copy-start | bytes 12292
  51.7 13.2 %copy-start = (s32[896]{0:T(1024)S(1)}, s32[896]{0:T(1024)}, u32[]{:S(2)}) copy-start(s32[896]{0:T(1024)} %param.15) | copy-start | bytes 10756
  59.9 18.9 %all-to-all-start.2 = ((bf16[8,16,4096]{2,1,0:T(8,128)(2,1)}), bf16[8,16,4096]{2,1,0:T(8,128)(2,1)S(1)}, u32[]{:S(2)}, u32[]{:S(2)}) async-start(bf16[8,16,4096]{2,1,0:T(8,128)(2,1)} %bitcast.17), calls=%async_computation.2 | async-start | bytes 2097152 | tf_op jit(solution)/shard_map/all_to_all | solution.py:199
  79.2 7.6 %collective-permute-start.2 = (bf16[16,4096]{1,0:T(8,128)(2,1)S(1)}, bf16[16,4096]{1,0:T(8,128)(2,1)S(1)}, u32[]{:S(2)}, u32[]{:S(2)}) collective-permute-start(bf16[16,4096]{1,0:T(8,128)(2,1)S(1)} %multiply_convert_fusion), channel_id=1, source_target_pairs={{0,3},{1,0},{2,1},{3,2},{4,7},{5,4},{6,5},{7,6},{8,11},{9,8},{10,9... | collective-permute-start | bytes 393224 | tf_op jit(solution)/shard_map/ppermute | solution.py:209
  82.9 11.6 %collective-permute-start.1 = (bf16[16,4096]{1,0:T(8,128)(2,1)S(1)}, bf16[16,4096]{1,0:T(8,128)(2,1)S(1)}, u32[]{:S(2)}, u32[]{:S(2)}) collective-permute-start(bf16[16,4096]{1,0:T(8,128)(2,1)S(1)} %multiply_convert_fusion), channel_id=1, source_target_pairs={{0,2},{1,3},{2,0},{3,1},{4,6},{5,7},{6,4},{7,5},{8,10},{9,11},{10,... | collective-permute-start | bytes 393224 | tf_op jit(solution)/shard_map/ppermute | solution.py:209
  82.9 11.6 %collective-permute-start = (bf16[16,4096]{1,0:T(8,128)(2,1)S(1)}, bf16[16,4096]{1,0:T(8,128)(2,1)S(1)}, u32[]{:S(2)}, u32[]{:S(2)}) collective-permute-start(bf16[16,4096]{1,0:T(8,128)(2,1)S(1)} %multiply_convert_fusion), channel_id=1, source_target_pairs={{0,1},{1,2},{2,3},{3,0},{4,5},{5,6},{6,7},{7,4},{8,9},{9,10},{10,1... | collective-permute-start | bytes 393224 | tf_op jit(solution)/shard_map/ppermute | solution.py:209
  105.9 17.9 %all-to-all-start.3 = ((bf16[4,16,4096]{2,1,0:T(8,128)(2,1)}), bf16[4,16,4096]{2,1,0:T(8,128)(2,1)S(1)}, u32[]{:S(2)}, u32[]{:S(2)}) async-start(bf16[4,16,4096]{2,1,0:T(8,128)(2,1)} %bitcast.47), calls=%async_computation.3 | async-start | bytes 1048576 | tf_op jit(solution)/shard_map/all_to_all | solution.py:220

commit v17 on v15

--- a/solution.py
+++ b/solution.py
@@ -52,7 +52,14 @@
 
     @pl.when(pl.program_id(0) == pl.num_programs(0) - 1)
     def _():
-        gd_ref[...] = acc_ref[...].astype(jnp.bfloat16)
+        pieces = lax.axis_size("blk")
+        rows = gd_ref.shape[0] // pieces
+        position = lax.axis_index("blk")
+        for block in range(pieces):
+            slot = lax.rem(position - block + pieces, pieces)
+            gd_ref[pl.ds(block * rows, rows), :] = acc_ref[
+                pl.ds(pl.multiple_of(slot * rows, rows), rows), :
+            ].astype(jnp.bfloat16)
 
 
 def unit_query_kernel(q_ref, qu_ref):
@@ -210,10 +217,11 @@
             for shift in range(1, cycle_size)
         ]
     )
-    arrival_of = (position - jnp.arange(cycle_size, dtype=jnp.int32)) % cycle_size
-    doc_piece = arrived[arrival_of].reshape(cycle_size * doc_unit.shape[0], emb_width)
+    doc_piece = arrived.reshape(cycle_size * doc_unit.shape[0], emb_width)
     piece_rows = doc_piece.shape[0]
-    hits = (positives[:, None] == jnp.arange(piece_rows, dtype=jnp.int32)[None, :]).astype(
+    arrival_slot = (position - positives // doc_unit.shape[0]) % cycle_size
+    arrival_index = arrival_slot * doc_unit.shape[0] + positives % doc_unit.shape[0]
+    hits = (arrival_index[:, None] == jnp.arange(piece_rows, dtype=jnp.int32)[None, :]).astype(
         jnp.bfloat16
     )
     loss_col, weights, totals, grad_part = scores(query_unit, doc_piece, hits)

time: 125 us -> 124 us (level)
  local copies, waits for them, and re-layouts: 13 us -> 11.6 us
    gather x1 -> x0, local copies, waits for them, and re-layouts: 1.37 us -> none  [on_device(): arrived[arrival_of].reshape(cycle_size * doc_unit.shape[0], emb_width)]
where the time goes in v17:
time: 124 us; the launch traced here: 123 us
  waiting for transfers between devices  38.4 us (31%)
  Pallas kernels  26.1 us (21%)
  starting transfers between devices  21.9 us (18%)
  other arithmetic  14.3 us (12%)
  local copies, waits for them, and re-layouts  11.6 us (9%)
  matrix products  9.37 us (8%)
  between operations  1.43 us (1%)
    all_to_all x1, waiting for transfers between devices, on_device(): lax.all_to_all(send_rows, 'dp', split_axis=0, concat_axis=0, tiled=True)  19.6 us
    ppermute x3, waiting for transfers between devices, on_device(): lax.ppermute(doc_unit, 'blk', [(i, (i + shift) % cycle_size) for i in ran...  10.5 us
    pallas_call x1, Pallas kernels, unit_queries(): pl.pallas_call(unit_query_kernel, grid=(rows // tile,), in_specs=[pl.Bloc...  9.9 us
    pallas_call x1, Pallas kernels, scores(): pl.pallas_call(score_kernel, grid=(rows // tile,), in_specs=[pl.BlockSpec...  9.17 us
    dot_general x1, matrix products, on_device(): partial = jnp.dot(selector, embedded, preferred_element_type=jnp.float32)  8.2 us
    pallas_call x1, Pallas kernels, query_grads(): pl.pallas_call(query_grad_kernel, grid=(rows // tile,), in_specs=[pl.Bloc...  7.05 us
    all_to_all x1, waiting for transfers between devices, on_device(): lax.all_to_all(grad_part.reshape(cycle_size, doc_unit.shape[0], emb_width...  5.23 us
    all_to_all x1, starting transfers between devices, on_device(): lax.all_to_all(partial, 'dp', split_axis=0, concat_axis=0, tiled=True)  4.97 us
  transfers between devices with their start and end apart: 7, of which 5 were waited for; matrix products, arithmetic and copies ran while one was open for 16% of the time, Pallas kernels for 14%

profile of v17, /device:TPU:2, one launch (start us, length us, event | category | flops | bytes accessed | tf_op | source)
XLA Modules:
  0.0 123.1 jit_solution(2461041465806365002)
XLA Ops:
  0.6 1.2 slice.9
  5.9 4.3 %all-to-all-start.1 = ((s32[8,1,154]{2,1,0:T(1,128)}), s32[8,1,154]{2,1,0:T(1,128)S(1)}, u32[]{:S(2)}, u32[]{:S(2)}) async-start(s32[8,1,154]{2,1,0:T(1,128)} %copy.19), calls=%async_computation.1 | async-start | bytes 16384 | tf_op jit(solution)/shard_map/all_to_all | solution.py:168
  10.2 3.2 %copy.17 = bf16[160,8,1024]{2,0,1:T(8,128)(2,1)S(1)} copy(bf16[160,8,1024]{2,1,0:T(8,128)(2,1)} %bitcast.44) | data formatting | bytes 5242880 | tf_op jit(solution)/shard_map/reshape | solution.py:157
  13.4 2.2 %gather_fusion = bf16[8,160,1024]{2,1,0:T(8,128)(2,1)} fusion(bf16[160,8,1024]{2,0,1:T(8,128)(2,1)S(1)} %copy.17, s32[1024]{0:T(1024)S(1)} %pad_clamp_fusion.1), kind=kCustom, calls=%fused_computation | custom fusion | bytes 5242912 | tf_op jit(solution)/shard_map/jit(_take)/gather | solution.py:158
  15.6 4.2 %all-to-all-start = ((bf16[8,154,1024]{2,1,0:T(8,128)(2,1)}), bf16[8,154,1024]{2,1,0:T(8,128)(2,1)S(1)}, u32[]{:S(2)}, u32[]{:S(2)}) async-start(bf16[8,154,1024]{2,1,0:T(8,128)(2,1)} %bitcast.40), calls=%async_computation | async-start | bytes 5242880 | tf_op jit(solution)/shard_map/all_to_all | solution.py:166
  21.6 4.3 %fusion.46 = (s32[320]{0:T(512)S(1)}, s32[320,1]{0,1:T(1,128)S(1)}) fusion(s32[]{:T(128)} %bitcast.8, s32[]{:T(128)} %bitcast.9, s32[]{:T(128)} %bitcast.10, s32[]{:T(128)} %bitcast.11, s32[]{:T(128)} %bitcast.12, s32[]{:T(128)} %bitcast.14, s32[]{:T(128)} %bitcast.13, s32[320]{0:T(512)S(1)} %get-tuple-element.23, s32[320]{0:T(512)S(1)} %get-tuple-element.22), kind=kLoop, calls=%fused_computation.87 | loop fusion | flops 4480 | bytes 5148 | tf_op jit(solution)/shard_map/gather | solution.py:176
  27.3 2.2 %gather_fusion.2 = s32[320]{0:T(512)S(1)} fusion(s32[1232]{0:T(1024)S(1)} %reshape.281, s32[1024]{0:T(1024)S(1)} %pad_clamp_fusion), kind=kCustom, calls=%fused_computation.2 | custom fusion | bytes 3840 | tf_op jit(solution)/shard_map/gather | solution.py:188
  30.9 19.6 %all-to-all-done = bf16[8,154,1024]{2,1,0:T(8,128)(2,1)S(1)} async-done(((bf16[8,154,1024]{2,1,0:T(8,128)(2,1)}), bf16[8,154,1024]{2,1,0:T(8,128)(2,1)S(1)}, u32[]{:S(2)}, u32[]{:S(2)}) %all-to-all-start) | async-done | bytes 2523168 | tf_op jit(solution)/shard_map/all_to_all | solution.py:166
  50.5 1.2 fusion.23
  51.7 8.2 %convolution_convert_fusion = bf16[128,4096]{1,0:T(8,128)(2,1)} fusion(bf16[1,1024,4096]{2,1,0:T(8,128)(2,1)} %param.12, bf16[320,1024]{1,0:T(8,128)(2,1)S(1)} %get-tuple-element.33, f32[1024]{0:T(1024)S(1)} %copy-done.1, f32[320]{0:T(512)S(1)} %add_rsqrt_fusion, s32[320]{0:T(512)S(1)} %add_select_fusion.3), kind=kOutput, calls=%fused_computation.14 | convolution fusion | flops 3033571328 | bytes 10099200 | tf_op jit(solution)/shard_map/dot_general | solution.py:204
  59.9 5.0 %all-to-all-start.2 = ((bf16[8,16,4096]{2,1,0:T(8,128)(2,1)}), bf16[8,16,4096]{2,1,0:T(8,128)(2,1)S(1)}, u32[]{:S(2)}, u32[]{:S(2)}) async-start(bf16[8,16,4096]{2,1,0:T(8,128)(2,1)} %bitcast.17), calls=%async_computation.2 | async-start | bytes 2097152 | tf_op jit(solution)/shard_map/all_to_all | solution.py:206
  64.9 0.9 fusion.35.hit_ref
  65.8 9.9 %shard_map.103.q_ref = bf16[896,4096]{1,0:T(8,128)(2,1)} custom-call(bf16[896,4096]{1,0:T(8,128)(2,1)} %q_ref), custom_call_target="tpu_custom_call" | custom-call | flops 14680064 | bytes 14680064 | tf_op jit(solution)/shard_map/pallas_call | solution.py:74
  75.7 3.1 %all-to-all-done.2 = bf16[8,16,4096]{2,1,0:T(8,128)(2,1)S(1)} async-done(((bf16[8,16,4096]{2,1,0:T(8,128)(2,1)}), bf16[8,16,4096]{2,1,0:T(8,128)(2,1)S(1)}, u32[]{:S(2)}, u32[]{:S(2)}) %all-to-all-start.2) | async-done | bytes 1048608 | tf_op jit(solution)/shard_map/all_to_all | solution.py:206
  79.2 3.7 %collective-permute-start.2 = (bf16[16,4096]{1,0:T(8,128)(2,1)S(1)}, bf16[16,4096]{1,0:T(8,128)(2,1)S(1)}, u32[]{:S(2)}, u32[]{:S(2)}) collective-permute-start(bf16[16,4096]{1,0:T(8,128)(2,1)S(1)} %multiply_convert_fusion), channel_id=1, source_target_pairs={{0,3},{1,0},{2,1},{3,2},{4,7},{5,4},{6,5},{7,6},{8,11},{9,8},{10,9... | collective-permute-start | bytes 393224 | tf_op jit(solution)/shard_map/ppermute | solution.py:216
  82.9 1.0 collective-permute-start
  84.0 2.8 %collective-permute-done.2 = bf16[16,4096]{1,0:T(8,128)(2,1)S(1)} collective-permute-done((bf16[16,4096]{1,0:T(8,128)(2,1)S(1)}, bf16[16,4096]{1,0:T(8,128)(2,1)S(1)}, u32[]{:S(2)}, u32[]{:S(2)}) %collective-permute-start.2) | collective-permute-done | bytes 131104 | tf_op jit(solution)/shard_map/ppermute | solution.py:216
  86.8 7.6 %collective-permute-done.1 = bf16[16,4096]{1,0:T(8,128)(2,1)S(1)} collective-permute-done((bf16[16,4096]{1,0:T(8,128)(2,1)S(1)}, bf16[16,4096]{1,0:T(8,128)(2,1)S(1)}, u32[]{:S(2)}, u32[]{:S(2)}) %collective-permute-start.1) | collective-permute-done | bytes 131104 | tf_op jit(solution)/shard_map/ppermute | solution.py:216
  94.5 0.9 pad_maximum_fusion
  95.3 9.2 %shard_map.104 = (f32[896,1]{1,0:T(8,128)}, bf16[896,64]{1,0:T(8,128)(2,1)}, f32[896,1]{1,0:T(8,128)}, bf16[64,4096]{1,0:T(8,128)(2,1)}) custom-call(bf16[896,4096]{1,0:T(8,128)(2,1)} %shard_map.103.q_ref, bf16[64,4096]{1,0:T(8,128)(2,1)} %bitcast.42, bf16[896,64]{1,0:T(8,128)(2,1)} %fusion.35.hit_ref), custom_call_target="tpu_custom_call" | custom-call | flops 939524096 | bytes 7340032 | tf_op jit(solution)/shard_map/pallas_call | solution.py:96
  104.5 3.8 %all-to-all-start.3 = ((bf16[4,16,4096]{2,1,0:T(8,128)(2,1)}), bf16[4,16,4096]{2,1,0:T(8,128)(2,1)S(1)}, u32[]{:S(2)}, u32[]{:S(2)}) async-start(bf16[4,16,4096]{2,1,0:T(8,128)(2,1)} %bitcast.45), calls=%async_computation.3 | async-start | bytes 1048576 | tf_op jit(solution)/shard_map/all_to_all | solution.py:228
  108.3 1.8 %reduce.7 = f32[896]{0:T(1024)} reduce(f32[896,1]{1,0:T(8,128)} %get-tuple-element.11, f32[]{:T(128)} %constant.104), dimensions={1}, to_apply=%get-tuple-element.11.reduce_sub_computation | reduce | bytes 7172 | tf_op jit(solution)/shard_map/pallas_call | solution.py:96
  110.1 7.0 %shard_map.105 = bf16[896,4096]{1,0:T(8,128)(2,1)} custom-call(bf16[896,64]{1,0:T(8,128)(2,1)} %get-tuple-element.12.wb_ref, f32[896,1]{1,0:T(8,128)} %get-tuple-element.13.tot_ref, bf16[896,64]{1,0:T(8,128)(2,1)} %fusion.35.hit_ref, bf16[64,4096]{1,0:T(8,128)(2,1)} %bitcast.43), custom_call_target="tpu_custom_call" | custom-call | flops 939524096 | bytes 7340032 | tf_op jit(solution)/shard_map/pallas_call | solution.py:127
  117.1 5.2 %all-to-all-done.3 = bf16[4,16,4096]{2,1,0:T(8,128)(2,1)S(1)} async-done(((bf16[4,16,4096]{2,1,0:T(8,128)(2,1)}), bf16[4,16,4096]{2,1,0:T(8,128)(2,1)S(1)}, u32[]{:S(2)}, u32[]{:S(2)}) %all-to-all-start.3) | async-done | bytes 524320 | tf_op jit(solution)/shard_map/all_to_all | solution.py:228
  (39 shorter events, 9.2 us)
Async XLA Ops:
  5.9 9.6 %all-to-all-start.1 = ((s32[8,1,154]{2,1,0:T(1,128)}), s32[8,1,154]{2,1,0:T(1,128)S(1)}, u32[]{:S(2)}, u32[]{:S(2)}) async-start(s32[8,1,154]{2,1,0:T(1,128)} %copy.19), calls=%async_computation.1 | async-start | bytes 16384 | tf_op jit(solution)/shard_map/all_to_all | solution.py:168
  15.6 35.0 %all-to-all-start = ((bf16[8,154,1024]{2,1,0:T(8,128)(2,1)}), bf16[8,154,1024]{2,1,0:T(8,128)(2,1)S(1)}, u32[]{:S(2)}, u32[]{:S(2)}) async-start(bf16[8,154,1024]{2,1,0:T(8,128)(2,1)} %bitcast.40), calls=%async_computation | async-start | bytes 5242880 | tf_op jit(solution)/shard_map/all_to_all | solution.py:166
  30.9 20.8 %copy-start.1 = (f32[1024]{0:T(1024)S(1)}, f32[1024]{0:T(1024)}, u32[]{:S(2)}) copy-start(f32[1024]{0:T(1024)} %param.13) | copy-start | bytes 12292
  51.7 13.2 %copy-start = (s32[896]{0:T(1024)S(1)}, s32[896]{0:T(1024)}, u32[]{:S(2)}) copy-start(s32[896]{0:T(1024)} %param.15) | copy-start | bytes 10756
  59.9 18.9 %all-to-all-start.2 = ((bf16[8,16,4096]{2,1,0:T(8,128)(2,1)}), bf16[8,16,4096]{2,1,0:T(8,128)(2,1)S(1)}, u32[]{:S(2)}, u32[]{:S(2)}) async-start(bf16[8,16,4096]{2,1,0:T(8,128)(2,1)} %bitcast.17), calls=%async_computation.2 | async-start | bytes 2097152 | tf_op jit(solution)/shard_map/all_to_all | solution.py:206
  79.2 7.6 %collective-permute-start.2 = (bf16[16,4096]{1,0:T(8,128)(2,1)S(1)}, bf16[16,4096]{1,0:T(8,128)(2,1)S(1)}, u32[]{:S(2)}, u32[]{:S(2)}) collective-permute-start(bf16[16,4096]{1,0:T(8,128)(2,1)S(1)} %multiply_convert_fusion), channel_id=1, source_target_pairs={{0,3},{1,0},{2,1},{3,2},{4,7},{5,4},{6,5},{7,6},{8,11},{9,8},{10,9... | collective-permute-start | bytes 393224 | tf_op jit(solution)/shard_map/ppermute | solution.py:216
  82.9 11.6 %collective-permute-start.1 = (bf16[16,4096]{1,0:T(8,128)(2,1)S(1)}, bf16[16,4096]{1,0:T(8,128)(2,1)S(1)}, u32[]{:S(2)}, u32[]{:S(2)}) collective-permute-start(bf16[16,4096]{1,0:T(8,128)(2,1)S(1)} %multiply_convert_fusion), channel_id=1, source_target_pairs={{0,2},{1,3},{2,0},{3,1},{4,6},{5,7},{6,4},{7,5},{8,10},{9,11},{10,... | collective-permute-start | bytes 393224 | tf_op jit(solution)/shard_map/ppermute | solution.py:216
  82.9 11.6 %collective-permute-start = (bf16[16,4096]{1,0:T(8,128)(2,1)S(1)}, bf16[16,4096]{1,0:T(8,128)(2,1)S(1)}, u32[]{:S(2)}, u32[]{:S(2)}) collective-permute-start(bf16[16,4096]{1,0:T(8,128)(2,1)S(1)} %multiply_convert_fusion), channel_id=1, source_target_pairs={{0,1},{1,2},{2,3},{3,0},{4,5},{5,6},{6,7},{7,4},{8,9},{9,10},{10,1... | collective-permute-start | bytes 393224 | tf_op jit(solution)/shard_map/ppermute | solution.py:216
  104.5 17.9 %all-to-all-start.3 = ((bf16[4,16,4096]{2,1,0:T(8,128)(2,1)}), bf16[4,16,4096]{2,1,0:T(8,128)(2,1)S(1)}, u32[]{:S(2)}, u32[]{:S(2)}) async-start(bf16[4,16,4096]{2,1,0:T(8,128)(2,1)} %bitcast.45), calls=%async_computation.3 | async-start | bytes 1048576 | tf_op jit(solution)/shard_map/all_to_all | solution.py:228

commit v18 on v17

--- a/solution.py
+++ b/solution.py
@@ -45,7 +45,7 @@
     loss_ref[...] = jnp.log(totals) - chosen_logit
     wb_ref[...] = weights.astype(jnp.bfloat16)
     tot_ref[...] = totals
-    coefficient_t = (weights / totals - hits).T.astype(jnp.bfloat16)
+    coefficient_t = (weights * (1.0 / totals) - hits).T.astype(jnp.bfloat16)
     acc_ref[...] += logit_scale * jnp.dot(
         coefficient_t, query_unit, preferred_element_type=jnp.float32
     )

time: 124 us -> 124 us (level)
  no operation moved by 1% of the time
where the time goes in v18:
time: 124 us; the launch traced here: 123 us
  waiting for transfers between devices  38.4 us (31%)
  Pallas kernels  26.1 us (21%)
  starting transfers between devices  21.9 us (18%)
  other arithmetic  14.3 us (12%)
  local copies, waits for them, and re-layouts  11.6 us (9%)
  matrix products  9.37 us (8%)
  between operations  1.43 us (1%)
    all_to_all x1, waiting for transfers between devices, on_device(): lax.all_to_all(send_rows, 'dp', split_axis=0, concat_axis=0, tiled=True)  19.6 us
    ppermute x3, waiting for transfers between devices, on_device(): lax.ppermute(doc_unit, 'blk', [(i, (i + shift) % cycle_size) for i in ran...  10.5 us
    pallas_call x1, Pallas kernels, unit_queries(): pl.pallas_call(unit_query_kernel, grid=(rows // tile,), in_specs=[pl.Bloc...  9.9 us
    pallas_call x1, Pallas kernels, scores(): pl.pallas_call(score_kernel, grid=(rows // tile,), in_specs=[pl.BlockSpec...  9.17 us
    dot_general x1, matrix products, on_device(): partial = jnp.dot(selector, embedded, preferred_element_type=jnp.float32)  8.2 us
    pallas_call x1, Pallas kernels, query_grads(): pl.pallas_call(query_grad_kernel, grid=(rows // tile,), in_specs=[pl.Bloc...  7.05 us
    all_to_all x1, waiting for transfers between devices, on_device(): lax.all_to_all(grad_part.reshape(cycle_size, doc_unit.shape[0], emb_width...  5.23 us
    all_to_all x1, starting transfers between devices, on_device(): lax.all_to_all(partial, 'dp', split_axis=0, concat_axis=0, tiled=True)  4.97 us
  transfers between devices with their start and end apart: 7, of which 5 were waited for; matrix products, arithmetic and copies ran while one was open for 16% of the time, Pallas kernels for 14%

profile of v18, /device:TPU:2, one launch (start us, length us, event | category | flops | bytes accessed | tf_op | source)
XLA Modules:
  0.0 123.1 jit_solution(2461041465806365002)
XLA Ops:
  0.6 1.2 slice.9
  5.9 4.3 %all-to-all-start.1 = ((s32[8,1,154]{2,1,0:T(1,128)}), s32[8,1,154]{2,1,0:T(1,128)S(1)}, u32[]{:S(2)}, u32[]{:S(2)}) async-start(s32[8,1,154]{2,1,0:T(1,128)} %copy.19), calls=%async_computation.1 | async-start | bytes 16384 | tf_op jit(solution)/shard_map/all_to_all | solution.py:168
  10.2 3.2 %copy.17 = bf16[160,8,1024]{2,0,1:T(8,128)(2,1)S(1)} copy(bf16[160,8,1024]{2,1,0:T(8,128)(2,1)} %bitcast.44) | data formatting | bytes 5242880 | tf_op jit(solution)/shard_map/reshape | solution.py:157
  13.4 2.2 %gather_fusion = bf16[8,160,1024]{2,1,0:T(8,128)(2,1)} fusion(bf16[160,8,1024]{2,0,1:T(8,128)(2,1)S(1)} %copy.17, s32[1024]{0:T(1024)S(1)} %pad_clamp_fusion.1), kind=kCustom, calls=%fused_computation | custom fusion | bytes 5242912 | tf_op jit(solution)/shard_map/jit(_take)/gather | solution.py:158
  15.6 4.2 %all-to-all-start = ((bf16[8,154,1024]{2,1,0:T(8,128)(2,1)}), bf16[8,154,1024]{2,1,0:T(8,128)(2,1)S(1)}, u32[]{:S(2)}, u32[]{:S(2)}) async-start(bf16[8,154,1024]{2,1,0:T(8,128)(2,1)} %bitcast.40), calls=%async_computation | async-start | bytes 5242880 | tf_op jit(solution)/shard_map/all_to_all | solution.py:166
  21.6 4.3 %fusion.46 = (s32[320]{0:T(512)S(1)}, s32[320,1]{0,1:T(1,128)S(1)}) fusion(s32[]{:T(128)} %bitcast.8, s32[]{:T(128)} %bitcast.9, s32[]{:T(128)} %bitcast.10, s32[]{:T(128)} %bitcast.11, s32[]{:T(128)} %bitcast.12, s32[]{:T(128)} %bitcast.14, s32[]{:T(128)} %bitcast.13, s32[320]{0:T(512)S(1)} %get-tuple-element.23, s32[320]{0:T(512)S(1)} %get-tuple-element.22), kind=kLoop, calls=%fused_computation.87 | loop fusion | flops 4480 | bytes 5148 | tf_op jit(solution)/shard_map/gather | solution.py:176
  27.3 2.2 %gather_fusion.2 = s32[320]{0:T(512)S(1)} fusion(s32[1232]{0:T(1024)S(1)} %reshape.281, s32[1024]{0:T(1024)S(1)} %pad_clamp_fusion), kind=kCustom, calls=%fused_computation.2 | custom fusion | bytes 3840 | tf_op jit(solution)/shard_map/gather | solution.py:188
  30.9 19.6 %all-to-all-done = bf16[8,154,1024]{2,1,0:T(8,128)(2,1)S(1)} async-done(((bf16[8,154,1024]{2,1,0:T(8,128)(2,1)}), bf16[8,154,1024]{2,1,0:T(8,128)(2,1)S(1)}, u32[]{:S(2)}, u32[]{:S(2)}) %all-to-all-start) | async-done | bytes 2523168 | tf_op jit(solution)/shard_map/all_to_all | solution.py:166
  50.5 1.2 fusion.23
  51.7 8.2 %convolution_convert_fusion = bf16[128,4096]{1,0:T(8,128)(2,1)} fusion(bf16[1,1024,4096]{2,1,0:T(8,128)(2,1)} %param.12, bf16[320,1024]{1,0:T(8,128)(2,1)S(1)} %get-tuple-element.33, f32[1024]{0:T(1024)S(1)} %copy-done.1, f32[320]{0:T(512)S(1)} %add_rsqrt_fusion, s32[320]{0:T(512)S(1)} %add_select_fusion.3), kind=kOutput, calls=%fused_computation.14 | convolution fusion | flops 3033571328 | bytes 10099200 | tf_op jit(solution)/shard_map/dot_general | solution.py:204
  59.9 5.0 %all-to-all-start.2 = ((bf16[8,16,4096]{2,1,0:T(8,128)(2,1)}), bf16[8,16,4096]{2,1,0:T(8,128)(2,1)S(1)}, u32[]{:S(2)}, u32[]{:S(2)}) async-start(bf16[8,16,4096]{2,1,0:T(8,128)(2,1)} %bitcast.17), calls=%async_computation.2 | async-start | bytes 2097152 | tf_op jit(solution)/shard_map/all_to_all | solution.py:206
  64.9 0.9 fusion.35.hit_ref
  65.8 9.9 %shard_map.103.q_ref = bf16[896,4096]{1,0:T(8,128)(2,1)} custom-call(bf16[896,4096]{1,0:T(8,128)(2,1)} %q_ref), custom_call_target="tpu_custom_call" | custom-call | flops 14680064 | bytes 14680064 | tf_op jit(solution)/shard_map/pallas_call | solution.py:74
  75.7 3.1 %all-to-all-done.2 = bf16[8,16,4096]{2,1,0:T(8,128)(2,1)S(1)} async-done(((bf16[8,16,4096]{2,1,0:T(8,128)(2,1)}), bf16[8,16,4096]{2,1,0:T(8,128)(2,1)S(1)}, u32[]{:S(2)}, u32[]{:S(2)}) %all-to-all-start.2) | async-done | bytes 1048608 | tf_op jit(solution)/shard_map/all_to_all | solution.py:206
  79.2 3.7 %collective-permute-start.2 = (bf16[16,4096]{1,0:T(8,128)(2,1)S(1)}, bf16[16,4096]{1,0:T(8,128)(2,1)S(1)}, u32[]{:S(2)}, u32[]{:S(2)}) collective-permute-start(bf16[16,4096]{1,0:T(8,128)(2,1)S(1)} %multiply_convert_fusion), channel_id=1, source_target_pairs={{0,3},{1,0},{2,1},{3,2},{4,7},{5,4},{6,5},{7,6},{8,11},{9,8},{10,9... | collective-permute-start | bytes 393224 | tf_op jit(solution)/shard_map/ppermute | solution.py:216
  82.9 1.0 collective-permute-start
  84.0 2.8 %collective-permute-done.2 = bf16[16,4096]{1,0:T(8,128)(2,1)S(1)} collective-permute-done((bf16[16,4096]{1,0:T(8,128)(2,1)S(1)}, bf16[16,4096]{1,0:T(8,128)(2,1)S(1)}, u32[]{:S(2)}, u32[]{:S(2)}) %collective-permute-start.2) | collective-permute-done | bytes 131104 | tf_op jit(solution)/shard_map/ppermute | solution.py:216
  86.8 7.6 %collective-permute-done.1 = bf16[16,4096]{1,0:T(8,128)(2,1)S(1)} collective-permute-done((bf16[16,4096]{1,0:T(8,128)(2,1)S(1)}, bf16[16,4096]{1,0:T(8,128)(2,1)S(1)}, u32[]{:S(2)}, u32[]{:S(2)}) %collective-permute-start.1) | collective-permute-done | bytes 131104 | tf_op jit(solution)/shard_map/ppermute | solution.py:216
  94.5 0.9 pad_maximum_fusion
  95.3 9.2 %shard_map.104 = (f32[896,1]{1,0:T(8,128)}, bf16[896,64]{1,0:T(8,128)(2,1)}, f32[896,1]{1,0:T(8,128)}, bf16[64,4096]{1,0:T(8,128)(2,1)}) custom-call(bf16[896,4096]{1,0:T(8,128)(2,1)} %shard_map.103.q_ref, bf16[64,4096]{1,0:T(8,128)(2,1)} %bitcast.42, bf16[896,64]{1,0:T(8,128)(2,1)} %fusion.35.hit_ref), custom_call_target="tpu_custom_call" | custom-call | flops 939524096 | bytes 7340032 | tf_op jit(solution)/shard_map/pallas_call | solution.py:96
  104.5 3.8 %all-to-all-start.3 = ((bf16[4,16,4096]{2,1,0:T(8,128)(2,1)}), bf16[4,16,4096]{2,1,0:T(8,128)(2,1)S(1)}, u32[]{:S(2)}, u32[]{:S(2)}) async-start(bf16[4,16,4096]{2,1,0:T(8,128)(2,1)} %bitcast.45), calls=%async_computation.3 | async-start | bytes 1048576 | tf_op jit(solution)/shard_map/all_to_all | solution.py:228
  108.3 1.8 %reduce.7 = f32[896]{0:T(1024)} reduce(f32[896,1]{1,0:T(8,128)} %get-tuple-element.11, f32[]{:T(128)} %constant.104), dimensions={1}, to_apply=%get-tuple-element.11.reduce_sub_computation | reduce | bytes 7172 | tf_op jit(solution)/shard_map/pallas_call | solution.py:96
  110.1 7.0 %shard_map.105 = bf16[896,4096]{1,0:T(8,128)(2,1)} custom-call(bf16[896,64]{1,0:T(8,128)(2,1)} %get-tuple-element.12.wb_ref, f32[896,1]{1,0:T(8,128)} %get-tuple-element.13.tot_ref, bf16[896,64]{1,0:T(8,128)(2,1)} %fusion.35.hit_ref, bf16[64,4096]{1,0:T(8,128)(2,1)} %bitcast.43), custom_call_target="tpu_custom_call" | custom-call | flops 939524096 | bytes 7340032 | tf_op jit(solution)/shard_map/pallas_call | solution.py:127
  117.1 5.2 %all-to-all-done.3 = bf16[4,16,4096]{2,1,0:T(8,128)(2,1)S(1)} async-done(((bf16[4,16,4096]{2,1,0:T(8,128)(2,1)}), bf16[4,16,4096]{2,1,0:T(8,128)(2,1)S(1)}, u32[]{:S(2)}, u32[]{:S(2)}) %all-to-all-start.3) | async-done | bytes 524320 | tf_op jit(solution)/shard_map/all_to_all | solution.py:228
  (39 shorter events, 9.2 us)
Async XLA Ops:
  5.9 9.6 %all-to-all-start.1 = ((s32[8,1,154]{2,1,0:T(1,128)}), s32[8,1,154]{2,1,0:T(1,128)S(1)}, u32[]{:S(2)}, u32[]{:S(2)}) async-start(s32[8,1,154]{2,1,0:T(1,128)} %copy.19), calls=%async_computation.1 | async-start | bytes 16384 | tf_op jit(solution)/shard_map/all_to_all | solution.py:168
  15.6 35.0 %all-to-all-start = ((bf16[8,154,1024]{2,1,0:T(8,128)(2,1)}), bf16[8,154,1024]{2,1,0:T(8,128)(2,1)S(1)}, u32[]{:S(2)}, u32[]{:S(2)}) async-start(bf16[8,154,1024]{2,1,0:T(8,128)(2,1)} %bitcast.40), calls=%async_computation | async-start | bytes 5242880 | tf_op jit(solution)/shard_map/all_to_all | solution.py:166
  30.9 20.8 %copy-start.1 = (f32[1024]{0:T(1024)S(1)}, f32[1024]{0:T(1024)}, u32[]{:S(2)}) copy-start(f32[1024]{0:T(1024)} %param.13) | copy-start | bytes 12292
  51.7 13.2 %copy-start = (s32[896]{0:T(1024)S(1)}, s32[896]{0:T(1024)}, u32[]{:S(2)}) copy-start(s32[896]{0:T(1024)} %param.15) | copy-start | bytes 10756
  59.9 18.9 %all-to-all-start.2 = ((bf16[8,16,4096]{2,1,0:T(8,128)(2,1)}), bf16[8,16,4096]{2,1,0:T(8,128)(2,1)S(1)}, u32[]{:S(2)}, u32[]{:S(2)}) async-start(bf16[8,16,4096]{2,1,0:T(8,128)(2,1)} %bitcast.17), calls=%async_computation.2 | async-start | bytes 2097152 | tf_op jit(solution)/shard_map/all_to_all | solution.py:206
  79.2 7.6 %collective-permute-start.2 = (bf16[16,4096]{1,0:T(8,128)(2,1)S(1)}, bf16[16,4096]{1,0:T(8,128)(2,1)S(1)}, u32[]{:S(2)}, u32[]{:S(2)}) collective-permute-start(bf16[16,4096]{1,0:T(8,128)(2,1)S(1)} %multiply_convert_fusion), channel_id=1, source_target_pairs={{0,3},{1,0},{2,1},{3,2},{4,7},{5,4},{6,5},{7,6},{8,11},{9,8},{10,9... | collective-permute-start | bytes 393224 | tf_op jit(solution)/shard_map/ppermute | solution.py:216
  82.9 11.6 %collective-permute-start.1 = (bf16[16,4096]{1,0:T(8,128)(2,1)S(1)}, bf16[16,4096]{1,0:T(8,128)(2,1)S(1)}, u32[]{:S(2)}, u32[]{:S(2)}) collective-permute-start(bf16[16,4096]{1,0:T(8,128)(2,1)S(1)} %multiply_convert_fusion), channel_id=1, source_target_pairs={{0,2},{1,3},{2,0},{3,1},{4,6},{5,7},{6,4},{7,5},{8,10},{9,11},{10,... | collective-permute-start | bytes 393224 | tf_op jit(solution)/shard_map/ppermute | solution.py:216
  82.9 11.6 %collective-permute-start = (bf16[16,4096]{1,0:T(8,128)(2,1)S(1)}, bf16[16,4096]{1,0:T(8,128)(2,1)S(1)}, u32[]{:S(2)}, u32[]{:S(2)}) collective-permute-start(bf16[16,4096]{1,0:T(8,128)(2,1)S(1)} %multiply_convert_fusion), channel_id=1, source_target_pairs={{0,1},{1,2},{2,3},{3,0},{4,5},{5,6},{6,7},{7,4},{8,9},{9,10},{10,1... | collective-permute-start | bytes 393224 | tf_op jit(solution)/shard_map/ppermute | solution.py:216
  104.5 17.9 %all-to-all-start.3 = ((bf16[4,16,4096]{2,1,0:T(8,128)(2,1)}), bf16[4,16,4096]{2,1,0:T(8,128)(2,1)S(1)}, u32[]{:S(2)}, u32[]{:S(2)}) async-start(bf16[4,16,4096]{2,1,0:T(8,128)(2,1)} %bitcast.45), calls=%async_computation.3 | async-start | bytes 1048576 | tf_op jit(solution)/shard_map/all_to_all | solution.py:228
